TPU v7x, 128 devices: a whole 4x4x4 slice. The times are simulated.
128 devices in a mesh: req: 4 (over y), exp: 32 (over z, x, core).
Axes of the slice: x: 4, y: 4, z: 4, core: 2. Of those that a mesh axis runs over, the one named last changes fastest.
Arguments:
- states: bfloat16 [2, 16384, 1024], P(None, ('req', 'exp')), may hold values from -6 to 6
- lengths: int32 [128, 4], P(('req', 'exp')), may hold values from 1 to 64, 128 in all within a row
- targets: int32 [16384], P('req'), may hold values from 0 to 36863
- routes: int32 [2, 16384, 8], P(None, ('req', 'exp')), may hold values from 0 to 31, all different within a row; in each aligned block of 128 rows (0 to 127, 128 to 255, ..., all dimensions but the last counted through in order) at most 40 rows name the same one
- gate_probs: float32 [2, 16384, 8], P(None, ('req', 'exp')), may hold values from 0.02 to 0.4
- owners: int32 [512], P(('req', 'exp')), may hold values from 0 to 511, each once
- norm_gains: float32 [2, 3, 1024], replicated, may hold values from 0.25 to 1.75
- qkv_weight: bfloat16 [2, 1024, 2048], replicated, may hold values from -14 to 14
- out_weight: bfloat16 [2, 1024, 1024], replicated, may hold values from -0.1875 to 0.1875
- expert_in: bfloat16 [2, 32, 1024, 1024], P(None, 'exp'), may hold values from -0.1875 to 0.1875
- expert_down: bfloat16 [2, 32, 512, 1024], P(None, 'exp'), may hold values from -0.25 to 0.25
- vocab_head: bfloat16 [2, 36864, 1024], P(None, 'exp'), may hold values from -170 to 170
Outputs:
- token_logp: float32 [2, 16384], P(None, ('req', 'exp'))
- seq_totals: float32 [512], P(('req', 'exp'))
Inputs may be any that keep to these rules, and one draw needn't show every extreme that they name: `lengths`: each row sums to 128; some row reaches 64. `routes`: the 8 experts of a token are distinct; among the 128 tokens of one device, no expert is named by more than 40 of them for one model, and that bound is reached. `owners`: a permutation of the sequence numbers.
All inputs are finite; a program needn't handle non-finite values.
Results may differ from a plain program's by a relative error of at most 0.012.
The roundings to bfloat16 on the way count: a program that leaves them out, or rounds other values in their place, can miss the bound.
Values may be sent and summed in bfloat16 or wider, within the bound.
No kernel may reach another device: no remote copies, remote signals or barrier semaphores. Data moves between devices by JAX's collectives and lax.ppermute only.
A program may use at most 128 MiB of HBM per device.

v0:
```python
import jax
import jax.numpy as jnp
from jax import lax
from jax.sharding import PartitionSpec as P

HEADS = 16
KV_HEADS = 8
HEAD_DIM = 64
EXPERT_FF = 512
EXPERTS = 32
TOP = 8
CAP = 40


EPSILON = 1e-06
RESIDUAL_SCALE = 0.22
SCORE_SCALE = 0.015625
LOGIT_DIVISOR = 6.0
ROTARY_BASE = 10000.0


def combined_all(x, axis, combine):
    everything = jax.tree.map(lambda part: lax.all_gather(part, axis), x)
    initial = jax.tree.map(lambda part: part[0], everything)

    def step(k, so_far):
        return combine(so_far, jax.tree.map(lambda part: part[k], everything))

    return lax.fori_loop(1, lax.axis_size(axis), step, initial)


def root_norm(values, gain_row):
    values = values.astype(jnp.float32)
    scaled = lax.rsqrt(jnp.mean(values * values, axis=-1, keepdims=True) + EPSILON)
    return values * scaled * gain_row


def segment_table(length_row, token_count):
    seq_ends = jnp.cumsum(length_row)
    seq_starts = seq_ends - length_row
    places = jnp.arange(token_count, dtype=jnp.int32)
    segment = jnp.sum((places[:, None] >= seq_ends[None, :]).astype(jnp.int32), axis=1)
    member = segment[:, None] == jnp.arange(length_row.shape[0], dtype=jnp.int32)[None, :]
    position = places - jnp.sum(member.astype(jnp.int32) * seq_starts[None, :], axis=1)
    return (segment, member, position)


def rotary(values, position):
    half_dim = values.shape[-1] // 2
    frequency = ROTARY_BASE ** (-2.0 * jnp.arange(half_dim, dtype=jnp.float32) / values.shape[-1])
    angles = position.astype(jnp.float32)[:, None] * frequency[None, :]
    angles = jnp.concatenate([angles, angles], axis=-1)[:, None, :]
    leading = values[..., :half_dim]
    trailing = values[..., half_dim:]
    turned = jnp.concatenate([-trailing, leading], axis=-1)
    return values * jnp.cos(angles) + turned * jnp.sin(angles)


def attend(block_states, segment, position, gain_row, qkv_weight, out_weight):
    token_count = block_states.shape[0]
    group_size = HEADS // KV_HEADS
    normed = root_norm(block_states, gain_row).astype(jnp.bfloat16)
    mixed = jnp.dot(normed, qkv_weight, preferred_element_type=jnp.float32)
    queries = rotary(
        mixed[:, : HEADS * HEAD_DIM].reshape(token_count, HEADS, HEAD_DIM), position
    ).astype(jnp.bfloat16)
    keys_all = rotary(
        mixed[:, HEADS * HEAD_DIM : (HEADS + KV_HEADS) * HEAD_DIM].reshape(
            token_count, KV_HEADS, HEAD_DIM
        ),
        position,
    ).astype(jnp.bfloat16)
    values_all = (
        mixed[:, (HEADS + KV_HEADS) * HEAD_DIM :]
        .reshape(token_count, KV_HEADS, HEAD_DIM)
        .astype(jnp.bfloat16)
    )
    grouped = queries.reshape(token_count, KV_HEADS, group_size, HEAD_DIM)
    scores = (
        jnp.einsum("tgqd,sgd->gqts", grouped, keys_all, preferred_element_type=jnp.float32)
        * SCORE_SCALE
    )
    places = jnp.arange(token_count, dtype=jnp.int32)
    allowed = (segment[:, None] == segment[None, :]) & (places[None, :] <= places[:, None])
    scores = jnp.where(allowed, scores, -1e30)
    highest = jnp.max(scores, axis=-1, keepdims=True)
    weights = jnp.exp(scores - highest)
    weights = (weights / jnp.sum(weights, axis=-1, keepdims=True)).astype(jnp.bfloat16)
    attended = jnp.einsum(
        "gqts,sgd->tgqd", weights, values_all, preferred_element_type=jnp.float32
    ).astype(jnp.bfloat16)
    projected = jnp.dot(
        attended.reshape(token_count, HEADS * HEAD_DIM),
        out_weight,
        preferred_element_type=jnp.float32,
    )
    return (block_states.astype(jnp.float32) + RESIDUAL_SCALE * projected).astype(jnp.bfloat16)


def join_parts(first_part, second_part):
    first_max, first_mass, first_hit = first_part
    second_max, second_mass, second_hit = second_part
    joined_max = jnp.maximum(first_max, second_max)
    joined_mass = first_mass * jnp.exp(first_max - joined_max) + second_mass * jnp.exp(
        second_max - joined_max
    )
    return (joined_max, joined_mass, first_hit + second_hit)


def per_device(
    states,
    lengths,
    targets,
    routes,
    gate_probs,
    owners,
    norm_gains,
    qkv_weight,
    out_weight,
    expert_in,
    expert_down,
    vocab_head,
):
    token_count = states.shape[1]
    width = states.shape[2]
    segment, member, position = segment_table(lengths[0], token_count)
    residual = jnp.stack(
        [
            attend(
                states[which],
                segment,
                position,
                norm_gains[which, 0],
                qkv_weight[which],
                out_weight[which],
            )
            for which in range(2)
        ]
    )
    moe_in = root_norm(residual, norm_gains[:, 1][:, None, :]).astype(jnp.bfloat16)
    groups = lax.axis_size("exp")
    local_count = expert_in.shape[1]
    flat_routes = routes.reshape(2, token_count * TOP)
    onehot = (flat_routes[..., None] == jnp.arange(EXPERTS, dtype=jnp.int32)).astype(jnp.int32)
    rank_slot = jnp.sum((jnp.cumsum(onehot, axis=1) - 1) * onehot, axis=2)
    slot_index = (
        flat_routes * CAP + rank_slot + jnp.arange(2, dtype=jnp.int32)[:, None] * (EXPERTS * CAP)
    ).reshape(-1)
    token_index = jnp.arange(token_count * TOP, dtype=jnp.int32) // TOP
    outgoing = (
        jnp.zeros((2 * EXPERTS * CAP, width), jnp.bfloat16)
        .at[slot_index]
        .set(moe_in[:, token_index].reshape(-1, width))
    )
    arrived = lax.all_to_all(
        outgoing.reshape(2, groups, local_count * CAP, width),
        "exp",
        split_axis=1,
        concat_axis=1,
        tiled=True,
    )
    inputs = arrived.reshape(2, groups, local_count, CAP, width)
    gate_up = jnp.einsum("mslcd,mldf->mslcf", inputs, expert_in, preferred_element_type=jnp.float32)
    hidden = (jax.nn.silu(gate_up[..., :EXPERT_FF]) * gate_up[..., EXPERT_FF:]).astype(jnp.bfloat16)
    produced = jnp.einsum(
        "mslcf,mlfd->mslcd", hidden, expert_down, preferred_element_type=jnp.float32
    ).astype(jnp.bfloat16)
    returned = lax.all_to_all(
        produced.reshape(2, groups, local_count * CAP, width),
        "exp",
        split_axis=1,
        concat_axis=1,
        tiled=True,
    )
    picked = returned.reshape(2 * EXPERTS * CAP, width)[slot_index].reshape(
        2, token_count, TOP, width
    )
    mixture = jnp.sum(gate_probs[..., None] * picked.astype(jnp.float32), axis=2)
    final = root_norm(
        residual.astype(jnp.float32) + RESIDUAL_SCALE * mixture, norm_gains[:, 2][:, None, :]
    ).astype(jnp.bfloat16)
    shard = lax.axis_index("exp")
    vocab_rows = vocab_head.shape[1]
    lowest = shard * vocab_rows
    vocab_ids = jnp.arange(vocab_rows, dtype=jnp.int32)
    shard_piece = lax.all_gather(final, "exp", axis=1, tiled=True)
    piece_rows = shard_piece.shape[1]
    block_rows = 512
    block_count = piece_rows // block_rows
    wanted_all = targets - lowest

    def one_block(block_number):
        row_block = lax.dynamic_slice_in_dim(shard_piece, block_number * block_rows, block_rows, 1)
        wanted = lax.dynamic_slice_in_dim(wanted_all, block_number * block_rows, block_rows, 0)
        logits = (
            jnp.einsum("mtd,mvd->mtv", row_block, vocab_head, preferred_element_type=jnp.float32)
            / LOGIT_DIVISOR
        )
        highest = jnp.max(logits, axis=2)
        masses = jnp.sum(jnp.exp(logits - highest[..., None]), axis=2)
        chosen = jnp.sum(
            jnp.where(wanted[None, :, None] == vocab_ids[None, None, :], logits, 0.0), axis=2
        )
        return (highest, masses, chosen)

    block_max, block_mass, block_hit = lax.map(one_block, jnp.arange(block_count, dtype=jnp.int32))

    def place(fresh):
        ordered = jnp.transpose(fresh, (1, 0, 2)).reshape(2, piece_rows)
        return ordered

    part_max = place(block_max)
    part_mass = place(block_mass)
    part_hit = place(block_hit)
    all_max, all_mass, all_hit = combined_all((part_max, part_mass, part_hit), "exp", join_parts)
    begin = shard * token_count
    final_max = lax.dynamic_slice_in_dim(all_max, begin, token_count, 1)
    final_mass = lax.dynamic_slice_in_dim(all_mass, begin, token_count, 1)
    final_hit = lax.dynamic_slice_in_dim(all_hit, begin, token_count, 1)
    token_logp = final_hit - (final_max + jnp.log(final_mass))
    difference = token_logp[0] - token_logp[1]
    seq_sums = jnp.sum(member.astype(jnp.float32) * difference[:, None], axis=0)
    devices = lax.axis_size("req") * lax.axis_size("exp")
    everyone = devices * seq_sums.shape[0]
    dense_totals = jnp.sum(
        (owners[:, None] == jnp.arange(everyone, dtype=jnp.int32)[None, :]).astype(jnp.float32)
        * seq_sums[:, None],
        axis=0,
    )
    seq_totals = lax.psum_scatter(dense_totals, ("req", "exp"), scatter_dimension=0, tiled=True)
    return (token_logp, seq_totals)


def solution(mesh):
    in_specs = (
        P(None, ("req", "exp"), None),
        P(("req", "exp"), None),
        P("req"),
        P(None, ("req", "exp"), None),
        P(None, ("req", "exp"), None),
        P(("req", "exp")),
        P(),
        P(),
        P(),
        P(None, "exp", None, None),
        P(None, "exp", None, None),
        P(None, "exp", None),
    )
    out_specs = (P(None, ("req", "exp")), P(("req", "exp")))
    return jax.shard_map(
        per_device, mesh=mesh, in_specs=in_specs, out_specs=out_specs, check_vma=False
    )
```

profile of v0, /device:TPU:1, one launch (start us, length us, event | category | flops | bytes accessed | tf_op | source)
XLA Modules:
  0.0 671.6 jit_solution(7500306601122006520)
XLA Ops:
  9.4 3.1 fusion.15
  21.6 3.1 fusion.13
  41.6 2.8 convolution_convert_fusion.1
  47.5 15.8 %gather_fusion = bf16[1024,2,1024]{2,1,0:T(2,128)(2,1)} fusion(bf16[2,128,1024]{2,0,1:T(2,128)(2,1)S(1)} %copy.125, s32[1024]{0:T(1024)S(1)} %broadcast_clamp_fusion.1), kind=kCustom, calls=%fused_computation | custom fusion | bytes 8392704 | tf_op jit(solution)/shard_map/gather | solution.py:153
  63.3 5.6 copy.126
  68.9 18.0 %reduce-window.11 = s32[2,32,8,128]{3,2,1,0:T(8,128)S(1)} reduce-window(s32[2,32,8,128]{3,2,1,0:T(8,128)S(1)} %fusion.101, s32[]{:T(128)} %constant.119.clone.1), window={size=1x1x1x128 pad=0_0x0_0x0_0x127_0}, to_apply=%region_9.10 | reduce-window | flops 8323072 | bytes 524292 | tf_op jit(solution)/shard_map/reduce-window.1
  88.0 13.6 %scatter_custom_fusion = bf16[2560,1024]{1,0:T(8,128)(2,1)} fusion(s32[2048]{0:T(1024)S(1)} %bitcast.262, bf16[2048,1024]{1,0:T(8,128)(2,1)} %bitcast.240, bf16[]{:T(256)} %constant.129.clone.1), kind=kCustom, calls=%fused_computation.37 | custom fusion | bytes 5243392 | tf_op jit(solution)/shard_map/scatter | solution.py:153
  101.7 3.3 copy.127
  105.0 71.5 %all_to_all.10 = bf16[2,32,40,1024]{3,2,0,1:T(8,128)(2,1)S(1)} all-to-all(bf16[2,32,40,1024]{3,2,0,1:T(8,128)(2,1)S(1)} %copy.127), channel_id=1, replica_groups=mesh['req'=4,'exp'=32] {'exp'}, dimensions={1} | all-to-all | bytes 10485760 | tf_op jit(solution)/shard_map/all_to_all | solution.py:155
  176.5 8.2 %fusion.19 = f32[2,32,1,40,1024]{4,3,1,0,2:T(8,128)} fusion(bf16[2,1,1024,1024]{3,2,1,0:T(8,128)(2,1)S(1)} %copy-done.20, bf16[2,32,40,1024]{3,2,0,1:T(8,128)(2,1)S(1)} %all_to_all.10), kind=kOutput, calls=%fused_computation.34 | convolution fusion | flops 5368709120 | bytes 19922944 | tf_op jit(solution)/shard_map/mslcd,mldf->mslcf/dot_general | solution.py:163
  184.7 7.2 %convolution_convert_fusion = bf16[2,32,40,1024]{3,2,1,0:T(8,128)(2,1)S(1)} fusion(f32[2,32,1,40,1024]{4,3,1,0,2:T(8,128)} %fusion.19, bf16[2,1,512,1024]{3,2,1,0:T(8,128)(2,1)S(1)} %copy-done), kind=kOutput, calls=%fused_computation.35 | convolution fusion | flops 2694840320 | bytes 17825792 | tf_op jit(solution)/shard_map/mslcf,mlfd->mslcd/dot_general | solution.py:165
  191.8 3.2 copy.129
  195.0 5.0 all-to-all-start.1
  200.2 61.7 %all-to-all-done.1 = bf16[2,32,40,1024]{3,2,0,1:T(8,128)(2,1)} async-done(((bf16[2,32,40,1024]{3,2,0,1:T(8,128)(2,1)}), bf16[2,32,40,1024]{3,2,0,1:T(8,128)(2,1)}, u32[]{:S(2)}, u32[]{:S(2)}) %all-to-all-start.1) | async-done | bytes 5242912 | tf_op jit(solution)/shard_map/all_to_all | solution.py:168
  261.9 5.6 copy.130
  267.5 14.1 %gather_fusion.1 = bf16[2048,1024]{1,0:T(8,128)(2,1)} fusion(bf16[2560,1024]{1,0:T(8,128)(2,1)} %bitcast.231, s32[2048]{0:T(1024)S(1)} %broadcast_clamp_fusion), kind=kCustom, calls=%fused_computation.1 | custom fusion | bytes 8396800 | tf_op jit(solution)/shard_map/gather | solution.py:175
  281.6 4.8 fusion.8
  287.8 73.6 %all-gather.5.cloned.1.call-done = bf16[2,4096,1024]{2,1,0:T(8,128)(2,1)} async-done(((bf16[2,128,1024]{2,1,0:T(8,128)(2,1)}), bf16[2,4096,1024]{2,1,0:T(8,128)(2,1)}) %all-gather.5.cloned.1.call-update) | async-done | bytes 16777232 | tf_op jit(solution)/shard_map/all_gather | solution.py:186
  361.4 79.6 %while.35 = (s32[]{:T(128)}, f32[8,2,512]{2,1,0:T(2,128)S(1)}, f32[8,2,512]{2,1,0:T(2,128)}, f32[8,2,512]{2,1,0:T(2,128)}, s32[8]{0:T(128)S(1)}, /*index=5*/bf16...) while((s32[]{:T(128)}, f32[8,2,512]{2,1,0:T(2,128)S(1)}, ...), condition=%wide.region_20.21_spmd.clone, body=%wide.region_16.20_spmd.clone.sunk | while | flops 2423583744 | bytes 17480380 | solution.py:206
  362.7 6.0 fusion.161
  372.6 6.0 fusion.161
  382.6 6.0 fusion.161
  392.5 6.0 fusion.161
  402.5 6.0 fusion.161
  412.4 6.0 fusion.161
  422.4 6.0 fusion.161
  432.3 6.0 fusion.161
  442.4 40.9 %all-gather.11.cloned.1.call-done = f32[32,2,4096]{2,1,0:T(2,128)} async-done(((f32[1,2,4096]{2,1,0:T(2,128)}), f32[32,2,4096]{2,1,0:T(2,128)}) %all-gather.11.cloned.1.call-update) | async-done | bytes 1048592 | tf_op jit(solution)/shard_map/all_gather | solution.py:23
  484.0 43.5 %all-gather.9.cloned.1.call-done = f32[32,2,4096]{2,1,0:T(2,128)} async-done(((f32[1,2,4096]{2,1,0:T(2,128)}), f32[32,2,4096]{2,1,0:T(2,128)}) %all-gather.9.cloned.1.call-update) | async-done | bytes 1048592 | tf_op jit(solution)/shard_map/all_gather | solution.py:23
  528.2 43.4 %all-gather.7.cloned.1.call-done = f32[32,2,4096]{2,1,0:T(2,128)} async-done(((f32[1,2,4096]{2,1,0:T(2,128)}), f32[32,2,4096]{2,1,0:T(2,128)}) %all-gather.7.cloned.1.call-update) | async-done | bytes 1048592 | tf_op jit(solution)/shard_map/all_gather | solution.py:23
  572.4 27.7 %while.34 = (s32[]{:T(128)}, f32[2,4096]{1,0:T(2,128)S(1)}, f32[2,4096]{1,0:T(2,128)S(1)}, f32[2,4096]{1,0:T(2,128)S(1)}, f32[32,2,4096]{2,1,0:T(2,128)}, /*inde...) while((s32[]{:T(128)}, f32[2,4096]{1,0:T(2,128)S(1)}, ...), condition=%wide.region_22.23_spmd, body=%wide.region_21.22_spmd.sunk | while | flops 57349 | bytes 295059 | solution.py:29
  600.3 64.1 %all-reduce = f32[512]{0:T(512)S(1)} all-reduce(f32[512]{0:T(512)S(1)} %select_reduce_fusion.1), channel_id=2, replica_groups=mesh['req'=4,'exp'=32] {'req','exp'}, use_global_device_ids=true, to_apply=%region_25.26.clone | all-reduce | flops 512 | bytes 4096
  (211 shorter events, 91.7 us)
Async XLA Ops:
  7.2 177.5 %copy-start = (bf16[2,1,512,1024]{3,2,1,0:T(8,128)(2,1)S(1)}, bf16[2,1,512,1024]{3,2,1,0:T(8,128)(2,1)}, u32[]{:S(2)}) copy-start(bf16[2,1,512,1024]{3,2,1,0:T(8,128)(2,1)} %param.26) | copy-start | bytes 6291460
  9.3 5.2 copy-start.21
  12.4 1.0 copy-start.2
  14.9 0.6 copy-start.15
  24.7 1.0 copy-start.3
  25.7 6.6 copy-start.11
  25.7 7.2 %copy-start.8 = (s32[2,128,8]{1,2,0:T(8,128)S(1)}, s32[2,128,8]{1,2,0:T(8,128)}, u32[]{:S(2)}) copy-start(s32[2,128,8]{1,2,0:T(8,128)} %param.19) | copy-start | bytes 24580
  31.3 8.2 %copy-start.4 = (bf16[2,128,1024]{2,1,0:T(8,128)(2,1)S(1)}, bf16[2,128,1024]{2,1,0:T(8,128)(2,1)}, u32[]{:S(2)}) copy-start(bf16[2,128,1024]{2,1,0:T(8,128)(2,1)} %param.16) | copy-start | bytes 1572868
  39.4 5.0 copy-start.5
  41.6 5.9 copy-start.13
  63.3 5.6 copy-start.7
  63.3 24.2 %copy-start.6 = (s32[2,1024]{1,0:T(2,128)S(1)}, s32[2,1024]{1,0:T(2,128)}, u32[]{:S(2)}) copy-start(s32[2,1024]{1,0:T(2,128)} %eq.95) | copy-start | bytes 24580
  63.3 24.3 %copy-start.9 = (s32[2,128,8]{1,2,0:T(8,128)S(1)}, s32[2,128,8]{1,2,0:T(8,128)}, u32[]{:S(2)}) copy-start(s32[2,128,8]{1,2,0:T(8,128)} %broadcast_multiply_fusion.1) | copy-start | bytes 24580
  63.3 24.6 %copy-start.18 = (s32[2]{0:T(128)S(1)}, s32[2]{0:T(128)}, u32[]{:S(2)}) copy-start(s32[2]{0:T(128)} %iota_multiply_fusion) | copy-start | bytes 28
  105.0 71.5 %copy-start.20 = (bf16[2,1,1024,1024]{3,2,1,0:T(8,128)(2,1)S(1)}, bf16[2,1,1024,1024]{3,2,1,0:T(8,128)(2,1)}, u32[]{:S(2)}) copy-start(bf16[2,1,1024,1024]{3,2,1,0:T(8,128)(2,1)} %param.25) | copy-start | bytes 12582916
  195.0 5.0 copy-start.14
  195.0 66.9 %all-to-all-start.1 = ((bf16[2,32,40,1024]{3,2,0,1:T(8,128)(2,1)}), bf16[2,32,40,1024]{3,2,0,1:T(8,128)(2,1)}, u32[]{:S(2)}, u32[]{:S(2)}) async-start(bf16[2,32,40,1024]{3,2,0,1:T(8,128)(2,1)} %copy.129), calls=%async_computation.1 | async-start | bytes 10485760 | tf_op jit(solution)/shard_map/all_to_all | solution.py:168
  200.0 161.4 %all-gather.5.cloned.1.call-start = ((), (), s32[]{:S(2)}) async-start(), calls=%async_computation.2 | async-start | bytes 17301504 | tf_op jit(solution)/shard_map/all_gather | solution.py:186
  281.6 6.2 copy-start.12
  287.7 195.5 %all-gather.11.cloned.1.call-start = ((), (), s32[]{:S(2)}) async-start(), calls=%async_computation.5 | async-start | bytes 1081344 | tf_op jit(solution)/shard_map/all_gather | solution.py:23
  361.4 238.7 %copy-start.16 = (s32[128]{0:T(128)S(1)}, s32[128]{0:T(128)}, u32[]{:S(2)}) copy-start(s32[128]{0:T(128)} %copy-done.15) | copy-start | bytes 1540
  361.4 238.8 %copy-start.19 = (s32[4]{0:T(128)S(1)}, s32[4]{0:T(128)}, u32[]{:S(2)}) copy-start(s32[4]{0:T(128)} %param.21) | copy-start | bytes 52
  441.0 0.8 copy-start.10
  441.0 224.0 %copy-start.1 = (bf16[2,1,512,1024]{3,2,1,0:T(8,128)(2,1)S(1)}, bf16[2,1,512,1024]{3,2,1,0:T(8,128)(2,1)}, u32[]{:S(2)}) copy-start(bf16[2,1,512,1024]{3,2,1,0:T(8,128)(2,1)} %param.26) | copy-start | bytes 6291460
  441.0 86.4 %all-gather.9.cloned.1.call-start = ((), (), s32[]{:S(2)}) async-start(), calls=%async_computation.4 | async-start | bytes 1081344 | tf_op jit(solution)/shard_map/all_gather | solution.py:23
  441.8 129.8 %all-gather.7.cloned.1.call-start = ((), (), s32[]{:S(2)}) async-start(), calls=%async_computation.3 | async-start | bytes 1081344 | tf_op jit(solution)/shard_map/all_gather | solution.py:23
  600.1 65.0 %copy-start.17 = (f32[2,128]{1,0:T(2,128)}, f32[2,128]{1,0:T(2,128)S(1)}, u32[]{:S(2)}) copy-start(f32[2,128]{1,0:T(2,128)S(1)} %add_subtract_fusion) | copy-start | bytes 3076
Sparse Core Ops, SparseCore 0:
  287.8 73.5 all-gather.4
  441.2 42.0 all-gather.10
  485.5 41.9 all-gather.8
  529.6 41.9 all-gather.6
where the time goes:
time: 675 us; the launch traced here: 672 us
  waiting for transfers between devices  264 us (39%)
  blocking collectives  136 us (20%)
  matrix products  88 us (13%)
  local copies, waits for them, and re-layouts  84.9 us (13%)
  other arithmetic  73.5 us (11%)
  between operations  14.3 us (2%)
    all_gather x3, waiting for transfers between devices, combined_all(): everything = jax.tree.map(lambda part: lax.all_gather(part, axis), x)  128 us
    all_gather x1, waiting for transfers between devices, per_device(): shard_piece = lax.all_gather(final, 'exp', axis=1, tiled=True)  73.6 us
    all_to_all x1, blocking collectives, per_device(): lax.all_to_all(outgoing.reshape(2, groups, local_count * CAP, width), 'ex...  71.5 us
    unnamed x1, blocking collectives  64.1 us
    all_to_all x1, waiting for transfers between devices, per_device(): lax.all_to_all(produced.reshape(2, groups, local_count * CAP, width), 'ex...  61.7 us
    dot_general x8, matrix products, one_block(): jnp.einsum('mtd,mvd->mtv', row_block, vocab_head, preferred_element_type=...  47.9 us
    add x31, other arithmetic, join_parts(): first_mass * jnp.exp(first_max - joined_max)  27.2 us
    gather x2, local copies, waits for them, and re-layouts, per_device(): moe_in[:, token_index].reshape(-1, width)  21.3 us
  transfers between devices with their start and end apart: 5, of which 5 were waited for; matrix products, arithmetic and copies ran while one was open for 0% of the time, Pallas kernels for 0%

commit v1 on v0

--- a/solution.py
+++ b/solution.py
@@ -209,25 +209,31 @@
         ordered = jnp.transpose(fresh, (1, 0, 2)).reshape(2, piece_rows)
         return ordered
 
-    part_max = place(block_max)
-    part_mass = place(block_mass)
-    part_hit = place(block_hit)
-    all_max, all_mass, all_hit = combined_all((part_max, part_mass, part_hit), "exp", join_parts)
-    begin = shard * token_count
-    final_max = lax.dynamic_slice_in_dim(all_max, begin, token_count, 1)
-    final_mass = lax.dynamic_slice_in_dim(all_mass, begin, token_count, 1)
-    final_hit = lax.dynamic_slice_in_dim(all_hit, begin, token_count, 1)
+    groups_exp = lax.axis_size("exp")
+    stacked = jnp.stack([place(block_max), place(block_mass), place(block_hit)])
+    stacked = jnp.transpose(stacked.reshape(3, 2, groups_exp, token_count), (2, 0, 1, 3))
+    gathered = lax.all_to_all(stacked, "exp", 0, 0, tiled=True)
+    all_max = gathered[:, 0]
+    all_mass = gathered[:, 1]
+    all_hit = gathered[:, 2]
+    final_max = jnp.max(all_max, axis=0)
+    final_mass = jnp.sum(all_mass * jnp.exp(all_max - final_max[None]), axis=0)
+    final_hit = jnp.sum(all_hit, axis=0)
     token_logp = final_hit - (final_max + jnp.log(final_mass))
     difference = token_logp[0] - token_logp[1]
     seq_sums = jnp.sum(member.astype(jnp.float32) * difference[:, None], axis=0)
     devices = lax.axis_size("req") * lax.axis_size("exp")
-    everyone = devices * seq_sums.shape[0]
+    per_device_seqs = seq_sums.shape[0]
+    everyone = devices * per_device_seqs
     dense_totals = jnp.sum(
         (owners[:, None] == jnp.arange(everyone, dtype=jnp.int32)[None, :]).astype(jnp.float32)
         * seq_sums[:, None],
         axis=0,
     )
-    seq_totals = lax.psum_scatter(dense_totals, ("req", "exp"), scatter_dimension=0, tiled=True)
+    delivered = lax.all_to_all(
+        dense_totals.reshape(devices, per_device_seqs), ("req", "exp"), 0, 0, tiled=True
+    )
+    seq_totals = jnp.sum(delivered, axis=0)
     return (token_logp, seq_totals)
 
 

time: 675 us -> 474 us (0.70)
  waiting for transfers between devices: 264 us -> 135 us
  blocking collectives: 136 us -> 99.2 us
  other arithmetic: 73.5 us -> 47.1 us
  local copies, waits for them, and re-layouts: 84.9 us -> 77.7 us
    all_gather x3 -> x0, waiting for transfers between devices: 128 us -> none  [combined_all(): everything = jax.tree.map(lambda part: lax.all_gather(part, axis), x)]
    unnamed x1 -> x0, blocking collectives: 64.1 us -> none
    all_to_all x0 -> x2, blocking collectives: none -> 27.7 us  [the longest x1 15 us: per_device(): lax.all_to_all(dense_totals.reshape(devices, per_device_seqs), ('req', 'e...]
    add x31 -> x0, other arithmetic: 27.2 us -> none  [join_parts(): first_mass * jnp.exp(first_max - joined_max)]
  transfers between devices with their start and end apart: 5 -> 2, of which waited for: 5 -> 2; matrix products, arithmetic and copies ran while one was open for 0% -> 0% of each run, Pallas kernels for 0% -> 0%
where the time goes in v1:
time: 474 us; the launch traced here: 473 us
  waiting for transfers between devices  135 us (28%)
  blocking collectives  99.2 us (21%)
  matrix products  88 us (19%)
  local copies, waits for them, and re-layouts  77.7 us (16%)
  other arithmetic  47.1 us (10%)
  between operations  14.6 us (3%)
  loops' own time  5.49 us (1%)
  starting transfers between devices  5.02 us (1%)
    all_gather x1, waiting for transfers between devices, per_device(): shard_piece = lax.all_gather(final, 'exp', axis=1, tiled=True)  73.6 us
    all_to_all x1, blocking collectives, per_device(): lax.all_to_all(outgoing.reshape(2, groups, local_count * CAP, width), 'ex...  71.5 us
    all_to_all x1, waiting for transfers between devices, per_device(): lax.all_to_all(produced.reshape(2, groups, local_count * CAP, width), 'ex...  61.7 us
    dot_general x8, matrix products, one_block(): jnp.einsum('mtd,mvd->mtv', row_block, vocab_head, preferred_element_type=...  47.9 us
    gather x2, local copies, waits for them, and re-layouts, per_device(): moe_in[:, token_index].reshape(-1, width)  21.3 us
    another operation x6, other arithmetic  18.2 us
    all_to_all x1, blocking collectives, per_device(): lax.all_to_all(dense_totals.reshape(devices, per_device_seqs), ('req', 'e...  15 us
    gather x1, local copies, waits for them, and re-layouts, per_device(): returned.reshape(2 * EXPERTS * CAP, width)[slot_index]  14.4 us
  transfers between devices with their start and end apart: 2, of which 2 were waited for; matrix products, arithmetic and copies ran while one was open for 0% of the time, Pallas kernels for 0%

profile of v1, /device:TPU:1, one launch (start us, length us, event | category | flops | bytes accessed | tf_op | source)
XLA Modules:
  0.0 472.6 jit_solution(2140811398933638405)
XLA Ops:
  9.4 3.1 fusion.13
  15.5 2.3 fusion.40
  21.5 3.1 fusion.11
  26.7 2.4 fusion.38
  36.6 2.7 convolution_convert_fusion.2
  41.6 2.8 convolution_convert_fusion.1
  47.5 15.8 %gather_fusion = bf16[1024,2,1024]{2,1,0:T(2,128)(2,1)} fusion(bf16[2,128,1024]{2,0,1:T(2,128)(2,1)S(1)} %copy.143, s32[1024]{0:T(1024)S(1)} %broadcast_clamp_fusion.1), kind=kCustom, calls=%fused_computation | custom fusion | bytes 8392704 | tf_op jit(solution)/shard_map/gather | solution.py:153
  63.2 5.6 %copy.144 = bf16[2,1024,1024]{2,1,0:T(8,128)(2,1)} copy(bf16[2,1024,1024]{2,0,1:T(2,128)(2,1)} %bitcast.223) | data formatting | bytes 8388608 | tf_op jit(solution)/shard_map/gather | solution.py:153
  68.8 18.0 %reduce-window.11 = s32[2,32,8,128]{3,2,1,0:T(8,128)S(1)} reduce-window(s32[2,32,8,128]{3,2,1,0:T(8,128)S(1)} %fusion.99, s32[]{:T(128)} %constant.53.clone.1), window={size=1x1x1x128 pad=0_0x0_0x0_0x127_0}, to_apply=%region_9.10 | reduce-window | flops 8323072 | bytes 524292 | tf_op jit(solution)/shard_map/reduce-window.1
  87.9 13.6 %scatter_custom_fusion = bf16[2560,1024]{1,0:T(8,128)(2,1)} fusion(s32[2048]{0:T(1024)S(1)} %bitcast.253, bf16[2048,1024]{1,0:T(8,128)(2,1)} %bitcast.230, bf16[]{:T(256)} %constant.91.clone.1), kind=kCustom, calls=%fused_computation.31 | custom fusion | bytes 5243392 | tf_op jit(solution)/shard_map/scatter | solution.py:153
  101.6 3.3 copy.145
  104.9 71.5 %all_to_all.24 = bf16[2,32,40,1024]{3,2,0,1:T(8,128)(2,1)S(1)} all-to-all(bf16[2,32,40,1024]{3,2,0,1:T(8,128)(2,1)S(1)} %copy.145), channel_id=1, replica_groups=mesh['req'=4,'exp'=32] {'exp'}, dimensions={1} | all-to-all | bytes 10485760 | tf_op jit(solution)/shard_map/all_to_all | solution.py:155
  176.4 8.2 %fusion.17 = f32[2,32,1,40,1024]{4,3,1,0,2:T(8,128)} fusion(bf16[2,1,1024,1024]{3,2,1,0:T(8,128)(2,1)S(1)} %copy-done.19, bf16[2,32,40,1024]{3,2,0,1:T(8,128)(2,1)S(1)} %all_to_all.24), kind=kOutput, calls=%fused_computation.28 | convolution fusion | flops 5368709120 | bytes 19922944 | tf_op jit(solution)/shard_map/mslcd,mldf->mslcf/dot_general | solution.py:163
  184.6 7.2 %convolution_convert_fusion = bf16[2,32,40,1024]{3,2,1,0:T(8,128)(2,1)S(1)} fusion(f32[2,32,1,40,1024]{4,3,1,0,2:T(8,128)} %fusion.17, bf16[2,1,512,1024]{3,2,1,0:T(8,128)(2,1)S(1)} %copy-done), kind=kOutput, calls=%fused_computation.29 | convolution fusion | flops 2694840320 | bytes 17825792 | tf_op jit(solution)/shard_map/mslcf,mlfd->mslcd/dot_general | solution.py:165
  191.8 3.2 copy.147
  195.0 5.0 %all-to-all-start.1 = ((bf16[2,32,40,1024]{3,2,0,1:T(8,128)(2,1)}), bf16[2,32,40,1024]{3,2,0,1:T(8,128)(2,1)}, u32[]{:S(2)}, u32[]{:S(2)}) async-start(bf16[2,32,40,1024]{3,2,0,1:T(8,128)(2,1)} %copy.147), calls=%async_computation.1 | async-start | bytes 10485760 | tf_op jit(solution)/shard_map/all_to_all | solution.py:168
  200.1 61.7 %all-to-all-done.1 = bf16[2,32,40,1024]{3,2,0,1:T(8,128)(2,1)} async-done(((bf16[2,32,40,1024]{3,2,0,1:T(8,128)(2,1)}), bf16[2,32,40,1024]{3,2,0,1:T(8,128)(2,1)}, u32[]{:S(2)}, u32[]{:S(2)}) %all-to-all-start.1) | async-done | bytes 5242912 | tf_op jit(solution)/shard_map/all_to_all | solution.py:168
  261.8 5.6 %copy.148 = bf16[2,32,40,1024]{3,2,1,0:T(8,128)(2,1)} copy(bf16[2,32,40,1024]{3,2,0,1:T(8,128)(2,1)} %all-to-all-done.1) | data formatting | bytes 10485760 | tf_op jit(solution)/shard_map/all_to_all | solution.py:168
  267.4 14.4 %gather_fusion.1 = bf16[2048,1024]{1,0:T(8,128)(2,1)} fusion(bf16[2560,1024]{1,0:T(8,128)(2,1)} %bitcast.221, s32[2048]{0:T(1024)S(1)} %broadcast_clamp_fusion), kind=kCustom, calls=%fused_computation.1 | custom fusion | bytes 8396800 | tf_op jit(solution)/shard_map/gather | solution.py:175
  281.8 4.8 %fusion.6 = f32[2,128,1024]{2,1,0:T(8,128)S(1)} fusion(f32[2,128,8]{2,1,0:T(8,128)S(1)} %copy.137, bf16[2048,1024]{1,0:T(8,128)(2,1)} %gather_fusion.1), kind=kLoop, calls=%fused_computation.16 | loop fusion | flops 6029312 | bytes 5251072 | tf_op jit(solution)/shard_map/reduce_sum | solution.py:178
  287.9 73.6 %all-gather.2.cloned.1.call-done = bf16[2,4096,1024]{2,1,0:T(8,128)(2,1)} async-done(((bf16[2,128,1024]{2,1,0:T(8,128)(2,1)}), bf16[2,4096,1024]{2,1,0:T(8,128)(2,1)}) %all-gather.2.cloned.1.call-update) | async-done | bytes 16777232 | tf_op jit(solution)/shard_map/all_gather | solution.py:186
  361.6 75.0 %while.15 = (s32[]{:T(128)}, f32[8,2,512]{2,1,0:T(2,128)S(1)}, f32[8,2,512]{2,1,0:T(2,128)S(1)}, f32[8,2,512]{2,1,0:T(2,128)S(1)}, s32[8]{0:T(128)S(1)}, /*index...) while((s32[]{:T(128)}, f32[8,2,512]{2,1,0:T(2,128)S(1)}, ...), condition=%wide.region_20.21_spmd.clone, body=%wide.region_16.20_spmd.clone.sunk | while | flops 2423583744 | bytes 17479872 | solution.py:206
  362.8 6.0 %fusion.160 = (f32[2,512]{1,0:T(2,128)S(1)}, f32[2,512,1152]{2,1,0:T(8,128)S(1)}) fusion(bf16[2,1152,1024]{2,1,0:T(8,128)(2,1)} %get-tuple-element.203, bf16[2,4096,1024]{2,1,0:T(8,128)(2,1)} %get-tuple-element.202, s32[]{:T(128)S(6)} %select_n.74), kind=kOutput, calls=%fused_computation.181.clone.1 | convolution fusion | flops 2418277376 | bytes 11538436 | tf_op jit(solution)/shard_map/while/body/eval_jaxpr/mtd,mvd->mtv/dot_general | solution.py:196
  372.2 6.0 %fusion.160 = (f32[2,512]{1,0:T(2,128)S(1)}, f32[2,512,1152]{2,1,0:T(8,128)S(1)}) fusion(bf16[2,1152,1024]{2,1,0:T(8,128)(2,1)} %get-tuple-element.203, bf16[2,4096,1024]{2,1,0:T(8,128)(2,1)} %get-tuple-element.202, s32[]{:T(128)S(6)} %select_n.74), kind=kOutput, calls=%fused_computation.181.clone.1 | convolution fusion | flops 2418277376 | bytes 11538436 | tf_op jit(solution)/shard_map/while/body/eval_jaxpr/mtd,mvd->mtv/dot_general | solution.py:196
  381.6 6.0 %fusion.160 = (f32[2,512]{1,0:T(2,128)S(1)}, f32[2,512,1152]{2,1,0:T(8,128)S(1)}) fusion(bf16[2,1152,1024]{2,1,0:T(8,128)(2,1)} %get-tuple-element.203, bf16[2,4096,1024]{2,1,0:T(8,128)(2,1)} %get-tuple-element.202, s32[]{:T(128)S(6)} %select_n.74), kind=kOutput, calls=%fused_computation.181.clone.1 | convolution fusion | flops 2418277376 | bytes 11538436 | tf_op jit(solution)/shard_map/while/body/eval_jaxpr/mtd,mvd->mtv/dot_general | solution.py:196
  391.0 6.0 %fusion.160 = (f32[2,512]{1,0:T(2,128)S(1)}, f32[2,512,1152]{2,1,0:T(8,128)S(1)}) fusion(bf16[2,1152,1024]{2,1,0:T(8,128)(2,1)} %get-tuple-element.203, bf16[2,4096,1024]{2,1,0:T(8,128)(2,1)} %get-tuple-element.202, s32[]{:T(128)S(6)} %select_n.74), kind=kOutput, calls=%fused_computation.181.clone.1 | convolution fusion | flops 2418277376 | bytes 11538436 | tf_op jit(solution)/shard_map/while/body/eval_jaxpr/mtd,mvd->mtv/dot_general | solution.py:196
  400.4 6.0 %fusion.160 = (f32[2,512]{1,0:T(2,128)S(1)}, f32[2,512,1152]{2,1,0:T(8,128)S(1)}) fusion(bf16[2,1152,1024]{2,1,0:T(8,128)(2,1)} %get-tuple-element.203, bf16[2,4096,1024]{2,1,0:T(8,128)(2,1)} %get-tuple-element.202, s32[]{:T(128)S(6)} %select_n.74), kind=kOutput, calls=%fused_computation.181.clone.1 | convolution fusion | flops 2418277376 | bytes 11538436 | tf_op jit(solution)/shard_map/while/body/eval_jaxpr/mtd,mvd->mtv/dot_general | solution.py:196
  409.7 6.0 %fusion.160 = (f32[2,512]{1,0:T(2,128)S(1)}, f32[2,512,1152]{2,1,0:T(8,128)S(1)}) fusion(bf16[2,1152,1024]{2,1,0:T(8,128)(2,1)} %get-tuple-element.203, bf16[2,4096,1024]{2,1,0:T(8,128)(2,1)} %get-tuple-element.202, s32[]{:T(128)S(6)} %select_n.74), kind=kOutput, calls=%fused_computation.181.clone.1 | convolution fusion | flops 2418277376 | bytes 11538436 | tf_op jit(solution)/shard_map/while/body/eval_jaxpr/mtd,mvd->mtv/dot_general | solution.py:196
  419.1 6.0 %fusion.160 = (f32[2,512]{1,0:T(2,128)S(1)}, f32[2,512,1152]{2,1,0:T(8,128)S(1)}) fusion(bf16[2,1152,1024]{2,1,0:T(8,128)(2,1)} %get-tuple-element.203, bf16[2,4096,1024]{2,1,0:T(8,128)(2,1)} %get-tuple-element.202, s32[]{:T(128)S(6)} %select_n.74), kind=kOutput, calls=%fused_computation.181.clone.1 | convolution fusion | flops 2418277376 | bytes 11538436 | tf_op jit(solution)/shard_map/while/body/eval_jaxpr/mtd,mvd->mtv/dot_general | solution.py:196
  428.5 6.0 %fusion.160 = (f32[2,512]{1,0:T(2,128)S(1)}, f32[2,512,1152]{2,1,0:T(8,128)S(1)}) fusion(bf16[2,1152,1024]{2,1,0:T(8,128)(2,1)} %get-tuple-element.203, bf16[2,4096,1024]{2,1,0:T(8,128)(2,1)} %get-tuple-element.202, s32[]{:T(128)S(6)} %select_n.74), kind=kOutput, calls=%fused_computation.181.clone.1 | convolution fusion | flops 2418277376 | bytes 11538436 | tf_op jit(solution)/shard_map/while/body/eval_jaxpr/mtd,mvd->mtv/dot_general | solution.py:196
  436.8 12.7 %all_to_all.25 = f32[32,3,2,128]{3,2,1,0:T(2,128)S(1)} all-to-all(f32[32,3,2,128]{3,2,1,0:T(2,128)S(1)} %copy.152), channel_id=1, replica_groups=mesh['req'=4,'exp'=32] {'exp'}, dimensions={0} | all-to-all | bytes 196608 | tf_op jit(solution)/shard_map/all_to_all | solution.py:215
  450.0 15.0 %all_to_all.26 = f32[128,1,4]{2,1,0:T(1,128)S(1)} all-to-all(f32[128,1,4]{2,1,0:T(1,128)S(1)} %bitcast.245), channel_id=1, replica_groups=mesh['req'=4,'exp'=32] {'req','exp'}, dimensions={0} | all-to-all | bytes 4096 | tf_op jit(solution)/shard_map/all_to_all | solution.py:233
  (178 shorter events, 49.2 us)
Async XLA Ops:
  7.2 177.4 %copy-start = (bf16[2,1,512,1024]{3,2,1,0:T(8,128)(2,1)S(1)}, bf16[2,1,512,1024]{3,2,1,0:T(8,128)(2,1)}, u32[]{:S(2)}) copy-start(bf16[2,1,512,1024]{3,2,1,0:T(8,128)(2,1)} %param.24) | copy-start | bytes 6291460
  9.3 5.2 %copy-start.20 = (s32[1,4]{1,0:T(1,128)S(1)}, s32[1,4]{1,0:T(1,128)}, u32[]{:S(2)}) copy-start(s32[1,4]{1,0:T(1,128)} %param.15) | copy-start | bytes 52
  12.4 1.0 copy-start.2
  14.9 0.5 copy-start.14
  24.6 1.0 copy-start.3
  25.6 6.6 %copy-start.10 = (f32[2,3,1024]{2,0,1:T(2,128)S(1)}, f32[2,3,1024]{2,0,1:T(2,128)}, u32[]{:S(2)}) copy-start(f32[2,3,1024]{2,0,1:T(2,128)} %param.20) | copy-start | bytes 73732
  25.6 7.2 %copy-start.8 = (s32[2,128,8]{1,2,0:T(8,128)S(1)}, s32[2,128,8]{1,2,0:T(8,128)}, u32[]{:S(2)}) copy-start(s32[2,128,8]{1,2,0:T(8,128)} %param.17) | copy-start | bytes 24580
  31.2 8.2 %copy-start.4 = (bf16[2,128,1024]{2,1,0:T(8,128)(2,1)S(1)}, bf16[2,128,1024]{2,1,0:T(8,128)(2,1)}, u32[]{:S(2)}) copy-start(bf16[2,128,1024]{2,1,0:T(8,128)(2,1)} %param.14) | copy-start | bytes 1572868
  39.3 5.0 %copy-start.5 = (bf16[2,128,1024]{2,1,0:T(8,128)(2,1)S(1)}, bf16[2,128,1024]{2,1,0:T(8,128)(2,1)}, u32[]{:S(2)}) copy-start(bf16[2,128,1024]{2,1,0:T(8,128)(2,1)} %param.14) | copy-start | bytes 1572868
  41.6 5.9 %copy-start.12 = (s32[1024,1]{0,1:T(1,128)S(1)}, s32[1024,1]{0,1:T(1,128)}, u32[]{:S(2)}) copy-start(s32[1024,1]{0,1:T(1,128)} %compare_select_fusion.1) | copy-start | bytes 12292
  63.2 5.6 %copy-start.7 = (s32[2,8,128]{2,1,0:T(8,128)S(1)}, s32[2,8,128]{2,1,0:T(8,128)}, u32[]{:S(2)}) copy-start(s32[2,8,128]{2,1,0:T(8,128)} %eq.99) | copy-start | bytes 24580
  63.2 24.2 %copy-start.6 = (s32[2,1024]{1,0:T(2,128)S(1)}, s32[2,1024]{1,0:T(2,128)}, u32[]{:S(2)}) copy-start(s32[2,1024]{1,0:T(2,128)} %eq.95) | copy-start | bytes 24580
  63.2 24.3 %copy-start.9 = (s32[2,128,8]{1,2,0:T(8,128)S(1)}, s32[2,128,8]{1,2,0:T(8,128)}, u32[]{:S(2)}) copy-start(s32[2,128,8]{1,2,0:T(8,128)} %broadcast_multiply_fusion.1) | copy-start | bytes 24580
  63.2 24.6 %copy-start.17 = (s32[2]{0:T(128)S(1)}, s32[2]{0:T(128)}, u32[]{:S(2)}) copy-start(s32[2]{0:T(128)} %iota_multiply_fusion) | copy-start | bytes 28
  104.9 71.5 %copy-start.19 = (bf16[2,1,1024,1024]{3,2,1,0:T(8,128)(2,1)S(1)}, bf16[2,1,1024,1024]{3,2,1,0:T(8,128)(2,1)}, u32[]{:S(2)}) copy-start(bf16[2,1,1024,1024]{3,2,1,0:T(8,128)(2,1)} %param.23) | copy-start | bytes 12582916
  195.0 5.0 %copy-start.13 = (f32[2,128,8]{1,2,0:T(8,128)S(1)}, f32[2,128,8]{1,2,0:T(8,128)}, u32[]{:S(2)}) copy-start(f32[2,128,8]{1,2,0:T(8,128)} %param.18) | copy-start | bytes 24580
  195.0 66.9 %all-to-all-start.1 = ((bf16[2,32,40,1024]{3,2,0,1:T(8,128)(2,1)}), bf16[2,32,40,1024]{3,2,0,1:T(8,128)(2,1)}, u32[]{:S(2)}, u32[]{:S(2)}) async-start(bf16[2,32,40,1024]{3,2,0,1:T(8,128)(2,1)} %copy.147), calls=%async_computation.1 | async-start | bytes 10485760 | tf_op jit(solution)/shard_map/all_to_all | solution.py:168
  199.9 161.7 %all-gather.2.cloned.1.call-start = ((), (), s32[]{:S(2)}) async-start(), calls=%async_computation.4 | async-start | bytes 17301504 | tf_op jit(solution)/shard_map/all_gather | solution.py:186
  281.8 6.1 %copy-start.11 = (s32[4096]{0:T(1024)S(1)}, s32[4096]{0:T(1024)}, u32[]{:S(2)}) copy-start(s32[4096]{0:T(1024)} %param.16) | copy-start | bytes 49156
  361.6 88.1 %copy-start.15 = (s32[128]{0:T(128)S(1)}, s32[128]{0:T(128)}, u32[]{:S(2)}) copy-start(s32[128]{0:T(128)} %copy-done.14) | copy-start | bytes 1540
  361.6 88.2 %copy-start.18 = (s32[4]{0:T(128)S(1)}, s32[4]{0:T(128)}, u32[]{:S(2)}) copy-start(s32[4]{0:T(128)} %param.19) | copy-start | bytes 52
  436.6 29.1 %copy-start.1 = (bf16[2,1,512,1024]{3,2,1,0:T(8,128)(2,1)S(1)}, bf16[2,1,512,1024]{3,2,1,0:T(8,128)(2,1)}, u32[]{:S(2)}) copy-start(bf16[2,1,512,1024]{3,2,1,0:T(8,128)(2,1)} %param.24) | copy-start | bytes 6291460
  449.7 16.0 %copy-start.16 = (f32[2,128]{1,0:T(2,128)}, f32[2,128]{1,0:T(2,128)S(1)}, u32[]{:S(2)}) copy-start(f32[2,128]{1,0:T(2,128)S(1)} %add_subtract_fusion) | copy-start | bytes 3076
Sparse Core Ops, SparseCore 0:
  288.0 73.5 all-gather.1

commit v2 on v1

--- a/solution.py
+++ b/solution.py
@@ -141,17 +141,23 @@
     groups = lax.axis_size("exp")
     local_count = expert_in.shape[1]
     flat_routes = routes.reshape(2, token_count * TOP)
-    onehot = (flat_routes[..., None] == jnp.arange(EXPERTS, dtype=jnp.int32)).astype(jnp.int32)
-    rank_slot = jnp.sum((jnp.cumsum(onehot, axis=1) - 1) * onehot, axis=2)
-    slot_index = (
-        flat_routes * CAP + rank_slot + jnp.arange(2, dtype=jnp.int32)[:, None] * (EXPERTS * CAP)
-    ).reshape(-1)
-    token_index = jnp.arange(token_count * TOP, dtype=jnp.int32) // TOP
-    outgoing = (
-        jnp.zeros((2 * EXPERTS * CAP, width), jnp.bfloat16)
-        .at[slot_index]
-        .set(moe_in[:, token_index].reshape(-1, width))
-    )
+    pairs = token_count * TOP
+    slots = EXPERTS * CAP
+    onehot = (flat_routes[..., None] == jnp.arange(EXPERTS, dtype=jnp.int32)).astype(jnp.bfloat16)
+    pair_ids = jnp.arange(pairs, dtype=jnp.int32)
+    lower = (pair_ids[None, :] <= pair_ids[:, None]).astype(jnp.bfloat16)
+    running = jnp.einsum("ij,mje->mie", lower, onehot, preferred_element_type=jnp.float32)
+    rank_slot = jnp.sum((running - 1.0) * onehot.astype(jnp.float32), axis=2).astype(jnp.int32)
+    local_slot = (flat_routes * CAP + rank_slot).reshape(2, token_count, TOP)
+    slot_ids = jnp.arange(slots, dtype=jnp.int32)
+    chooser = jnp.sum(
+        (local_slot[:, None, :, :] == slot_ids[None, :, None, None]).astype(jnp.bfloat16),
+        axis=3,
+        dtype=jnp.bfloat16,
+    )
+    outgoing = jnp.einsum(
+        "mst,mtd->msd", chooser, moe_in, preferred_element_type=jnp.float32
+    ).astype(jnp.bfloat16)
     arrived = lax.all_to_all(
         outgoing.reshape(2, groups, local_count * CAP, width),
         "exp",
@@ -171,11 +177,10 @@
         split_axis=1,
         concat_axis=1,
         tiled=True,
-    )
-    picked = returned.reshape(2 * EXPERTS * CAP, width)[slot_index].reshape(
-        2, token_count, TOP, width
-    )
-    mixture = jnp.sum(gate_probs[..., None] * picked.astype(jnp.float32), axis=2)
+    ).reshape(2, slots, width)
+    picker = (local_slot[..., None] == slot_ids[None, None, None, :]).astype(jnp.bfloat16)
+    picked = jnp.einsum("mtks,msd->mtkd", picker, returned, preferred_element_type=jnp.float32)
+    mixture = jnp.sum(gate_probs[..., None] * picked, axis=2)
     final = root_norm(
         residual.astype(jnp.float32) + RESIDUAL_SCALE * mixture, norm_gains[:, 2][:, None, :]
     ).astype(jnp.bfloat16)
@@ -183,35 +188,43 @@
     vocab_rows = vocab_head.shape[1]
     lowest = shard * vocab_rows
     vocab_ids = jnp.arange(vocab_rows, dtype=jnp.int32)
-    shard_piece = lax.all_gather(final, "exp", axis=1, tiled=True)
-    piece_rows = shard_piece.shape[1]
+    groups_exp = lax.axis_size("exp")
+    halves = 2
+    half_rows = token_count // halves
+    wanted_all = (targets - lowest).reshape(groups_exp, halves, half_rows)
     block_rows = 512
-    block_count = piece_rows // block_rows
-    wanted_all = targets - lowest
-
-    def one_block(block_number):
-        row_block = lax.dynamic_slice_in_dim(shard_piece, block_number * block_rows, block_rows, 1)
-        wanted = lax.dynamic_slice_in_dim(wanted_all, block_number * block_rows, block_rows, 0)
-        logits = (
-            jnp.einsum("mtd,mvd->mtv", row_block, vocab_head, preferred_element_type=jnp.float32)
-            / LOGIT_DIVISOR
-        )
-        highest = jnp.max(logits, axis=2)
-        masses = jnp.sum(jnp.exp(logits - highest[..., None]), axis=2)
-        chosen = jnp.sum(
-            jnp.where(wanted[None, :, None] == vocab_ids[None, None, :], logits, 0.0), axis=2
-        )
-        return (highest, masses, chosen)
-
-    block_max, block_mass, block_hit = lax.map(one_block, jnp.arange(block_count, dtype=jnp.int32))
-
-    def place(fresh):
-        ordered = jnp.transpose(fresh, (1, 0, 2)).reshape(2, piece_rows)
-        return ordered
-
-    groups_exp = lax.axis_size("exp")
-    stacked = jnp.stack([place(block_max), place(block_mass), place(block_hit)])
-    stacked = jnp.transpose(stacked.reshape(3, 2, groups_exp, token_count), (2, 0, 1, 3))
+    pieces = []
+    for which in range(2):
+        for half in range(halves):
+            chunk = lax.all_gather(
+                final[which, half * half_rows : (half + 1) * half_rows], "exp", axis=0, tiled=True
+            )
+            chunk_rows = chunk.shape[0]
+            block_count = chunk_rows // block_rows
+            wanted_chunk = wanted_all[:, half].reshape(chunk_rows)
+            head = vocab_head[which]
+
+            def one_block(block_number, chunk=chunk, wanted_chunk=wanted_chunk, head=head):
+                row_block = lax.dynamic_slice_in_dim(chunk, block_number * block_rows, block_rows, 0)
+                wanted = lax.dynamic_slice_in_dim(wanted_chunk, block_number * block_rows, block_rows, 0)
+                logits = (
+                    jnp.einsum("td,vd->tv", row_block, head, preferred_element_type=jnp.float32)
+                    / LOGIT_DIVISOR
+                )
+                highest = jnp.max(logits, axis=1)
+                masses = jnp.sum(jnp.exp(logits - highest[:, None]), axis=1)
+                chosen = jnp.sum(
+                    jnp.where(wanted[:, None] == vocab_ids[None, :], logits, 0.0), axis=1
+                )
+                return jnp.stack([highest, masses, chosen])
+
+            stats = lax.map(one_block, jnp.arange(block_count, dtype=jnp.int32))
+            stats = jnp.transpose(stats, (1, 0, 2)).reshape(3, groups_exp, half_rows)
+            pieces.append(stats)
+    stacked = jnp.stack(
+        [jnp.concatenate([pieces[which * halves + half] for half in range(halves)], axis=2) for which in range(2)]
+    )
+    stacked = jnp.transpose(stacked, (2, 1, 0, 3))
     gathered = lax.all_to_all(stacked, "exp", 0, 0, tiled=True)
     all_max = gathered[:, 0]
     all_mass = gathered[:, 1]

time: 474 us -> 463 us (0.977)
  blocking collectives: 99.2 us -> 165 us
  local copies, waits for them, and re-layouts: 77.7 us -> 28 us
  waiting for transfers between devices: 135 us -> 112 us
  other arithmetic: 47.1 us -> 27.3 us
  matrix products: 88 us -> 105 us
  loops' own time: 5.49 us -> 10.6 us
  starting transfers between devices: 5.02 us -> 0.16 us
    all_to_all x0 -> x1, blocking collectives: none -> 65.8 us  [per_device(): lax.all_to_all(produced.reshape(2, groups, local_count * CAP, width), 'ex...]
    all_to_all x1 -> x0, waiting for transfers between devices: 61.7 us -> none  [per_device(): lax.all_to_all(produced.reshape(2, groups, local_count * CAP, width), 'ex...]
    all_gather x1 -> x4, waiting for transfers between devices: 73.6 us -> 111 us  [per_device(): lax.all_gather(final[which, half * half_rows:(half + 1) * half_rows], 'ex...]
    gather x3 -> x0, local copies, waits for them, and re-layouts: 35.7 us -> none  [the longest x2 21.3 us: per_device(): moe_in[:, token_index].reshape(-1, width)]
    dot_general x8 -> x19, matrix products: 47.9 us -> 67.6 us  [the longest x16 59.4 us: one_block(): jnp.einsum('td,vd->tv', row_block, head, preferred_element_type=jnp.float32)]
    another operation x6 -> x3, other arithmetic: 18.2 us -> 0.34 us
    scatter x1 -> x0, local copies, waits for them, and re-layouts: 13.6 us -> none  [per_device(): outgoing = jnp.zeros((2 * EXPERTS * CAP, width), jnp.bfloat16).at[slot_in...]
    dynamic_slice x16 -> x32, local copies, waits for them, and re-layouts: 5.32 us -> 11.1 us  [the longest x16 9.91 us: per_device(): stats = lax.map(one_block, jnp.arange(block_count, dtype=jnp.int32))]
  transfers between devices with their start and end apart: 2 -> 4, of which waited for: 2 -> 4; matrix products, arithmetic and copies ran while one was open for 0% -> 15% of each run, Pallas kernels for 0% -> 0%
where the time goes in v2:
time: 463 us; the launch traced here: 462 us
  blocking collectives  165 us (36%)
  waiting for transfers between devices  112 us (24%)
  matrix products  105 us (23%)
  local copies, waits for them, and re-layouts  28 us (6%)
  other arithmetic  27.3 us (6%)
  between operations  14.3 us (3%)
  loops' own time  10.6 us (2%)
    all_gather x4, waiting for transfers between devices, per_device(): lax.all_gather(final[which, half * half_rows:(half + 1) * half_rows], 'ex...  111 us
    all_to_all x1, blocking collectives, per_device(): lax.all_to_all(outgoing.reshape(2, groups, local_count * CAP, width), 'ex...  71.5 us
    all_to_all x1, blocking collectives, per_device(): lax.all_to_all(produced.reshape(2, groups, local_count * CAP, width), 'ex...  65.8 us
    dot_general x16, matrix products, one_block(): jnp.einsum('td,vd->tv', row_block, head, preferred_element_type=jnp.float32)  59.4 us
    all_to_all x1, blocking collectives, per_device(): lax.all_to_all(dense_totals.reshape(devices, per_device_seqs), ('req', 'e...  15 us
    all_to_all x1, blocking collectives, per_device(): gathered = lax.all_to_all(stacked, 'exp', 0, 0, tiled=True)  12.6 us
    reduce_sum x16, other arithmetic, one_block(): masses = jnp.sum(jnp.exp(logits - highest[:, None]), axis=1)  11.3 us
    another operation x4, loops' own time, per_device(): stats = lax.map(one_block, jnp.arange(block_count, dtype=jnp.int32))  10.6 us
  transfers between devices with their start and end apart: 4, of which 4 were waited for; matrix products, arithmetic and copies ran while one was open for 15% of the time, Pallas kernels for 0%

profile of v2, /device:TPU:1, one launch (start us, length us, event | category | flops | bytes accessed | tf_op | source)
XLA Modules:
  0.0 461.9 jit_solution(9129609755430206089)
XLA Ops:
  41.3 10.3 %fusion.24 = bf16[2,1280,128]{2,1,0:T(8,128)(2,1)S(1)} fusion(s32[2,128,8]{1,2,0:T(8,128)S(1)} %multiply_add_fusion), kind=kLoop, calls=%fused_computation.44 | loop fusion | flops 7536640 | bytes 663552 | tf_op jit(solution)/shard_map/reduce_sum | solution.py:153
  54.0 71.5 %all_to_all.24 = bf16[2,32,40,1024]{3,2,0,1:T(8,128)(2,1)S(1)} all-to-all(bf16[2,32,40,1024]{3,2,0,1:T(8,128)(2,1)S(1)} %copy.139), channel_id=1, replica_groups=mesh['req'=4,'exp'=32] {'exp'}, dimensions={1} | all-to-all | bytes 10485760 | tf_op jit(solution)/shard_map/all_to_all | solution.py:161
  125.5 8.2 %fusion.39 = f32[2,32,1,40,1024]{4,3,1,0,2:T(8,128)} fusion(bf16[2,1,1024,1024]{3,2,1,0:T(8,128)(2,1)S(1)} %copy-done.10, bf16[2,32,40,1024]{3,2,0,1:T(8,128)(2,1)S(1)} %all_to_all.24), kind=kOutput, calls=%fused_computation.60 | convolution fusion | flops 5368709120 | bytes 19922944 | tf_op jit(solution)/shard_map/mslcd,mldf->mslcf/dot_general | solution.py:169
  133.7 7.2 %convolution_convert_fusion.1 = bf16[2,32,40,1024]{3,2,1,0:T(8,128)(2,1)S(1)} fusion(f32[2,32,1,40,1024]{4,3,1,0,2:T(8,128)} %fusion.39, bf16[2,1,512,1024]{3,2,1,0:T(8,128)(2,1)S(1)} %copy-done), kind=kOutput, calls=%fused_computation.61 | convolution fusion | flops 2694840320 | bytes 17825792 | tf_op jit(solution)/shard_map/mslcf,mlfd->mslcd/dot_general | solution.py:171
  141.7 65.8 %all_to_all.25 = bf16[2,32,40,1024]{3,2,0,1:T(8,128)(2,1)S(1)} all-to-all(bf16[2,32,40,1024]{3,2,0,1:T(8,128)(2,1)S(1)} %copy.141), channel_id=1, replica_groups=mesh['req'=4,'exp'=32] {'exp'}, dimensions={1} | all-to-all | bytes 10485760 | tf_op jit(solution)/shard_map/all_to_all | solution.py:174
  208.2 6.0 %multiply_reduce_fusion = f32[2,128,1024]{2,1,0:T(8,128)S(1)} fusion(f32[2,128,8]{1,2,0:T(8,128)S(1)} %copy-done.11, bf16[2,1280,1024,1]{2,1,3,0:T(8,128)(2,1)S(1)} %bitcast.303, s32[2,128,8]{1,2,0:T(8,128)S(1)} %multiply_add_fusion), kind=kOutput, calls=%fused_computation.42 | convolution fusion | flops 5375262720 | bytes 6307840 | tf_op jit(solution)/shard_map/mtks,msd->mtkd/dot_general | solution.py:182
  217.5 5.0 %slice_bitcast_fusion.1 = (bf16[1152,1024]{1,0:T(8,128)(2,1)}, bf16[1152,1024]{1,0:T(8,128)(2,1)}) fusion(bf16[2,1152,1024]{2,1,0:T(8,128)(2,1)} %param.31), kind=kLoop, calls=%fused_computation.64 | loop fusion | bytes 9437184 | tf_op jit(solution)/shard_map/squeeze | solution.py:205
  222.5 37.4 %all-gather.9.cloned.1.call-done = bf16[1,2048,1024]{2,1,0:T(8,128)(2,1)} async-done(((bf16[1,64,1024]{2,1,0:T(8,128)(2,1)}), bf16[1,2048,1024]{2,1,0:T(8,128)(2,1)}) %all-gather.9.cloned.1.call-update) | async-done | bytes 4194320 | tf_op jit(solution)/shard_map/all_gather | solution.py:199
  259.9 23.3 %while.44 = (s32[]{:T(128)}, f32[4,3,512]{2,1,0:T(4,128)S(1)}, s32[4]{0:T(128)S(1)}, bf16[2048,1024]{1,0:T(8,128)(2,1)}, bf16[1152,1024]{1,0:T(8,128)(2,1)}, /*i...) while((s32[]{:T(128)}, f32[4,3,512]{2,1,0:T(4,128)S(1)}, ...), condition=%wide.region_18.19_spmd.clone, body=%wide.region_14.18_spmd.clone.sunk | while | flops 1212089856 | bytes 8155307 | solution.py:221
  261.2 3.7 fusion.214
  267.1 3.7 fusion.214
  278.7 3.7 fusion.214
  283.4 24.3 %all-gather.11.cloned.1.call-done = bf16[1,2048,1024]{2,1,0:T(8,128)(2,1)} async-done(((bf16[1,64,1024]{2,1,0:T(8,128)(2,1)}), bf16[1,2048,1024]{2,1,0:T(8,128)(2,1)}) %all-gather.11.cloned.1.call-update) | async-done | bytes 4194320 | tf_op jit(solution)/shard_map/all_gather | solution.py:199
  307.7 23.2 %while.45 = (s32[]{:T(128)}, f32[4,3,512]{2,1,0:T(4,128)S(1)}, s32[4]{0:T(128)S(1)}, bf16[2048,1024]{1,0:T(8,128)(2,1)}, bf16[1152,1024]{1,0:T(8,128)(2,1)}, /*i...) while((s32[]{:T(128)}, f32[4,3,512]{2,1,0:T(4,128)S(1)}, ...), condition=%wide.region_23.24_spmd.clone, body=%wide.region_19.23_spmd.clone.sunk | while | flops 1212089856 | bytes 8155307 | solution.py:221
  308.9 3.7 fusion.217
  314.8 3.7 fusion.217
  320.6 3.7 fusion.217
  326.4 3.7 fusion.217
  331.0 24.4 %all-gather.13.cloned.1.call-done = bf16[1,2048,1024]{2,1,0:T(8,128)(2,1)} async-done(((bf16[1,64,1024]{2,1,0:T(8,128)(2,1)}), bf16[1,2048,1024]{2,1,0:T(8,128)(2,1)}) %all-gather.13.cloned.1.call-update) | async-done | bytes 4194320 | tf_op jit(solution)/shard_map/all_gather | solution.py:199
  355.4 23.1 %while.46 = (s32[]{:T(128)}, f32[4,3,512]{2,1,0:T(4,128)S(1)}, s32[4]{0:T(128)S(1)}, bf16[2048,1024]{1,0:T(8,128)(2,1)}, bf16[1152,1024]{1,0:T(8,128)(2,1)}, /*i...) while((s32[]{:T(128)}, f32[4,3,512]{2,1,0:T(4,128)S(1)}, ...), condition=%wide.region_28.29_spmd.clone, body=%wide.region_24.28_spmd.clone.sunk | while | flops 1212089856 | bytes 8155307 | solution.py:221
  356.7 3.7 fusion.220
  362.4 3.7 fusion.220
  368.2 3.7 fusion.220
  374.0 3.7 fusion.220
  378.7 24.4 %all-gather.15.cloned.1.call-done = bf16[1,2048,1024]{2,1,0:T(8,128)(2,1)} async-done(((bf16[1,64,1024]{2,1,0:T(8,128)(2,1)}), bf16[1,2048,1024]{2,1,0:T(8,128)(2,1)}) %all-gather.15.cloned.1.call-update) | async-done | bytes 4194320 | tf_op jit(solution)/shard_map/all_gather | solution.py:199
  403.1 23.1 %while.47 = (s32[]{:T(128)}, f32[4,3,512]{2,1,0:T(4,128)S(1)}, s32[4]{0:T(128)S(1)}, bf16[2048,1024]{1,0:T(8,128)(2,1)}, bf16[1152,1024]{1,0:T(8,128)(2,1)}, /*i...) while((s32[]{:T(128)}, f32[4,3,512]{2,1,0:T(4,128)S(1)}, ...), condition=%wide.region_33.34_spmd.clone, body=%wide.region_29.33_spmd.clone.sunk | while | flops 1212089856 | bytes 8155307 | solution.py:221
  404.4 3.7 fusion.223
  410.1 3.7 fusion.223
  415.9 3.7 fusion.223
  421.7 3.7 fusion.223
  426.6 12.6 %all_to_all.26 = f32[32,3,2,128]{3,2,1,0:T(2,128)S(1)} all-to-all(f32[32,3,2,128]{3,2,1,0:T(2,128)S(1)} %copy.147), channel_id=1, replica_groups=mesh['req'=4,'exp'=32] {'exp'}, dimensions={0} | all-to-all | bytes 196608 | tf_op jit(solution)/shard_map/all_to_all | solution.py:228
  439.7 15.0 %all_to_all.27 = f32[128,1,4]{2,1,0:T(1,128)S(1)} all-to-all(f32[128,1,4]{2,1,0:T(1,128)S(1)} %bitcast.324), channel_id=1, replica_groups=mesh['req'=4,'exp'=32] {'req','exp'}, dimensions={0} | all-to-all | bytes 4096 | tf_op jit(solution)/shard_map/all_to_all | solution.py:246
  (189 shorter events, 69.3 us)
Async XLA Ops:
  7.2 126.6 %copy-start = (bf16[2,1,512,1024]{3,2,1,0:T(8,128)(2,1)S(1)}, bf16[2,1,512,1024]{3,2,1,0:T(8,128)(2,1)}, u32[]{:S(2)}) copy-start(bf16[2,1,512,1024]{3,2,1,0:T(8,128)(2,1)} %param.30) | copy-start | bytes 6291460
  7.2 252.7 %all-gather.9.cloned.1.call-start = ((), (), s32[]{:S(2)}) async-start(), calls=%async_computation.4 | async-start | bytes 4325376 | tf_op jit(solution)/shard_map/all_gather | solution.py:199
  12.4 1.0 copy-start.2
  12.5 2.1 copy-start.12
  23.7 1.0 copy-start.3
  25.9 4.9 %copy-start.6 = (f32[2,3,1024]{2,0,1:T(2,128)S(1)}, f32[2,3,1024]{2,0,1:T(2,128)}, u32[]{:S(2)}) copy-start(f32[2,3,1024]{2,0,1:T(2,128)} %param.26) | copy-start | bytes 73732
  29.7 4.2 copy-start.4
  37.9 2.3 copy-start.5
  54.0 71.5 %copy-start.10 = (bf16[2,1,1024,1024]{3,2,1,0:T(8,128)(2,1)S(1)}, bf16[2,1,1024,1024]{3,2,1,0:T(8,128)(2,1)}, u32[]{:S(2)}) copy-start(bf16[2,1,1024,1024]{3,2,1,0:T(8,128)(2,1)} %param.29) | copy-start | bytes 12582916
  207.5 0.7 copy-start.11
  214.2 2.9 copy-start.7
  215.6 92.1 %all-gather.11.cloned.1.call-start = ((), (), s32[]{:S(2)}) async-start(), calls=%async_computation.5 | async-start | bytes 4325376 | tf_op jit(solution)/shard_map/all_gather | solution.py:199
  216.3 139.1 %all-gather.13.cloned.1.call-start = ((), (), s32[]{:S(2)}) async-start(), calls=%async_computation.6 | async-start | bytes 4325376 | tf_op jit(solution)/shard_map/all_gather | solution.py:199
  217.1 186.0 %all-gather.15.cloned.1.call-start = ((), (), s32[]{:S(2)}) async-start(), calls=%async_computation.7 | async-start | bytes 4325376 | tf_op jit(solution)/shard_map/all_gather | solution.py:199
  403.1 36.4 %copy-start.9 = (s32[4]{0:T(128)S(1)}, s32[4]{0:T(128)}, u32[]{:S(2)}) copy-start(s32[4]{0:T(128)} %param.25) | copy-start | bytes 52
  426.2 29.2 %copy-start.1 = (bf16[2,1,512,1024]{3,2,1,0:T(8,128)(2,1)S(1)}, bf16[2,1,512,1024]{3,2,1,0:T(8,128)(2,1)}, u32[]{:S(2)}) copy-start(bf16[2,1,512,1024]{3,2,1,0:T(8,128)(2,1)} %param.30) | copy-start | bytes 6291460
  439.4 16.0 %copy-start.8 = (f32[2,128]{1,0:T(2,128)}, f32[2,128]{1,0:T(2,128)S(1)}, u32[]{:S(2)}) copy-start(f32[2,128]{1,0:T(2,128)S(1)} %add_subtract_fusion) | copy-start | bytes 3076
Sparse Core Ops, SparseCore 0:
  215.7 44.1 all-gather.8
  262.2 45.4 all-gather.10
  309.9 45.4 all-gather.12
  357.6 45.4 all-gather.14

commit v3 on v1

--- a/solution.py
+++ b/solution.py
@@ -124,94 +124,104 @@
     token_count = states.shape[1]
     width = states.shape[2]
     segment, member, position = segment_table(lengths[0], token_count)
-    residual = jnp.stack(
-        [
-            attend(
-                states[which],
-                segment,
-                position,
-                norm_gains[which, 0],
-                qkv_weight[which],
-                out_weight[which],
-            )
-            for which in range(2)
-        ]
-    )
-    moe_in = root_norm(residual, norm_gains[:, 1][:, None, :]).astype(jnp.bfloat16)
     groups = lax.axis_size("exp")
     local_count = expert_in.shape[1]
-    flat_routes = routes.reshape(2, token_count * TOP)
-    onehot = (flat_routes[..., None] == jnp.arange(EXPERTS, dtype=jnp.int32)).astype(jnp.int32)
-    rank_slot = jnp.sum((jnp.cumsum(onehot, axis=1) - 1) * onehot, axis=2)
-    slot_index = (
-        flat_routes * CAP + rank_slot + jnp.arange(2, dtype=jnp.int32)[:, None] * (EXPERTS * CAP)
-    ).reshape(-1)
-    token_index = jnp.arange(token_count * TOP, dtype=jnp.int32) // TOP
-    outgoing = (
-        jnp.zeros((2 * EXPERTS * CAP, width), jnp.bfloat16)
-        .at[slot_index]
-        .set(moe_in[:, token_index].reshape(-1, width))
-    )
-    arrived = lax.all_to_all(
-        outgoing.reshape(2, groups, local_count * CAP, width),
-        "exp",
-        split_axis=1,
-        concat_axis=1,
-        tiled=True,
-    )
-    inputs = arrived.reshape(2, groups, local_count, CAP, width)
-    gate_up = jnp.einsum("mslcd,mldf->mslcf", inputs, expert_in, preferred_element_type=jnp.float32)
-    hidden = (jax.nn.silu(gate_up[..., :EXPERT_FF]) * gate_up[..., EXPERT_FF:]).astype(jnp.bfloat16)
-    produced = jnp.einsum(
-        "mslcf,mlfd->mslcd", hidden, expert_down, preferred_element_type=jnp.float32
-    ).astype(jnp.bfloat16)
-    returned = lax.all_to_all(
-        produced.reshape(2, groups, local_count * CAP, width),
-        "exp",
-        split_axis=1,
-        concat_axis=1,
-        tiled=True,
-    )
-    picked = returned.reshape(2 * EXPERTS * CAP, width)[slot_index].reshape(
-        2, token_count, TOP, width
-    )
-    mixture = jnp.sum(gate_probs[..., None] * picked.astype(jnp.float32), axis=2)
-    final = root_norm(
-        residual.astype(jnp.float32) + RESIDUAL_SCALE * mixture, norm_gains[:, 2][:, None, :]
-    ).astype(jnp.bfloat16)
+    pairs = token_count * TOP
+    slots = EXPERTS * CAP
+    pair_ids = jnp.arange(pairs, dtype=jnp.int32)
+    lower = (pair_ids[None, :] <= pair_ids[:, None]).astype(jnp.bfloat16)
+    slot_ids = jnp.arange(slots, dtype=jnp.int32)
     shard = lax.axis_index("exp")
     vocab_rows = vocab_head.shape[1]
     lowest = shard * vocab_rows
     vocab_ids = jnp.arange(vocab_rows, dtype=jnp.int32)
-    shard_piece = lax.all_gather(final, "exp", axis=1, tiled=True)
-    piece_rows = shard_piece.shape[1]
+    wanted_all = targets - lowest
     block_rows = 512
-    block_count = piece_rows // block_rows
-    wanted_all = targets - lowest
-
-    def one_block(block_number):
-        row_block = lax.dynamic_slice_in_dim(shard_piece, block_number * block_rows, block_rows, 1)
-        wanted = lax.dynamic_slice_in_dim(wanted_all, block_number * block_rows, block_rows, 0)
-        logits = (
-            jnp.einsum("mtd,mvd->mtv", row_block, vocab_head, preferred_element_type=jnp.float32)
-            / LOGIT_DIVISOR
-        )
-        highest = jnp.max(logits, axis=2)
-        masses = jnp.sum(jnp.exp(logits - highest[..., None]), axis=2)
-        chosen = jnp.sum(
-            jnp.where(wanted[None, :, None] == vocab_ids[None, None, :], logits, 0.0), axis=2
-        )
-        return (highest, masses, chosen)
-
-    block_max, block_mass, block_hit = lax.map(one_block, jnp.arange(block_count, dtype=jnp.int32))
-
-    def place(fresh):
-        ordered = jnp.transpose(fresh, (1, 0, 2)).reshape(2, piece_rows)
-        return ordered
-
-    groups_exp = lax.axis_size("exp")
-    stacked = jnp.stack([place(block_max), place(block_mass), place(block_hit)])
-    stacked = jnp.transpose(stacked.reshape(3, 2, groups_exp, token_count), (2, 0, 1, 3))
+
+    def model_final(which):
+        residual = attend(
+            states[which],
+            segment,
+            position,
+            norm_gains[which, 0],
+            qkv_weight[which],
+            out_weight[which],
+        )
+        moe_in = root_norm(residual, norm_gains[which, 1]).astype(jnp.bfloat16)
+        flat_routes = routes[which].reshape(pairs)
+        onehot = (flat_routes[:, None] == jnp.arange(EXPERTS, dtype=jnp.int32)).astype(
+            jnp.bfloat16
+        )
+        running = jnp.dot(lower, onehot, preferred_element_type=jnp.float32)
+        rank_slot = jnp.sum((running - 1.0) * onehot.astype(jnp.float32), axis=1).astype(jnp.int32)
+        local_slot = (flat_routes * CAP + rank_slot).reshape(token_count, TOP)
+        chooser = jnp.sum(
+            (local_slot[None, :, :] == slot_ids[:, None, None]).astype(jnp.bfloat16),
+            axis=2,
+            dtype=jnp.bfloat16,
+        )
+        outgoing = jnp.dot(chooser, moe_in, preferred_element_type=jnp.float32).astype(
+            jnp.bfloat16
+        )
+        arrived = lax.all_to_all(
+            outgoing.reshape(groups, local_count * CAP, width),
+            "exp",
+            split_axis=0,
+            concat_axis=0,
+            tiled=True,
+        )
+        inputs = arrived.reshape(groups, local_count, CAP, width)
+        gate_up = jnp.einsum(
+            "slcd,ldf->slcf", inputs, expert_in[which], preferred_element_type=jnp.float32
+        )
+        hidden = (jax.nn.silu(gate_up[..., :EXPERT_FF]) * gate_up[..., EXPERT_FF:]).astype(
+            jnp.bfloat16
+        )
+        produced = jnp.einsum(
+            "slcf,lfd->slcd", hidden, expert_down[which], preferred_element_type=jnp.float32
+        ).astype(jnp.bfloat16)
+        returned = lax.all_to_all(
+            produced.reshape(groups, local_count * CAP, width),
+            "exp",
+            split_axis=0,
+            concat_axis=0,
+            tiled=True,
+        ).reshape(slots, width)
+        picker = (local_slot[..., None] == slot_ids[None, None, :]).astype(jnp.bfloat16)
+        picked = jnp.einsum("tks,sd->tkd", picker, returned, preferred_element_type=jnp.float32)
+        mixture = jnp.sum(gate_probs[which][..., None] * picked, axis=1)
+        final = root_norm(
+            residual.astype(jnp.float32) + RESIDUAL_SCALE * mixture, norm_gains[which, 2]
+        ).astype(jnp.bfloat16)
+        return final
+
+    def model_stats(which, chunk):
+        chunk_rows = chunk.shape[0]
+        block_count = chunk_rows // block_rows
+        head = vocab_head[which]
+
+        def one_block(block_number):
+            row_block = lax.dynamic_slice_in_dim(chunk, block_number * block_rows, block_rows, 0)
+            wanted = lax.dynamic_slice_in_dim(wanted_all, block_number * block_rows, block_rows, 0)
+            logits = (
+                jnp.einsum("td,vd->tv", row_block, head, preferred_element_type=jnp.float32)
+                / LOGIT_DIVISOR
+            )
+            highest = jnp.max(logits, axis=1)
+            masses = jnp.sum(jnp.exp(logits - highest[:, None]), axis=1)
+            chosen = jnp.sum(jnp.where(wanted[:, None] == vocab_ids[None, :], logits, 0.0), axis=1)
+            return jnp.stack([highest, masses, chosen])
+
+        stats = lax.map(one_block, jnp.arange(block_count, dtype=jnp.int32))
+        return jnp.transpose(stats, (1, 0, 2)).reshape(3, groups, token_count)
+
+    final_first = model_final(0)
+    gathered_first = lax.all_gather(final_first, "exp", axis=0, tiled=True)
+    final_second = model_final(1)
+    gathered_second = lax.all_gather(final_second, "exp", axis=0, tiled=True)
+    stats_first = model_stats(0, gathered_first)
+    stats_second = model_stats(1, gathered_second)
+    stacked = jnp.transpose(jnp.stack([stats_first, stats_second]), (2, 1, 0, 3))
     gathered = lax.all_to_all(stacked, "exp", 0, 0, tiled=True)
     all_max = gathered[:, 0]
     all_mass = gathered[:, 1]

time: 474 us -> 370 us (0.78)
  waiting for transfers between devices: 135 us -> 67.7 us
  local copies, waits for them, and re-layouts: 77.7 us -> 21 us
  blocking collectives: 99.2 us -> 127 us
  other arithmetic: 47.1 us -> 30.2 us
  loops' own time: 5.49 us -> 10.8 us
    all_gather x1 -> x2, waiting for transfers between devices: 73.6 us -> 0.08 us  [the longest x1 0.08 us: per_device(): gathered_second = lax.all_gather(final_second, 'exp', axis=0, tiled=True)]
    gather x3 -> x0, local copies, waits for them, and re-layouts: 35.7 us -> none  [the longest x2 21.3 us: per_device(): moe_in[:, token_index].reshape(-1, width)]
    all_to_all x1 -> x2, blocking collectives: 71.5 us -> 99.7 us  [model_final(): lax.all_to_all(outgoing.reshape(groups, local_count * CAP, width), 'exp',...]
    another operation x6 -> x1, other arithmetic: 18.2 us -> 0.18 us
    scatter x1 -> x0, local copies, waits for them, and re-layouts: 13.6 us -> none  [per_device(): outgoing = jnp.zeros((2 * EXPERTS * CAP, width), jnp.bfloat16).at[slot_in...]
    dot_general x10 -> x26, matrix products: 63.3 us -> 76 us  [the longest x16 54.2 us: one_block(): jnp.einsum('td,vd->tv', row_block, head, preferred_element_type=jnp.float32)]
    reduce_sum x10 -> x18, other arithmetic: 17.8 us -> 24.8 us  [the longest x2 13.4 us: model_final(): jnp.sum((local_slot[None, :, :] == slot_ids[:, None, None]).astype(jnp.bf...]
    all_to_all x1 -> x2, waiting for transfers between devices: 61.7 us -> 67.6 us  [model_final(): lax.all_to_all(produced.reshape(groups, local_count * CAP, width), 'exp',...]
  transfers between devices with their start and end apart: 2 -> 4, of which waited for: 2 -> 3; matrix products, arithmetic and copies ran while one was open for 0% -> 20% of each run, Pallas kernels for 0% -> 0%
where the time goes in v3:
time: 370 us; the launch traced here: 369 us
  blocking collectives  127 us (34%)
  matrix products  89 us (24%)
  waiting for transfers between devices  67.7 us (18%)
  other arithmetic  30.2 us (8%)
  local copies, waits for them, and re-layouts  21 us (6%)
  between operations  14.7 us (4%)
  loops' own time  10.8 us (3%)
  starting transfers between devices  8.62 us (2%)
    all_to_all x2, blocking collectives, model_final(): lax.all_to_all(outgoing.reshape(groups, local_count * CAP, width), 'exp',...  99.7 us
    all_to_all x2, waiting for transfers between devices, model_final(): lax.all_to_all(produced.reshape(groups, local_count * CAP, width), 'exp',...  67.6 us
    dot_general x16, matrix products, one_block(): jnp.einsum('td,vd->tv', row_block, head, preferred_element_type=jnp.float32)  54.2 us
    all_to_all x1, blocking collectives, per_device(): lax.all_to_all(dense_totals.reshape(devices, per_device_seqs), ('req', 'e...  15 us
    reduce_sum x2, other arithmetic, model_final(): jnp.sum((local_slot[None, :, :] == slot_ids[:, None, None]).astype(jnp.bf...  13.4 us
    all_to_all x1, blocking collectives, per_device(): gathered = lax.all_to_all(stacked, 'exp', 0, 0, tiled=True)  12.6 us
    reduce_sum x16, other arithmetic, one_block(): masses = jnp.sum(jnp.exp(logits - highest[:, None]), axis=1)  11.3 us
    another operation x2, loops' own time, model_stats(): stats = lax.map(one_block, jnp.arange(block_count, dtype=jnp.int32))  10.8 us
  transfers between devices with their start and end apart: 4, of which 3 were waited for; matrix products, arithmetic and copies ran while one was open for 20% of the time, Pallas kernels for 0%

profile of v3, /device:TPU:1, one launch (start us, length us, event | category | flops | bytes accessed | tf_op | source)
XLA Modules:
  0.0 369.2 jit_solution(6983227868482238789)
XLA Ops:
  9.2 3.1 fusion.18
  19.9 6.7 %fusion.25 = bf16[1280,128]{1,0:T(8,128)(2,1)S(1)} fusion(s32[128,8]{0,1:T(8,128)S(1)} %copy.95), kind=kLoop, calls=%fused_computation.42 | loop fusion | flops 3768320 | bytes 331776 | tf_op jit(solution)/shard_map/reduce_sum | solution.py:158
  27.5 43.4 %all_to_all.34 = bf16[32,40,1024]{2,1,0:T(8,128)(2,1)S(1)} all-to-all(bf16[32,40,1024]{2,1,0:T(8,128)(2,1)S(1)} %bitcast.266), channel_id=1, replica_groups=mesh['req'=4,'exp'=32] {'exp'}, dimensions={0} | all-to-all | bytes 5242880 | tf_op jit(solution)/shard_map/all_to_all | solution.py:166
  70.9 2.9 convolution_bitcast_fusion.1
  73.9 3.3 convolution_convert_fusion.3
  77.1 4.4 %all-to-all-start.1 = ((bf16[32,40,1024]{2,1,0:T(8,128)(2,1)}), bf16[32,40,1024]{2,1,0:T(8,128)(2,1)S(1)}, u32[]{:S(2)}, u32[]{:S(2)}) async-start(bf16[32,40,1024]{2,1,0:T(8,128)(2,1)} %convolution_convert_fusion.3), calls=%async_computation.1 | async-start | bytes 5242880 | tf_op jit(solution)/shard_map/all_to_all | solution.py:183
  81.8 33.8 %all-to-all-done.1 = bf16[32,40,1024]{2,1,0:T(8,128)(2,1)S(1)} async-done(((bf16[32,40,1024]{2,1,0:T(8,128)(2,1)}), bf16[32,40,1024]{2,1,0:T(8,128)(2,1)S(1)}, u32[]{:S(2)}, u32[]{:S(2)}) %all-to-all-start.1) | async-done | bytes 2621472 | tf_op jit(solution)/shard_map/all_to_all | solution.py:183
  115.6 3.2 multiply_reduce_fusion.1
  119.9 3.0 fusion.16
  124.3 6.7 %fusion.24 = bf16[1280,128]{1,0:T(8,128)(2,1)S(1)} fusion(s32[128,8]{0,1:T(8,128)S(1)} %copy.104), kind=kLoop, calls=%fused_computation.41 | loop fusion | flops 3768320 | bytes 331776 | tf_op jit(solution)/shard_map/reduce_sum | solution.py:158
  136.2 56.3 %all_to_all.35 = bf16[32,40,1024]{2,1,0:T(8,128)(2,1)S(1)} all-to-all(bf16[32,40,1024]{2,1,0:T(8,128)(2,1)S(1)} %bitcast.267), channel_id=1, replica_groups=mesh['req'=4,'exp'=32] {'exp'}, dimensions={0} | all-to-all | bytes 5242880 | tf_op jit(solution)/shard_map/all_to_all | solution.py:166
  192.5 2.9 convolution_bitcast_fusion
  195.4 3.3 convolution_convert_fusion.2
  198.8 4.1 %all-to-all-start.3 = ((bf16[32,40,1024]{2,1,0:T(8,128)(2,1)}), bf16[32,40,1024]{2,1,0:T(8,128)(2,1)S(1)}, u32[]{:S(2)}, u32[]{:S(2)}) async-start(bf16[32,40,1024]{2,1,0:T(8,128)(2,1)} %convolution_convert_fusion.2), calls=%async_computation.3 | async-start | bytes 5242880 | tf_op jit(solution)/shard_map/all_to_all | solution.py:183
  203.1 33.8 %all-to-all-done.3 = bf16[32,40,1024]{2,1,0:T(8,128)(2,1)S(1)} async-done(((bf16[32,40,1024]{2,1,0:T(8,128)(2,1)}), bf16[32,40,1024]{2,1,0:T(8,128)(2,1)S(1)}, u32[]{:S(2)}, u32[]{:S(2)}) %all-to-all-start.3) | async-done | bytes 2621472 | tf_op jit(solution)/shard_map/all_to_all | solution.py:183
  236.9 3.2 multiply_reduce_fusion
  241.2 4.3 %slice_bitcast_fusion.1 = (bf16[1152,1024]{1,0:T(8,128)(2,1)}, bf16[1152,1024]{1,0:T(8,128)(2,1)S(1)}) fusion(bf16[2,1152,1024]{2,1,0:T(8,128)(2,1)} %param.27), kind=kLoop, calls=%fused_computation.52 | loop fusion | bytes 9437184 | tf_op jit(solution)/shard_map/squeeze | solution.py:201
  245.5 47.7 %while.22 = (s32[]{:T(128)}, f32[8,3,512]{2,1,0:T(4,128)S(1)}, s32[8]{0:T(128)S(1)}, bf16[4096,1024]{1,0:T(8,128)(2,1)}, bf16[1152,1024]{1,0:T(8,128)(2,1)}, /*i...) while((s32[]{:T(128)}, f32[8,3,512]{2,1,0:T(4,128)S(1)}, ...), condition=%wide.region_15.16_spmd.clone, body=%wide.region_11.15_spmd.clone.sunk | while | flops 1212089856 | bytes 8155307 | solution.py:215
  246.8 3.7 %fusion.198 = (f32[512]{0:T(512)S(1)}, f32[512,1152]{1,0:T(8,128)S(1)}) fusion(bf16[1152,1024]{1,0:T(8,128)(2,1)} %get-tuple-element.312, bf16[4096,1024]{1,0:T(8,128)(2,1)} %get-tuple-element.311, s32[]{:T(128)S(6)} %select_n.42), kind=kOutput, calls=%fused_computation.219.clone.1 | convolution fusion | flops 1209138688 | bytes 5769220 | tf_op jit(solution)/shard_map/while/body/eval_jaxpr/td,vd->tv/dot_general | solution.py:207
  252.7 3.7 %fusion.198 = (f32[512]{0:T(512)S(1)}, f32[512,1152]{1,0:T(8,128)S(1)}) fusion(bf16[1152,1024]{1,0:T(8,128)(2,1)} %get-tuple-element.312, bf16[4096,1024]{1,0:T(8,128)(2,1)} %get-tuple-element.311, s32[]{:T(128)S(6)} %select_n.42), kind=kOutput, calls=%fused_computation.219.clone.1 | convolution fusion | flops 1209138688 | bytes 5769220 | tf_op jit(solution)/shard_map/while/body/eval_jaxpr/td,vd->tv/dot_general | solution.py:207
  258.5 3.8 %fusion.198 = (f32[512]{0:T(512)S(1)}, f32[512,1152]{1,0:T(8,128)S(1)}) fusion(bf16[1152,1024]{1,0:T(8,128)(2,1)} %get-tuple-element.312, bf16[4096,1024]{1,0:T(8,128)(2,1)} %get-tuple-element.311, s32[]{:T(128)S(6)} %select_n.42), kind=kOutput, calls=%fused_computation.219.clone.1 | convolution fusion | flops 1209138688 | bytes 5769220 | tf_op jit(solution)/shard_map/while/body/eval_jaxpr/td,vd->tv/dot_general | solution.py:207
  264.4 3.7 %fusion.198 = (f32[512]{0:T(512)S(1)}, f32[512,1152]{1,0:T(8,128)S(1)}) fusion(bf16[1152,1024]{1,0:T(8,128)(2,1)} %get-tuple-element.312, bf16[4096,1024]{1,0:T(8,128)(2,1)} %get-tuple-element.311, s32[]{:T(128)S(6)} %select_n.42), kind=kOutput, calls=%fused_computation.219.clone.1 | convolution fusion | flops 1209138688 | bytes 5769220 | tf_op jit(solution)/shard_map/while/body/eval_jaxpr/td,vd->tv/dot_general | solution.py:207
  270.2 4.4 %fusion.198 = (f32[512]{0:T(512)S(1)}, f32[512,1152]{1,0:T(8,128)S(1)}) fusion(bf16[1152,1024]{1,0:T(8,128)(2,1)} %get-tuple-element.312, bf16[4096,1024]{1,0:T(8,128)(2,1)} %get-tuple-element.311, s32[]{:T(128)S(6)} %select_n.42), kind=kOutput, calls=%fused_computation.219.clone.1 | convolution fusion | flops 1209138688 | bytes 5769220 | tf_op jit(solution)/shard_map/while/body/eval_jaxpr/td,vd->tv/dot_general | solution.py:207
  276.7 3.9 %fusion.198 = (f32[512]{0:T(512)S(1)}, f32[512,1152]{1,0:T(8,128)S(1)}) fusion(bf16[1152,1024]{1,0:T(8,128)(2,1)} %get-tuple-element.312, bf16[4096,1024]{1,0:T(8,128)(2,1)} %get-tuple-element.311, s32[]{:T(128)S(6)} %select_n.42), kind=kOutput, calls=%fused_computation.219.clone.1 | convolution fusion | flops 1209138688 | bytes 5769220 | tf_op jit(solution)/shard_map/while/body/eval_jaxpr/td,vd->tv/dot_general | solution.py:207
  282.7 3.9 %fusion.198 = (f32[512]{0:T(512)S(1)}, f32[512,1152]{1,0:T(8,128)S(1)}) fusion(bf16[1152,1024]{1,0:T(8,128)(2,1)} %get-tuple-element.312, bf16[4096,1024]{1,0:T(8,128)(2,1)} %get-tuple-element.311, s32[]{:T(128)S(6)} %select_n.42), kind=kOutput, calls=%fused_computation.219.clone.1 | convolution fusion | flops 1209138688 | bytes 5769220 | tf_op jit(solution)/shard_map/while/body/eval_jaxpr/td,vd->tv/dot_general | solution.py:207
  288.7 3.7 %fusion.198 = (f32[512]{0:T(512)S(1)}, f32[512,1152]{1,0:T(8,128)S(1)}) fusion(bf16[1152,1024]{1,0:T(8,128)(2,1)} %get-tuple-element.312, bf16[4096,1024]{1,0:T(8,128)(2,1)} %get-tuple-element.311, s32[]{:T(128)S(6)} %select_n.42), kind=kOutput, calls=%fused_computation.219.clone.1 | convolution fusion | flops 1209138688 | bytes 5769220 | tf_op jit(solution)/shard_map/while/body/eval_jaxpr/td,vd->tv/dot_general | solution.py:207
  293.4 40.0 %while.23 = (s32[]{:T(128)}, f32[8,3,512]{2,1,0:T(4,128)S(1)}, s32[8]{0:T(128)S(1)}, bf16[4096,1024]{1,0:T(8,128)(2,1)}, bf16[1152,1024]{1,0:T(8,128)(2,1)S(1)},...) while((s32[]{:T(128)}, f32[8,3,512]{2,1,0:T(4,128)S(1)}, ...), condition=%wide.region_28.29_spmd.clone, body=%wide.region_24.28_spmd.clone.sunk | while | flops 1212089856 | bytes 8155307 | solution.py:215
  304.7 2.9 fusion.201
  309.7 2.9 fusion.201
  319.7 2.9 fusion.201
  333.6 12.6 %all_to_all.36 = f32[32,3,2,128]{3,2,1,0:T(2,128)S(1)} all-to-all(f32[32,3,2,128]{3,2,1,0:T(2,128)S(1)} %copy.106), channel_id=1, replica_groups=mesh['req'=4,'exp'=32] {'exp'}, dimensions={0} | all-to-all | bytes 196608 | tf_op jit(solution)/shard_map/all_to_all | solution.py:225
  346.7 15.0 %all_to_all.37 = f32[128,1,4]{2,1,0:T(1,128)S(1)} all-to-all(f32[128,1,4]{2,1,0:T(1,128)S(1)} %bitcast.292), channel_id=1, replica_groups=mesh['req'=4,'exp'=32] {'req','exp'}, dimensions={0} | all-to-all | bytes 4096 | tf_op jit(solution)/shard_map/all_to_all | solution.py:243
  (191 shorter events, 58.1 us)
Async XLA Ops:
  12.3 1.0 copy-start
  12.3 1.4 copy-start.13
  15.2 1.6 copy-start.1
  16.8 2.2 copy-start.5
  27.5 43.4 %copy-start.9 = (bf16[2,1,1024,1024]{3,2,1,0:T(8,128)(2,1)S(1)}, bf16[2,1,1024,1024]{3,2,1,0:T(8,128)(2,1)}, u32[]{:S(2)}) copy-start(bf16[2,1,1024,1024]{3,2,1,0:T(8,128)(2,1)} %param.25) | copy-start | bytes 12582916
  70.9 3.0 copy-start.11
  77.1 4.6 %copy-start.6 = (f32[2,128,8]{1,2,0:T(8,128)S(1)}, f32[2,128,8]{1,2,0:T(8,128)}, u32[]{:S(2)}) copy-start(f32[2,128,8]{1,2,0:T(8,128)} %param.20) | copy-start | bytes 24580
  77.1 38.4 %all-to-all-start.1 = ((bf16[32,40,1024]{2,1,0:T(8,128)(2,1)}), bf16[32,40,1024]{2,1,0:T(8,128)(2,1)S(1)}, u32[]{:S(2)}, u32[]{:S(2)}) async-start(bf16[32,40,1024]{2,1,0:T(8,128)(2,1)} %convolution_convert_fusion.3), calls=%async_computation.1 | async-start | bytes 5242880 | tf_op jit(solution)/shard_map/all_to_all | solution.py:183
  81.6 164.0 %all-gather.3.cloned.1.call-start = ((), (), s32[]{:S(2)}) async-start(), calls=%async_computation.6 | async-start | bytes 8650752 | tf_op jit(solution)/shard_map/all_gather | solution.py:219
  118.8 1.1 copy-start.2
  132.0 1.0 copy-start.3
  136.1 56.3 %copy-start.10 = (bf16[2,1,1024,1024]{3,2,1,0:T(8,128)(2,1)S(1)}, bf16[2,1,1024,1024]{3,2,1,0:T(8,128)(2,1)}, u32[]{:S(2)}) copy-start(bf16[2,1,1024,1024]{3,2,1,0:T(8,128)(2,1)} %param.25) | copy-start | bytes 12582916
  192.5 3.0 copy-start.12
  198.8 38.1 %all-to-all-start.3 = ((bf16[32,40,1024]{2,1,0:T(8,128)(2,1)}), bf16[32,40,1024]{2,1,0:T(8,128)(2,1)S(1)}, u32[]{:S(2)}, u32[]{:S(2)}) async-start(bf16[32,40,1024]{2,1,0:T(8,128)(2,1)} %convolution_convert_fusion.2), calls=%async_computation.3 | async-start | bytes 5242880 | tf_op jit(solution)/shard_map/all_to_all | solution.py:183
  202.9 90.5 %all-gather.5.cloned.1.call-start = ((), (), s32[]{:S(2)}) async-start(), calls=%async_computation.7 | async-start | bytes 8650752 | tf_op jit(solution)/shard_map/all_gather | solution.py:221
  240.1 1.1 copy-start.4
  293.4 53.1 %copy-start.8 = (s32[4]{0:T(128)S(1)}, s32[4]{0:T(128)}, u32[]{:S(2)}) copy-start(s32[4]{0:T(128)} %param.21) | copy-start | bytes 52
  346.3 16.0 %copy-start.7 = (f32[2,128]{1,0:T(2,128)}, f32[2,128]{1,0:T(2,128)S(1)}, u32[]{:S(2)}) copy-start(f32[2,128]{1,0:T(2,128)S(1)} %add_subtract_fusion) | copy-start | bytes 3076
Sparse Core Ops, SparseCore 0:
  120.0 72.2 all-gather.2
  241.3 52.0 all-gather.4

commit v4 on v3

--- a/solution.py
+++ b/solution.py
@@ -94,7 +94,8 @@
         out_weight,
         preferred_element_type=jnp.float32,
     )
-    return (block_states.astype(jnp.float32) + RESIDUAL_SCALE * projected).astype(jnp.bfloat16)
+    summed = block_states.astype(jnp.float32) + RESIDUAL_SCALE * projected
+    return lax.reduce_precision(summed, exponent_bits=8, mantissa_bits=7).astype(jnp.bfloat16)
 
 
 def join_parts(first_part, second_part):
@@ -136,7 +137,7 @@
     lowest = shard * vocab_rows
     vocab_ids = jnp.arange(vocab_rows, dtype=jnp.int32)
     wanted_all = targets - lowest
-    block_rows = 512
+    block_rows = 1024
 
     def model_final(which):
         residual = attend(

time: 370 us -> 361 us (0.976)
  matrix products: 89 us -> 74.4 us
  waiting for transfers between devices: 67.7 us -> 81.3 us
  local copies, waits for them, and re-layouts: 21 us -> 15 us
  loops' own time: 10.8 us -> 5.46 us
    dot_general x16 -> x8, matrix products: 54.2 us -> 39.5 us  [one_block(): jnp.einsum('td,vd->tv', row_block, head, preferred_element_type=jnp.float32)]
    all_gather x1, waiting for transfers between devices: 0.08 us -> 14 us  [per_device(): gathered_second = lax.all_gather(final_second, 'exp', axis=0, tiled=True)]
    another operation x2, loops' own time: 10.8 us -> 5.46 us  [model_stats(): stats = lax.map(one_block, jnp.arange(block_count, dtype=jnp.int32))]
    dynamic_slice x16 -> x8, local copies, waits for them, and re-layouts: 9.93 us -> 4.96 us  [model_stats(): stats = lax.map(one_block, jnp.arange(block_count, dtype=jnp.int32))]
    reduce_sum x16 -> x8, other arithmetic: 11.3 us -> 14 us  [one_block(): masses = jnp.sum(jnp.exp(logits - highest[:, None]), axis=1)]
  transfers between devices with their start and end apart: 4 -> 4, of which waited for: 3 -> 3; matrix products, arithmetic and copies ran while one was open for 20% -> 17% of each run, Pallas kernels for 0% -> 0%
where the time goes in v4:
time: 361 us; the launch traced here: 360 us
  blocking collectives  127 us (35%)
  waiting for transfers between devices  81.3 us (23%)
  matrix products  74.4 us (21%)
  other arithmetic  32.7 us (9%)
  local copies, waits for them, and re-layouts  15 us (4%)
  between operations  14.7 us (4%)
  starting transfers between devices  8.84 us (2%)
  loops' own time  5.46 us (2%)
    all_to_all x2, blocking collectives, model_final(): lax.all_to_all(outgoing.reshape(groups, local_count * CAP, width), 'exp',...  99.7 us
    all_to_all x2, waiting for transfers between devices, model_final(): lax.all_to_all(produced.reshape(groups, local_count * CAP, width), 'exp',...  67.3 us
    dot_general x8, matrix products, one_block(): jnp.einsum('td,vd->tv', row_block, head, preferred_element_type=jnp.float32)  39.5 us
    all_to_all x1, blocking collectives, per_device(): lax.all_to_all(dense_totals.reshape(devices, per_device_seqs), ('req', 'e...  15 us
    reduce_sum x8, other arithmetic, one_block(): masses = jnp.sum(jnp.exp(logits - highest[:, None]), axis=1)  14 us
    all_gather x1, waiting for transfers between devices, per_device(): gathered_second = lax.all_gather(final_second, 'exp', axis=0, tiled=True)  14 us
    reduce_sum x2, other arithmetic, model_final(): jnp.sum((local_slot[None, :, :] == slot_ids[:, None, None]).astype(jnp.bf...  13.4 us
    all_to_all x1, blocking collectives, per_device(): gathered = lax.all_to_all(stacked, 'exp', 0, 0, tiled=True)  12.7 us
  transfers between devices with their start and end apart: 4, of which 3 were waited for; matrix products, arithmetic and copies ran while one was open for 17% of the time, Pallas kernels for 0%

profile of v4, /device:TPU:1, one launch (start us, length us, event | category | flops | bytes accessed | tf_op | source)
XLA Modules:
  0.0 359.7 jit_solution(572011436602492720)
XLA Ops:
  9.2 3.1 fusion.18
  16.8 2.2 multiply_reduce_fusion.5
  19.9 6.7 %fusion.25 = bf16[1280,128]{1,0:T(8,128)(2,1)S(1)} fusion(s32[128,8]{0,1:T(8,128)S(1)} %copy.95), kind=kLoop, calls=%fused_computation.42 | loop fusion | flops 3768320 | bytes 331776 | tf_op jit(solution)/shard_map/reduce_sum | solution.py:159
  27.5 43.4 %all_to_all.34 = bf16[32,40,1024]{2,1,0:T(8,128)(2,1)S(1)} all-to-all(bf16[32,40,1024]{2,1,0:T(8,128)(2,1)S(1)} %bitcast.270), channel_id=1, replica_groups=mesh['req'=4,'exp'=32] {'exp'}, dimensions={0} | all-to-all | bytes 5242880 | tf_op jit(solution)/shard_map/all_to_all | solution.py:167
  70.9 2.9 convolution_bitcast_fusion.1
  73.9 3.3 convolution_convert_fusion.3
  77.2 4.4 %all-to-all-start.1 = ((bf16[32,40,1024]{2,1,0:T(8,128)(2,1)}), bf16[32,40,1024]{2,1,0:T(8,128)(2,1)S(1)}, u32[]{:S(2)}, u32[]{:S(2)}) async-start(bf16[32,40,1024]{2,1,0:T(8,128)(2,1)} %convolution_convert_fusion.3), calls=%async_computation.1 | async-start | bytes 5242880 | tf_op jit(solution)/shard_map/all_to_all | solution.py:184
  81.8 33.8 %all-to-all-done.1 = bf16[32,40,1024]{2,1,0:T(8,128)(2,1)S(1)} async-done(((bf16[32,40,1024]{2,1,0:T(8,128)(2,1)}), bf16[32,40,1024]{2,1,0:T(8,128)(2,1)S(1)}, u32[]{:S(2)}, u32[]{:S(2)}) %all-to-all-start.1) | async-done | bytes 2621472 | tf_op jit(solution)/shard_map/all_to_all | solution.py:184
  115.6 3.2 multiply_reduce_fusion.1
  119.9 3.0 fusion.16
  124.3 6.7 %fusion.24 = bf16[1280,128]{1,0:T(8,128)(2,1)S(1)} fusion(s32[128,8]{0,1:T(8,128)S(1)} %copy.104), kind=kLoop, calls=%fused_computation.41 | loop fusion | flops 3768320 | bytes 331776 | tf_op jit(solution)/shard_map/reduce_sum | solution.py:159
  133.1 2.2 multiply_reduce_fusion.3
  136.2 56.3 %all_to_all.35 = bf16[32,40,1024]{2,1,0:T(8,128)(2,1)S(1)} all-to-all(bf16[32,40,1024]{2,1,0:T(8,128)(2,1)S(1)} %bitcast.271), channel_id=1, replica_groups=mesh['req'=4,'exp'=32] {'exp'}, dimensions={0} | all-to-all | bytes 5242880 | tf_op jit(solution)/shard_map/all_to_all | solution.py:167
  192.5 2.9 convolution_bitcast_fusion
  195.5 3.3 convolution_convert_fusion.2
  198.8 4.1 %all-to-all-start.3 = ((bf16[32,40,1024]{2,1,0:T(8,128)(2,1)}), bf16[32,40,1024]{2,1,0:T(8,128)(2,1)S(1)}, u32[]{:S(2)}, u32[]{:S(2)}) async-start(bf16[32,40,1024]{2,1,0:T(8,128)(2,1)} %convolution_convert_fusion.2), calls=%async_computation.3 | async-start | bytes 5242880 | tf_op jit(solution)/shard_map/all_to_all | solution.py:184
  203.4 33.6 %all-to-all-done.3 = bf16[32,40,1024]{2,1,0:T(8,128)(2,1)S(1)} async-done(((bf16[32,40,1024]{2,1,0:T(8,128)(2,1)}), bf16[32,40,1024]{2,1,0:T(8,128)(2,1)S(1)}, u32[]{:S(2)}, u32[]{:S(2)}) %all-to-all-start.3) | async-done | bytes 2621472 | tf_op jit(solution)/shard_map/all_to_all | solution.py:184
  236.9 3.2 multiply_reduce_fusion
  241.3 4.3 %slice_bitcast_fusion.1 = (bf16[1152,1024]{1,0:T(8,128)(2,1)}, bf16[1152,1024]{1,0:T(8,128)(2,1)S(1)}) fusion(bf16[2,1152,1024]{2,1,0:T(8,128)(2,1)} %param.27), kind=kLoop, calls=%fused_computation.52 | loop fusion | bytes 9437184 | tf_op jit(solution)/shard_map/squeeze | solution.py:202
  245.6 33.7 %while.22 = (s32[]{:T(128)}, f32[4,3,1024]{2,1,0:T(4,128)S(1)}, s32[4]{0:T(128)S(1)}, bf16[4096,1024]{1,0:T(8,128)(2,1)}, bf16[1152,1024]{1,0:T(8,128)(2,1)}, /*...) while((s32[]{:T(128)}, f32[4,3,1024]{2,1,0:T(4,128)S(1)}, ...), condition=%wide.region_15.16_spmd.clone, body=%wide.region_11.15_spmd.clone.sunk | while | flops 2424179712 | bytes 13951147 | solution.py:216
  246.9 5.3 %fusion.204 = (f32[1024]{0:T(1024)S(1)}, f32[1024,1152]{1,0:T(8,128)S(1)}) fusion(bf16[1152,1024]{1,0:T(8,128)(2,1)} %get-tuple-element.312, bf16[4096,1024]{1,0:T(8,128)(2,1)} %get-tuple-element.311, s32[]{:T(128)S(6)} %select_n.42), kind=kOutput, calls=%fused_computation.221.clone.1 | convolution fusion | flops 2418277376 | bytes 9179140 | tf_op jit(solution)/shard_map/while/body/eval_jaxpr/td,vd->tv/dot_general | solution.py:208
  255.3 5.3 %fusion.204 = (f32[1024]{0:T(1024)S(1)}, f32[1024,1152]{1,0:T(8,128)S(1)}) fusion(bf16[1152,1024]{1,0:T(8,128)(2,1)} %get-tuple-element.312, bf16[4096,1024]{1,0:T(8,128)(2,1)} %get-tuple-element.311, s32[]{:T(128)S(6)} %select_n.42), kind=kOutput, calls=%fused_computation.221.clone.1 | convolution fusion | flops 2418277376 | bytes 9179140 | tf_op jit(solution)/shard_map/while/body/eval_jaxpr/td,vd->tv/dot_general | solution.py:208
  263.8 5.3 %fusion.204 = (f32[1024]{0:T(1024)S(1)}, f32[1024,1152]{1,0:T(8,128)S(1)}) fusion(bf16[1152,1024]{1,0:T(8,128)(2,1)} %get-tuple-element.312, bf16[4096,1024]{1,0:T(8,128)(2,1)} %get-tuple-element.311, s32[]{:T(128)S(6)} %select_n.42), kind=kOutput, calls=%fused_computation.221.clone.1 | convolution fusion | flops 2418277376 | bytes 9179140 | tf_op jit(solution)/shard_map/while/body/eval_jaxpr/td,vd->tv/dot_general | solution.py:208
  272.2 5.3 %fusion.204 = (f32[1024]{0:T(1024)S(1)}, f32[1024,1152]{1,0:T(8,128)S(1)}) fusion(bf16[1152,1024]{1,0:T(8,128)(2,1)} %get-tuple-element.312, bf16[4096,1024]{1,0:T(8,128)(2,1)} %get-tuple-element.311, s32[]{:T(128)S(6)} %select_n.42), kind=kOutput, calls=%fused_computation.221.clone.1 | convolution fusion | flops 2418277376 | bytes 9179140 | tf_op jit(solution)/shard_map/while/body/eval_jaxpr/td,vd->tv/dot_general | solution.py:208
  279.3 14.0 %all-gather.5.cloned.1.call-done = bf16[4096,1024]{1,0:T(8,128)(2,1)} async-done(((bf16[128,1024]{1,0:T(8,128)(2,1)}), bf16[4096,1024]{1,0:T(8,128)(2,1)}) %all-gather.5.cloned.1.call-update) | async-done | bytes 8388624 | tf_op jit(solution)/shard_map/all_gather | solution.py:222
  293.3 30.6 %while.23 = (s32[]{:T(128)}, f32[4,3,1024]{2,1,0:T(4,128)S(1)}, s32[4]{0:T(128)S(1)}, bf16[4096,1024]{1,0:T(8,128)(2,1)}, bf16[1152,1024]{1,0:T(8,128)(2,1)S(1)}...) while((s32[]{:T(128)}, f32[4,3,1024]{2,1,0:T(4,128)S(1)}, ...), condition=%wide.region_28.29_spmd.clone, body=%wide.region_24.28_spmd.clone.sunk | while | flops 2424179712 | bytes 13951147 | solution.py:216
  294.6 4.6 %fusion.207 = (f32[1024]{0:T(1024)S(1)}, f32[1024,1152]{1,0:T(8,128)S(1)}) fusion(bf16[1152,1024]{1,0:T(8,128)(2,1)S(1)} %get-tuple-element.282, bf16[4096,1024]{1,0:T(8,128)(2,1)} %get-tuple-element.281, s32[]{:T(128)S(6)} %select_n.43), kind=kOutput, calls=%fused_computation.222.clone.1 | convolution fusion | flops 2418277376 | bytes 9179140 | tf_op jit(solution)/shard_map/while/body/eval_jaxpr/td,vd->tv/dot_general | solution.py:208
  302.2 4.6 %fusion.207 = (f32[1024]{0:T(1024)S(1)}, f32[1024,1152]{1,0:T(8,128)S(1)}) fusion(bf16[1152,1024]{1,0:T(8,128)(2,1)S(1)} %get-tuple-element.282, bf16[4096,1024]{1,0:T(8,128)(2,1)} %get-tuple-element.281, s32[]{:T(128)S(6)} %select_n.43), kind=kOutput, calls=%fused_computation.222.clone.1 | convolution fusion | flops 2418277376 | bytes 9179140 | tf_op jit(solution)/shard_map/while/body/eval_jaxpr/td,vd->tv/dot_general | solution.py:208
  309.9 4.6 %fusion.207 = (f32[1024]{0:T(1024)S(1)}, f32[1024,1152]{1,0:T(8,128)S(1)}) fusion(bf16[1152,1024]{1,0:T(8,128)(2,1)S(1)} %get-tuple-element.282, bf16[4096,1024]{1,0:T(8,128)(2,1)} %get-tuple-element.281, s32[]{:T(128)S(6)} %select_n.43), kind=kOutput, calls=%fused_computation.222.clone.1 | convolution fusion | flops 2418277376 | bytes 9179140 | tf_op jit(solution)/shard_map/while/body/eval_jaxpr/td,vd->tv/dot_general | solution.py:208
  317.5 4.6 %fusion.207 = (f32[1024]{0:T(1024)S(1)}, f32[1024,1152]{1,0:T(8,128)S(1)}) fusion(bf16[1152,1024]{1,0:T(8,128)(2,1)S(1)} %get-tuple-element.282, bf16[4096,1024]{1,0:T(8,128)(2,1)} %get-tuple-element.281, s32[]{:T(128)S(6)} %select_n.43), kind=kOutput, calls=%fused_computation.222.clone.1 | convolution fusion | flops 2418277376 | bytes 9179140 | tf_op jit(solution)/shard_map/while/body/eval_jaxpr/td,vd->tv/dot_general | solution.py:208
  324.1 12.7 %all_to_all.36 = f32[32,3,2,128]{3,2,1,0:T(2,128)S(1)} all-to-all(f32[32,3,2,128]{3,2,1,0:T(2,128)S(1)} %copy.106), channel_id=1, replica_groups=mesh['req'=4,'exp'=32] {'exp'}, dimensions={0} | all-to-all | bytes 196608 | tf_op jit(solution)/shard_map/all_to_all | solution.py:226
  337.2 15.0 %all_to_all.37 = f32[128,1,4]{2,1,0:T(1,128)S(1)} all-to-all(f32[128,1,4]{2,1,0:T(1,128)S(1)} %bitcast.302), channel_id=1, replica_groups=mesh['req'=4,'exp'=32] {'req','exp'}, dimensions={0} | all-to-all | bytes 4096 | tf_op jit(solution)/shard_map/all_to_all | solution.py:244
  (151 shorter events, 35.8 us)
Async XLA Ops:
  12.3 1.0 copy-start
  12.3 1.4 copy-start.13
  15.2 1.6 copy-start.1
  16.8 2.2 copy-start.5
  27.5 43.4 %copy-start.9 = (bf16[2,1,1024,1024]{3,2,1,0:T(8,128)(2,1)S(1)}, bf16[2,1,1024,1024]{3,2,1,0:T(8,128)(2,1)}, u32[]{:S(2)}) copy-start(bf16[2,1,1024,1024]{3,2,1,0:T(8,128)(2,1)} %param.25) | copy-start | bytes 12582916
  70.9 3.0 copy-start.11
  77.2 4.6 %copy-start.6 = (f32[2,128,8]{1,2,0:T(8,128)S(1)}, f32[2,128,8]{1,2,0:T(8,128)}, u32[]{:S(2)}) copy-start(f32[2,128,8]{1,2,0:T(8,128)} %param.20) | copy-start | bytes 24580
  77.2 38.4 %all-to-all-start.1 = ((bf16[32,40,1024]{2,1,0:T(8,128)(2,1)}), bf16[32,40,1024]{2,1,0:T(8,128)(2,1)S(1)}, u32[]{:S(2)}, u32[]{:S(2)}) async-start(bf16[32,40,1024]{2,1,0:T(8,128)(2,1)} %convolution_convert_fusion.3), calls=%async_computation.1 | async-start | bytes 5242880 | tf_op jit(solution)/shard_map/all_to_all | solution.py:184
  81.6 164.0 %all-gather.3.cloned.1.call-start = ((), (), s32[]{:S(2)}) async-start(), calls=%async_computation.6 | async-start | bytes 8650752 | tf_op jit(solution)/shard_map/all_gather | solution.py:220
  118.8 1.1 copy-start.2
  132.0 1.0 copy-start.3
  136.2 56.3 %copy-start.10 = (bf16[2,1,1024,1024]{3,2,1,0:T(8,128)(2,1)S(1)}, bf16[2,1,1024,1024]{3,2,1,0:T(8,128)(2,1)}, u32[]{:S(2)}) copy-start(bf16[2,1,1024,1024]{3,2,1,0:T(8,128)(2,1)} %param.25) | copy-start | bytes 12582916
  192.5 3.0 copy-start.12
  198.8 38.1 %all-to-all-start.3 = ((bf16[32,40,1024]{2,1,0:T(8,128)(2,1)}), bf16[32,40,1024]{2,1,0:T(8,128)(2,1)S(1)}, u32[]{:S(2)}, u32[]{:S(2)}) async-start(bf16[32,40,1024]{2,1,0:T(8,128)(2,1)} %convolution_convert_fusion.2), calls=%async_computation.3 | async-start | bytes 5242880 | tf_op jit(solution)/shard_map/all_to_all | solution.py:184
  202.9 90.4 %all-gather.5.cloned.1.call-start = ((), (), s32[]{:S(2)}) async-start(), calls=%async_computation.7 | async-start | bytes 8650752 | tf_op jit(solution)/shard_map/all_gather | solution.py:222
  240.2 1.1 copy-start.4
  293.3 43.7 %copy-start.8 = (s32[4]{0:T(128)S(1)}, s32[4]{0:T(128)}, u32[]{:S(2)}) copy-start(s32[4]{0:T(128)} %param.21) | copy-start | bytes 52
  336.9 16.0 %copy-start.7 = (f32[2,128]{1,0:T(2,128)}, f32[2,128]{1,0:T(2,128)S(1)}, u32[]{:S(2)}) copy-start(f32[2,128]{1,0:T(2,128)S(1)} %add_subtract_fusion) | copy-start | bytes 3076
Sparse Core Ops, SparseCore 0:
  120.0 72.2 all-gather.2
  241.3 51.9 all-gather.4

commit v5 on v4

--- a/solution.py
+++ b/solution.py
@@ -139,7 +139,7 @@
     wanted_all = targets - lowest
     block_rows = 1024
 
-    def model_final(which):
+    def model_entry(which):
         residual = attend(
             states[which],
             segment,
@@ -164,13 +164,9 @@
         outgoing = jnp.dot(chooser, moe_in, preferred_element_type=jnp.float32).astype(
             jnp.bfloat16
         )
-        arrived = lax.all_to_all(
-            outgoing.reshape(groups, local_count * CAP, width),
-            "exp",
-            split_axis=0,
-            concat_axis=0,
-            tiled=True,
-        )
+        return residual, local_slot, outgoing.reshape(groups, local_count * CAP, width)
+
+    def model_experts(which, arrived):
         inputs = arrived.reshape(groups, local_count, CAP, width)
         gate_up = jnp.einsum(
             "slcd,ldf->slcf", inputs, expert_in[which], preferred_element_type=jnp.float32
@@ -181,13 +177,10 @@
         produced = jnp.einsum(
             "slcf,lfd->slcd", hidden, expert_down[which], preferred_element_type=jnp.float32
         ).astype(jnp.bfloat16)
-        returned = lax.all_to_all(
-            produced.reshape(groups, local_count * CAP, width),
-            "exp",
-            split_axis=0,
-            concat_axis=0,
-            tiled=True,
-        ).reshape(slots, width)
+        return produced.reshape(groups, local_count * CAP, width)
+
+    def model_exit(which, residual, local_slot, returned):
+        returned = returned.reshape(slots, width)
         picker = (local_slot[..., None] == slot_ids[None, None, :]).astype(jnp.bfloat16)
         picked = jnp.einsum("tks,sd->tkd", picker, returned, preferred_element_type=jnp.float32)
         mixture = jnp.sum(gate_probs[which][..., None] * picked, axis=1)
@@ -195,6 +188,9 @@
             residual.astype(jnp.float32) + RESIDUAL_SCALE * mixture, norm_gains[which, 2]
         ).astype(jnp.bfloat16)
         return final
+
+    def exchange(blocks):
+        return lax.all_to_all(blocks, "exp", split_axis=0, concat_axis=0, tiled=True)
 
     def model_stats(which, chunk):
         chunk_rows = chunk.shape[0]
@@ -216,9 +212,15 @@
         stats = lax.map(one_block, jnp.arange(block_count, dtype=jnp.int32))
         return jnp.transpose(stats, (1, 0, 2)).reshape(3, groups, token_count)
 
-    final_first = model_final(0)
+    row_span = local_count * CAP
+    residual_first, slot_first, outgoing_first = model_entry(0)
+    produced_first = model_experts(0, exchange(outgoing_first))
+    residual_second, slot_second, outgoing_second = model_entry(1)
+    crossed = exchange(jnp.concatenate([produced_first, outgoing_second], axis=1))
+    final_first = model_exit(0, residual_first, slot_first, crossed[:, :row_span])
     gathered_first = lax.all_gather(final_first, "exp", axis=0, tiled=True)
-    final_second = model_final(1)
+    produced_second = model_experts(1, crossed[:, row_span:])
+    final_second = model_exit(1, residual_second, slot_second, exchange(produced_second))
     gathered_second = lax.all_gather(final_second, "exp", axis=0, tiled=True)
     stats_first = model_stats(0, gathered_first)
     stats_second = model_stats(1, gathered_second)

time: 361 us -> 358 us (level); the launches traced: 360 us -> 351 us
  blocking collectives: 127 us -> 27.7 us
  waiting for transfers between devices: 81.3 us -> 127 us
  starting transfers between devices: 8.84 us -> 37 us
  matrix products: 74.4 us -> 81.3 us
  local copies, waits for them, and re-layouts: 15 us -> 21.6 us
    all_to_all x2 -> x0, blocking collectives: 99.7 us -> none  [model_final(): lax.all_to_all(outgoing.reshape(groups, local_count * CAP, width), 'exp',...]
    all_to_all x2 -> x3, waiting for transfers between devices: 67.3 us -> 98.7 us  [exchange(): lax.all_to_all(blocks, 'exp', split_axis=0, concat_axis=0, tiled=True)]
    all_to_all x2 -> x3, starting transfers between devices: 8.54 us -> 25.2 us  [exchange(): lax.all_to_all(blocks, 'exp', split_axis=0, concat_axis=0, tiled=True)]
    all_gather x1, starting transfers between devices: 0.04 us -> 11.7 us  [per_device(): gathered_first = lax.all_gather(final_first, 'exp', axis=0, tiled=True)]
    all_gather x1, waiting for transfers between devices: 0.01 us -> 8.07 us  [per_device(): gathered_first = lax.all_gather(final_first, 'exp', axis=0, tiled=True)]
    all_gather x1, waiting for transfers between devices: 14 us -> 20.4 us  [per_device(): gathered_second = lax.all_gather(final_second, 'exp', axis=0, tiled=True)]
    dot_general x10, matrix products: 21.8 us -> 26.8 us  [the longest x2 10.9 us: model_experts(): jnp.einsum('slcd,ldf->slcf', inputs, expert_in[which], preferred_element_...]
  transfers between devices with their start and end apart: 4 -> 5, of which waited for: 3 -> 5; matrix products, arithmetic and copies ran while one was open for 17% -> 19% of each run, Pallas kernels for 0% -> 0%
where the time goes in v5:
time: 358 us; the launch traced here: 351 us
  waiting for transfers between devices  127 us (35%)
  matrix products  81.3 us (23%)
  starting transfers between devices  37 us (10%)
  other arithmetic  35.7 us (10%)
  blocking collectives  27.7 us (8%)
  local copies, waits for them, and re-layouts  21.6 us (6%)
  between operations  14.9 us (4%)
  loops' own time  5.46 us (2%)
    all_to_all x3, waiting for transfers between devices, exchange(): lax.all_to_all(blocks, 'exp', split_axis=0, concat_axis=0, tiled=True)  98.7 us
    dot_general x8, matrix products, one_block(): jnp.einsum('td,vd->tv', row_block, head, preferred_element_type=jnp.float32)  39.7 us
    all_to_all x3, starting transfers between devices, exchange(): lax.all_to_all(blocks, 'exp', split_axis=0, concat_axis=0, tiled=True)  25.2 us
    all_gather x1, waiting for transfers between devices, per_device(): gathered_second = lax.all_gather(final_second, 'exp', axis=0, tiled=True)  20.4 us
    all_to_all x1, blocking collectives, per_device(): lax.all_to_all(dense_totals.reshape(devices, per_device_seqs), ('req', 'e...  15 us
    reduce_sum x8, other arithmetic, one_block(): masses = jnp.sum(jnp.exp(logits - highest[:, None]), axis=1)  14 us
    reduce_sum x2, other arithmetic, model_entry(): jnp.sum((local_slot[None, :, :] == slot_ids[:, None, None]).astype(jnp.bf...  13.4 us
    all_to_all x1, blocking collectives, per_device(): gathered = lax.all_to_all(stacked, 'exp', 0, 0, tiled=True)  12.7 us
  transfers between devices with their start and end apart: 5, of which 5 were waited for; matrix products, arithmetic and copies ran while one was open for 19% of the time, Pallas kernels for 0%

profile of v5, /device:TPU:1, one launch (start us, length us, event | category | flops | bytes accessed | tf_op | source)
XLA Modules:
  0.0 350.8 jit_solution(3546603313654688870)
XLA Ops:
  9.8 3.1 fusion.18
  21.6 6.7 %fusion.25 = bf16[1280,128]{1,0:T(8,128)(2,1)S(1)} fusion(s32[128,8]{0,1:T(8,128)S(1)} %copy.95), kind=kLoop, calls=%fused_computation.43 | loop fusion | flops 3768320 | bytes 331776 | tf_op jit(solution)/shard_map/reduce_sum | solution.py:159
  30.8 9.9 %all-to-all-start = ((bf16[32,40,1024]{2,1,0:T(8,128)(2,1)}), bf16[32,40,1024]{2,1,0:T(8,128)(2,1)}, u32[]{:S(2)}, u32[]{:S(2)}) async-start(bf16[32,40,1024]{2,1,0:T(8,128)(2,1)} %bitcast.26), calls=%async_computation | async-start | bytes 5242880 | tf_op jit(solution)/shard_map/all_to_all | solution.py:193
  40.7 3.0 fusion.16
  47.0 6.7 %fusion.24 = bf16[1280,128]{1,0:T(8,128)(2,1)S(1)} fusion(s32[128,8]{0,1:T(8,128)S(1)} %copy.97), kind=kLoop, calls=%fused_computation.42 | loop fusion | flops 3768320 | bytes 331776 | tf_op jit(solution)/shard_map/reduce_sum | solution.py:159
  61.5 13.1 %all-to-all-done = bf16[32,40,1024]{2,1,0:T(8,128)(2,1)} async-done(((bf16[32,40,1024]{2,1,0:T(8,128)(2,1)}), bf16[32,40,1024]{2,1,0:T(8,128)(2,1)}, u32[]{:S(2)}, u32[]{:S(2)}) %all-to-all-start) | async-done | bytes 2621472 | tf_op jit(solution)/shard_map/all_to_all | solution.py:193
  74.6 5.5 %convolution_bitcast_fusion = f32[32,1,40,1024]{3,2,0,1:T(8,128)S(1)} fusion(bf16[32,40,1024]{2,1,0:T(8,128)(2,1)} %all-to-all-done, bf16[2,1,1024,1024]{3,2,1,0:T(8,128)(2,1)} %param.25), kind=kOutput, calls=%fused_computation.53 | convolution fusion | flops 2684354560 | bytes 9961472 | tf_op jit(solution)/shard_map/slcd,ldf->slcf/dot_general | solution.py:171
  81.8 3.0 pad_maximum_fusion
  84.8 7.1 %all-to-all-start.1 = ((bf16[32,80,1024]{2,1,0:T(8,128)(2,1)}), bf16[32,80,1024]{2,1,0:T(8,128)(2,1)}, u32[]{:S(2)}, u32[]{:S(2)}) async-start(bf16[32,80,1024]{2,1,0:T(8,128)(2,1)} %pad_maximum_fusion), calls=%async_computation.1 | async-start | bytes 10485760 | tf_op jit(solution)/shard_map/all_to_all | solution.py:193
  91.9 11.7 %all-gather.3.cloned.1.call-start = ((), (), s32[]{:S(2)}) async-start(), calls=%async_computation.5 | async-start | bytes 8650752 | tf_op jit(solution)/shard_map/all_gather | solution.py:221
  103.8 50.0 %all-to-all-done.1 = bf16[32,80,1024]{2,1,0:T(8,128)(2,1)} async-done(((bf16[32,80,1024]{2,1,0:T(8,128)(2,1)}), bf16[32,80,1024]{2,1,0:T(8,128)(2,1)}, u32[]{:S(2)}, u32[]{:S(2)}) %all-to-all-start.1) | async-done | bytes 5242912 | tf_op jit(solution)/shard_map/all_to_all | solution.py:193
  155.8 3.3 multiply_reduce_fusion.1
  160.1 5.4 %fusion.32 = f32[32,1,40,1024]{3,2,0,1:T(8,128)S(1)} fusion(bf16[32,80,1024]{2,1,0:T(8,128)(2,1)} %all-to-all-done.1, bf16[2,1,1024,1024]{3,2,1,0:T(8,128)(2,1)} %param.25), kind=kOutput, calls=%fused_computation.52 | convolution fusion | flops 2684354560 | bytes 9961472 | tf_op jit(solution)/shard_map/slcd,ldf->slcf/dot_general | solution.py:171
  165.6 3.3 convolution_convert_fusion.2
  168.9 8.2 %all-to-all-start.2 = ((bf16[32,40,1024]{2,1,0:T(8,128)(2,1)}), bf16[32,40,1024]{2,1,0:T(8,128)(2,1)S(1)}, u32[]{:S(2)}, u32[]{:S(2)}) async-start(bf16[32,40,1024]{2,1,0:T(8,128)(2,1)} %convolution_convert_fusion.2), calls=%async_computation.2 | async-start | bytes 5242880 | tf_op jit(solution)/shard_map/all_to_all | solution.py:193
  177.3 35.7 %all-to-all-done.2 = bf16[32,40,1024]{2,1,0:T(8,128)(2,1)S(1)} async-done(((bf16[32,40,1024]{2,1,0:T(8,128)(2,1)}), bf16[32,40,1024]{2,1,0:T(8,128)(2,1)S(1)}, u32[]{:S(2)}, u32[]{:S(2)}) %all-to-all-start.2) | async-done | bytes 2621472 | tf_op jit(solution)/shard_map/all_to_all | solution.py:193
  213.0 3.2 multiply_reduce_fusion
  217.3 4.5 %slice_bitcast_fusion.1 = (bf16[1152,1024]{1,0:T(8,128)(2,1)}, bf16[1152,1024]{1,0:T(8,128)(2,1)S(1)}) fusion(bf16[2,1152,1024]{2,1,0:T(8,128)(2,1)} %param.27), kind=kLoop, calls=%fused_computation.55 | loop fusion | bytes 9437184 | tf_op jit(solution)/shard_map/squeeze | solution.py:198
  221.8 8.1 %all-gather.3.cloned.1.call-done = bf16[4096,1024]{1,0:T(8,128)(2,1)} async-done(((bf16[128,1024]{1,0:T(8,128)(2,1)}), bf16[4096,1024]{1,0:T(8,128)(2,1)}) %all-gather.3.cloned.1.call-update) | async-done | bytes 8388624 | tf_op jit(solution)/shard_map/all_gather | solution.py:221
  229.9 33.8 %while.22 = (s32[]{:T(128)}, f32[4,3,1024]{2,1,0:T(4,128)S(1)}, s32[4]{0:T(128)S(1)}, bf16[4096,1024]{1,0:T(8,128)(2,1)}, bf16[1152,1024]{1,0:T(8,128)(2,1)}, /*...) while((s32[]{:T(128)}, f32[4,3,1024]{2,1,0:T(4,128)S(1)}, ...), condition=%wide.region_21.22_spmd.clone, body=%wide.region_17.21_spmd.clone.sunk | while | flops 2424179712 | bytes 13951147 | solution.py:212
  231.2 5.3 %fusion.208 = (f32[1024]{0:T(1024)S(1)}, f32[1024,1152]{1,0:T(8,128)S(1)}) fusion(bf16[1152,1024]{1,0:T(8,128)(2,1)} %get-tuple-element.312, bf16[4096,1024]{1,0:T(8,128)(2,1)} %get-tuple-element.311, s32[]{:T(128)S(6)} %select_n.42), kind=kOutput, calls=%fused_computation.224.clone.1 | convolution fusion | flops 2418277376 | bytes 9179140 | tf_op jit(solution)/shard_map/while/body/eval_jaxpr/td,vd->tv/dot_general | solution.py:204
  239.6 5.5 %fusion.208 = (f32[1024]{0:T(1024)S(1)}, f32[1024,1152]{1,0:T(8,128)S(1)}) fusion(bf16[1152,1024]{1,0:T(8,128)(2,1)} %get-tuple-element.312, bf16[4096,1024]{1,0:T(8,128)(2,1)} %get-tuple-element.311, s32[]{:T(128)S(6)} %select_n.42), kind=kOutput, calls=%fused_computation.224.clone.1 | convolution fusion | flops 2418277376 | bytes 9179140 | tf_op jit(solution)/shard_map/while/body/eval_jaxpr/td,vd->tv/dot_general | solution.py:204
  248.1 5.3 %fusion.208 = (f32[1024]{0:T(1024)S(1)}, f32[1024,1152]{1,0:T(8,128)S(1)}) fusion(bf16[1152,1024]{1,0:T(8,128)(2,1)} %get-tuple-element.312, bf16[4096,1024]{1,0:T(8,128)(2,1)} %get-tuple-element.311, s32[]{:T(128)S(6)} %select_n.42), kind=kOutput, calls=%fused_computation.224.clone.1 | convolution fusion | flops 2418277376 | bytes 9179140 | tf_op jit(solution)/shard_map/while/body/eval_jaxpr/td,vd->tv/dot_general | solution.py:204
  256.6 5.3 %fusion.208 = (f32[1024]{0:T(1024)S(1)}, f32[1024,1152]{1,0:T(8,128)S(1)}) fusion(bf16[1152,1024]{1,0:T(8,128)(2,1)} %get-tuple-element.312, bf16[4096,1024]{1,0:T(8,128)(2,1)} %get-tuple-element.311, s32[]{:T(128)S(6)} %select_n.42), kind=kOutput, calls=%fused_computation.224.clone.1 | convolution fusion | flops 2418277376 | bytes 9179140 | tf_op jit(solution)/shard_map/while/body/eval_jaxpr/td,vd->tv/dot_general | solution.py:204
  263.7 20.4 %all-gather.5.cloned.1.call-done = bf16[4096,1024]{1,0:T(8,128)(2,1)} async-done(((bf16[128,1024]{1,0:T(8,128)(2,1)}), bf16[4096,1024]{1,0:T(8,128)(2,1)}) %all-gather.5.cloned.1.call-update) | async-done | bytes 8388624 | tf_op jit(solution)/shard_map/all_gather | solution.py:224
  284.2 30.6 %while.23 = (s32[]{:T(128)}, f32[4,3,1024]{2,1,0:T(4,128)S(1)}, s32[4]{0:T(128)S(1)}, bf16[4096,1024]{1,0:T(8,128)(2,1)}, bf16[1152,1024]{1,0:T(8,128)(2,1)S(1)}...) while((s32[]{:T(128)}, f32[4,3,1024]{2,1,0:T(4,128)S(1)}, ...), condition=%wide.region_28.29_spmd.clone, body=%wide.region_24.28_spmd.clone.sunk | while | flops 2424179712 | bytes 13951147 | solution.py:212
  285.5 4.6 %fusion.211 = (f32[1024]{0:T(1024)S(1)}, f32[1024,1152]{1,0:T(8,128)S(1)}) fusion(bf16[1152,1024]{1,0:T(8,128)(2,1)S(1)} %get-tuple-element.282, bf16[4096,1024]{1,0:T(8,128)(2,1)} %get-tuple-element.281, s32[]{:T(128)S(6)} %select_n.43), kind=kOutput, calls=%fused_computation.225.clone.1 | convolution fusion | flops 2418277376 | bytes 9179140 | tf_op jit(solution)/shard_map/while/body/eval_jaxpr/td,vd->tv/dot_general | solution.py:204
  293.1 4.6 %fusion.211 = (f32[1024]{0:T(1024)S(1)}, f32[1024,1152]{1,0:T(8,128)S(1)}) fusion(bf16[1152,1024]{1,0:T(8,128)(2,1)S(1)} %get-tuple-element.282, bf16[4096,1024]{1,0:T(8,128)(2,1)} %get-tuple-element.281, s32[]{:T(128)S(6)} %select_n.43), kind=kOutput, calls=%fused_computation.225.clone.1 | convolution fusion | flops 2418277376 | bytes 9179140 | tf_op jit(solution)/shard_map/while/body/eval_jaxpr/td,vd->tv/dot_general | solution.py:204
  300.8 4.6 %fusion.211 = (f32[1024]{0:T(1024)S(1)}, f32[1024,1152]{1,0:T(8,128)S(1)}) fusion(bf16[1152,1024]{1,0:T(8,128)(2,1)S(1)} %get-tuple-element.282, bf16[4096,1024]{1,0:T(8,128)(2,1)} %get-tuple-element.281, s32[]{:T(128)S(6)} %select_n.43), kind=kOutput, calls=%fused_computation.225.clone.1 | convolution fusion | flops 2418277376 | bytes 9179140 | tf_op jit(solution)/shard_map/while/body/eval_jaxpr/td,vd->tv/dot_general | solution.py:204
  308.4 4.6 %fusion.211 = (f32[1024]{0:T(1024)S(1)}, f32[1024,1152]{1,0:T(8,128)S(1)}) fusion(bf16[1152,1024]{1,0:T(8,128)(2,1)S(1)} %get-tuple-element.282, bf16[4096,1024]{1,0:T(8,128)(2,1)} %get-tuple-element.281, s32[]{:T(128)S(6)} %select_n.43), kind=kOutput, calls=%fused_computation.225.clone.1 | convolution fusion | flops 2418277376 | bytes 9179140 | tf_op jit(solution)/shard_map/while/body/eval_jaxpr/td,vd->tv/dot_general | solution.py:204
  315.0 12.7 %all_to_all.29 = f32[32,3,2,128]{3,2,1,0:T(2,128)S(1)} all-to-all(f32[32,3,2,128]{3,2,1,0:T(2,128)S(1)} %copy.106), channel_id=1, replica_groups=mesh['req'=4,'exp'=32] {'exp'}, dimensions={0} | all-to-all | bytes 196608 | tf_op jit(solution)/shard_map/all_to_all | solution.py:228
  328.1 15.0 %all_to_all.30 = f32[128,1,4]{2,1,0:T(1,128)S(1)} all-to-all(f32[128,1,4]{2,1,0:T(1,128)S(1)} %bitcast.300), channel_id=1, replica_groups=mesh['req'=4,'exp'=32] {'req','exp'}, dimensions={0} | all-to-all | bytes 4096 | tf_op jit(solution)/shard_map/all_to_all | solution.py:246
  (175 shorter events, 51.3 us)
Async XLA Ops:
  9.8 4.5 %copy-start.24 = (s32[1,4]{1,0:T(1,128)S(1)}, s32[1,4]{1,0:T(1,128)}, u32[]{:S(2)}) copy-start(s32[1,4]{1,0:T(1,128)} %param.17) | copy-start | bytes 52
  12.9 1.0 copy-start.4
  14.6 2.8 copy-start.18
  15.3 2.1 copy-start.5
  15.8 3.7 %copy-start.16 = (s32[2,128,8]{1,2,0:T(8,128)S(1)}, s32[2,128,8]{1,2,0:T(8,128)}, u32[]{:S(2)}) copy-start(s32[2,128,8]{1,2,0:T(8,128)} %param.19) | copy-start | bytes 24580
  20.2 10.6 %copy-start.2 = (s32[1,128,8]{2,1,0:T(8,128)}, s32[1,128,8]{2,1,0:T(8,128)S(1)}, u32[]{:S(2)}) copy-start(s32[1,128,8]{2,1,0:T(8,128)S(1)} %copy.115) | copy-start | bytes 12292
  20.9 0.6 copy-start.10
  30.8 43.8 %all-to-all-start = ((bf16[32,40,1024]{2,1,0:T(8,128)(2,1)}), bf16[32,40,1024]{2,1,0:T(8,128)(2,1)}, u32[]{:S(2)}, u32[]{:S(2)}) async-start(bf16[32,40,1024]{2,1,0:T(8,128)(2,1)} %bitcast.26), calls=%async_computation | async-start | bytes 5242880 | tf_op jit(solution)/shard_map/all_to_all | solution.py:193
  46.3 0.6 copy-start.8
  53.8 0.7 copy-start.7
  56.2 1.4 copy-start.6
  56.2 4.3 %copy-start.14 = (f32[1,1,1024]{2,0,1:T(1,128)S(1)}, f32[1,1,1024]{2,0,1:T(1,128)}, u32[]{:S(2)}) copy-start(f32[1,1,1024]{2,0,1:T(1,128)} %get-tuple-element.151) | copy-start | bytes 12292
  59.8 0.8 copy-start
  74.5 5.5 %copy-start.22 = (bf16[2,1,512,1024]{3,2,1,0:T(8,128)(2,1)S(1)}, bf16[2,1,512,1024]{3,2,1,0:T(8,128)(2,1)}, u32[]{:S(2)}) copy-start(bf16[2,1,512,1024]{3,2,1,0:T(8,128)(2,1)} %param.26) | copy-start | bytes 6291460
  84.8 18.8 %copy-start.11 = (s32[1024]{0:T(1024)S(1)}, s32[1024]{0:T(1024)}, u32[]{:S(2)}) copy-start(s32[1024]{0:T(1024)} %copy-done.10) | copy-start | bytes 12292
  84.8 18.9 %copy-start.3 = (s32[1,128,8]{2,1,0:T(8,128)S(1)}, s32[1,128,8]{2,1,0:T(8,128)}, u32[]{:S(2)}) copy-start(s32[1,128,8]{2,1,0:T(8,128)} %copy-done.2) | copy-start | bytes 12292
  84.8 19.0 %copy-start.17 = (f32[2,128,8]{1,2,0:T(8,128)S(1)}, f32[2,128,8]{1,2,0:T(8,128)}, u32[]{:S(2)}) copy-start(f32[2,128,8]{1,2,0:T(8,128)} %param.20) | copy-start | bytes 24580
  84.8 69.0 %all-to-all-start.1 = ((bf16[32,80,1024]{2,1,0:T(8,128)(2,1)}), bf16[32,80,1024]{2,1,0:T(8,128)(2,1)}, u32[]{:S(2)}, u32[]{:S(2)}) async-start(bf16[32,80,1024]{2,1,0:T(8,128)(2,1)} %pad_maximum_fusion), calls=%async_computation.1 | async-start | bytes 10485760 | tf_op jit(solution)/shard_map/all_to_all | solution.py:193
  91.9 138.0 %all-gather.3.cloned.1.call-start = ((), (), s32[]{:S(2)}) async-start(), calls=%async_computation.5 | async-start | bytes 8650752 | tf_op jit(solution)/shard_map/all_gather | solution.py:221
  155.8 3.5 copy-start.13
  160.1 5.5 %copy-start.23 = (bf16[2,1,512,1024]{3,2,1,0:T(8,128)(2,1)S(1)}, bf16[2,1,512,1024]{3,2,1,0:T(8,128)(2,1)}, u32[]{:S(2)}) copy-start(bf16[2,1,512,1024]{3,2,1,0:T(8,128)(2,1)} %param.26) | copy-start | bytes 6291460
  168.9 8.3 %copy-start.9 = (s32[1024]{0:T(1024)S(1)}, s32[1024]{0:T(1024)}, u32[]{:S(2)}) copy-start(s32[1024]{0:T(1024)} %copy-done.8) | copy-start | bytes 12292
  168.9 44.1 %all-to-all-start.2 = ((bf16[32,40,1024]{2,1,0:T(8,128)(2,1)}), bf16[32,40,1024]{2,1,0:T(8,128)(2,1)S(1)}, u32[]{:S(2)}, u32[]{:S(2)}) async-start(bf16[32,40,1024]{2,1,0:T(8,128)(2,1)} %convolution_convert_fusion.2), calls=%async_computation.2 | async-start | bytes 5242880 | tf_op jit(solution)/shard_map/all_to_all | solution.py:193
  177.1 107.1 %all-gather.5.cloned.1.call-start = ((), (), s32[]{:S(2)}) async-start(), calls=%async_computation.6 | async-start | bytes 8650752 | tf_op jit(solution)/shard_map/all_gather | solution.py:224
  213.0 3.2 copy-start.1
  213.0 3.4 copy-start.12
  213.0 4.3 %copy-start.15 = (s32[4096]{0:T(1024)S(1)}, s32[4096]{0:T(1024)}, u32[]{:S(2)}) copy-start(s32[4096]{0:T(1024)} %param.18) | copy-start | bytes 49156
  284.2 43.6 %copy-start.19 = (s32[128]{0:T(128)S(1)}, s32[128]{0:T(128)}, u32[]{:S(2)}) copy-start(s32[128]{0:T(128)} %copy-done.18) | copy-start | bytes 1540
  284.2 43.7 %copy-start.21 = (s32[4]{0:T(128)S(1)}, s32[4]{0:T(128)}, u32[]{:S(2)}) copy-start(s32[4]{0:T(128)} %param.21) | copy-start | bytes 52
  327.8 16.0 %copy-start.20 = (f32[2,128]{1,0:T(2,128)}, f32[2,128]{1,0:T(2,128)S(1)}, u32[]{:S(2)}) copy-start(f32[2,128]{1,0:T(2,128)S(1)} %add_subtract_fusion) | copy-start | bytes 3076
Sparse Core Ops, SparseCore 0:
  160.3 69.5 all-gather.2
  232.1 52.0 all-gather.4

commit v6 on v5

--- a/solution.py
+++ b/solution.py
@@ -156,14 +156,11 @@
         running = jnp.dot(lower, onehot, preferred_element_type=jnp.float32)
         rank_slot = jnp.sum((running - 1.0) * onehot.astype(jnp.float32), axis=1).astype(jnp.int32)
         local_slot = (flat_routes * CAP + rank_slot).reshape(token_count, TOP)
-        chooser = jnp.sum(
-            (local_slot[None, :, :] == slot_ids[:, None, None]).astype(jnp.bfloat16),
-            axis=2,
-            dtype=jnp.bfloat16,
-        )
-        outgoing = jnp.dot(chooser, moe_in, preferred_element_type=jnp.float32).astype(
-            jnp.bfloat16
-        )
+        chooser = (local_slot.reshape(pairs)[:, None] == slot_ids[None, :]).astype(jnp.bfloat16)
+        repeated = jnp.repeat(moe_in, TOP, axis=0)
+        outgoing = jnp.einsum(
+            "ps,pd->sd", chooser, repeated, preferred_element_type=jnp.float32
+        ).astype(jnp.bfloat16)
         return residual, local_slot, outgoing.reshape(groups, local_count * CAP, width)
 
     def model_experts(which, arrived):
@@ -195,9 +192,8 @@
     def model_stats(which, chunk):
         chunk_rows = chunk.shape[0]
         block_count = chunk_rows // block_rows
-        head = vocab_head[which]
-
         def one_block(block_number):
+            head = vocab_head[which]
             row_block = lax.dynamic_slice_in_dim(chunk, block_number * block_rows, block_rows, 0)
             wanted = lax.dynamic_slice_in_dim(wanted_all, block_number * block_rows, block_rows, 0)
             logits = (

time: 358 us -> 347 us (0.969); the launches traced: 351 us -> 346 us
  waiting for transfers between devices: 127 us -> 149 us
  other arithmetic: 35.7 us -> 22.4 us
  local copies, waits for them, and re-layouts: 21.6 us -> 10.3 us
  starting transfers between devices: 37 us -> 26 us
  matrix products: 81.3 us -> 90.3 us
    all_to_all x3, waiting for transfers between devices: 98.7 us -> 117 us  [exchange(): lax.all_to_all(blocks, 'exp', split_axis=0, concat_axis=0, tiled=True)]
    reduce_sum x2 -> x0, other arithmetic: 13.4 us -> none  [model_entry(): jnp.sum((local_slot[None, :, :] == slot_ids[:, None, None]).astype(jnp.bf...]
    all_gather x1, starting transfers between devices: 11.7 us -> 0.26 us  [per_device(): gathered_first = lax.all_gather(final_first, 'exp', axis=0, tiled=True)]
    dot_general x2, matrix products: 3.34 us -> 9.81 us  [model_entry(): jnp.einsum('ps,pd->sd', chooser, repeated, preferred_element_type=jnp.flo...]
    squeeze x1 -> x0, local copies, waits for them, and re-layouts: 4.5 us -> none  [model_stats(): head = vocab_head[which]]
  transfers between devices with their start and end apart: 5 -> 5, of which waited for: 5 -> 5; matrix products, arithmetic and copies ran while one was open for 19% -> 17% of each run, Pallas kernels for 0% -> 0%
where the time goes in v6:
time: 347 us; the launch traced here: 346 us
  waiting for transfers between devices  149 us (43%)
  matrix products  90.3 us (26%)
  blocking collectives  27.7 us (8%)
  starting transfers between devices  26 us (7%)
  other arithmetic  22.4 us (6%)
  between operations  14.6 us (4%)
  local copies, waits for them, and re-layouts  10.3 us (3%)
  loops' own time  5.45 us (2%)
    all_to_all x3, waiting for transfers between devices, exchange(): lax.all_to_all(blocks, 'exp', split_axis=0, concat_axis=0, tiled=True)  117 us
    dot_general x8, matrix products, one_block(): jnp.einsum('td,vd->tv', row_block, head, preferred_element_type=jnp.float32)  42.4 us
    all_to_all x3, starting transfers between devices, exchange(): lax.all_to_all(blocks, 'exp', split_axis=0, concat_axis=0, tiled=True)  25.4 us
    all_gather x1, waiting for transfers between devices, per_device(): gathered_second = lax.all_gather(final_second, 'exp', axis=0, tiled=True)  21.2 us
    all_to_all x1, blocking collectives, per_device(): lax.all_to_all(dense_totals.reshape(devices, per_device_seqs), ('req', 'e...  15 us
    reduce_sum x8, other arithmetic, one_block(): masses = jnp.sum(jnp.exp(logits - highest[:, None]), axis=1)  14 us
    all_to_all x1, blocking collectives, per_device(): gathered = lax.all_to_all(stacked, 'exp', 0, 0, tiled=True)  12.7 us
    all_gather x1, waiting for transfers between devices, per_device(): gathered_first = lax.all_gather(final_first, 'exp', axis=0, tiled=True)  10.8 us
  transfers between devices with their start and end apart: 5, of which 5 were waited for; matrix products, arithmetic and copies ran while one was open for 17% of the time, Pallas kernels for 0%

profile of v6, /device:TPU:1, one launch (start us, length us, event | category | flops | bytes accessed | tf_op | source)
XLA Modules:
  0.0 345.8 jit_solution(383004494774133216)
XLA Ops:
  9.2 3.1 fusion.22
  15.6 2.2 multiply_reduce_fusion.5
  18.0 5.0 %fusion.29 = bf16[1280,1024]{1,0:T(8,128)(2,1)} fusion(s32[1024]{0:T(1024)S(1)} %multiply_add_fusion.3, bf16[128,1024]{1,0:T(8,128)(2,1)S(1)} %multiply_convert_fusion.3), kind=kOutput, calls=%fused_computation.45 | convolution fusion | flops 2686976000 | bytes 2887680 | tf_op jit(solution)/shard_map/ps,pd->sd/dot_general | solution.py:161
  22.9 9.6 %all-to-all-start = ((bf16[32,40,1024]{2,1,0:T(8,128)(2,1)}), bf16[32,40,1024]{2,1,0:T(8,128)(2,1)}, u32[]{:S(2)}, u32[]{:S(2)}) async-start(bf16[32,40,1024]{2,1,0:T(8,128)(2,1)} %bitcast.26), calls=%async_computation | async-start | bytes 5242880 | tf_op jit(solution)/shard_map/all_to_all | solution.py:190
  32.7 3.0 fusion.20
  38.8 2.2 multiply_reduce_fusion.4
  41.1 4.9 %fusion.28 = bf16[1280,1024]{1,0:T(8,128)(2,1)} fusion(s32[1024]{0:T(1024)S(1)} %multiply_add_fusion.2, bf16[128,1024]{1,0:T(8,128)(2,1)S(1)} %multiply_convert_fusion.2), kind=kOutput, calls=%fused_computation.44 | convolution fusion | flops 2686976000 | bytes 2887680 | tf_op jit(solution)/shard_map/ps,pd->sd/dot_general | solution.py:161
  46.0 20.5 %all-to-all-done = bf16[32,40,1024]{2,1,0:T(8,128)(2,1)} async-done(((bf16[32,40,1024]{2,1,0:T(8,128)(2,1)}), bf16[32,40,1024]{2,1,0:T(8,128)(2,1)}, u32[]{:S(2)}, u32[]{:S(2)}) %all-to-all-start) | async-done | bytes 2621472 | tf_op jit(solution)/shard_map/all_to_all | solution.py:190
  66.5 5.3 %convolution_bitcast_fusion = f32[32,1,40,1024]{3,2,0,1:T(8,128)S(1)} fusion(bf16[32,40,1024]{2,1,0:T(8,128)(2,1)} %all-to-all-done, bf16[2,1,1024,1024]{3,2,1,0:T(8,128)(2,1)} %param.25), kind=kOutput, calls=%fused_computation.57 | convolution fusion | flops 2684354560 | bytes 9961472 | tf_op jit(solution)/shard_map/slcd,ldf->slcf/dot_general | solution.py:168
  73.6 2.9 pad_maximum_fusion
  76.5 7.1 %all-to-all-start.1 = ((bf16[32,80,1024]{2,1,0:T(8,128)(2,1)}), bf16[32,80,1024]{2,1,0:T(8,128)(2,1)}, u32[]{:S(2)}, u32[]{:S(2)}) async-start(bf16[32,80,1024]{2,1,0:T(8,128)(2,1)} %pad_maximum_fusion), calls=%async_computation.1 | async-start | bytes 10485760 | tf_op jit(solution)/shard_map/all_to_all | solution.py:190
  84.0 61.5 %all-to-all-done.1 = bf16[32,80,1024]{2,1,0:T(8,128)(2,1)} async-done(((bf16[32,80,1024]{2,1,0:T(8,128)(2,1)}), bf16[32,80,1024]{2,1,0:T(8,128)(2,1)}, u32[]{:S(2)}, u32[]{:S(2)}) %all-to-all-start.1) | async-done | bytes 5242912 | tf_op jit(solution)/shard_map/all_to_all | solution.py:190
  147.4 3.3 multiply_reduce_fusion.1
  151.8 5.3 %fusion.38 = f32[32,1,40,1024]{3,2,0,1:T(8,128)S(1)} fusion(bf16[32,80,1024]{2,1,0:T(8,128)(2,1)} %all-to-all-done.1, bf16[2,1,1024,1024]{3,2,1,0:T(8,128)(2,1)} %param.25), kind=kOutput, calls=%fused_computation.56 | convolution fusion | flops 2684354560 | bytes 9961472 | tf_op jit(solution)/shard_map/slcd,ldf->slcf/dot_general | solution.py:168
  157.1 3.3 convolution_convert_fusion
  160.4 8.8 %all-to-all-start.2 = ((bf16[32,40,1024]{2,1,0:T(8,128)(2,1)}), bf16[32,40,1024]{2,1,0:T(8,128)(2,1)}, u32[]{:S(2)}, u32[]{:S(2)}) async-start(bf16[32,40,1024]{2,1,0:T(8,128)(2,1)} %convolution_convert_fusion), calls=%async_computation.2 | async-start | bytes 5242880 | tf_op jit(solution)/shard_map/all_to_all | solution.py:190
  169.7 35.0 %all-to-all-done.2 = bf16[32,40,1024]{2,1,0:T(8,128)(2,1)} async-done(((bf16[32,40,1024]{2,1,0:T(8,128)(2,1)}), bf16[32,40,1024]{2,1,0:T(8,128)(2,1)}, u32[]{:S(2)}, u32[]{:S(2)}) %all-to-all-start.2) | async-done | bytes 2621472 | tf_op jit(solution)/shard_map/all_to_all | solution.py:190
  204.7 5.1 %multiply_reduce_fusion = f32[128,1024]{1,0:T(8,128)S(1)} fusion(f32[128,8]{0,1:T(8,128)S(1)} %get-tuple-element.157, bf16[1280,1024,1]{1,0,2:T(8,128)(2,1)} %bitcast.75, s32[128,8]{0,1:T(8,128)S(1)} %copy.100), kind=kOutput, calls=%fused_computation.37 | convolution fusion | flops 2687631360 | bytes 3153920 | tf_op jit(solution)/shard_map/tks,sd->tkd/dot_general | solution.py:182
  210.8 10.8 %all-gather.3.cloned.1.call-done = bf16[4096,1024]{1,0:T(8,128)(2,1)} async-done(((bf16[128,1024]{1,0:T(8,128)(2,1)}), bf16[4096,1024]{1,0:T(8,128)(2,1)}) %all-gather.3.cloned.1.call-update) | async-done | bytes 8388624 | tf_op jit(solution)/shard_map/all_gather | solution.py:217
  221.6 33.6 %while.22 = (s32[]{:T(128)}, f32[4,3,1024]{2,1,0:T(4,128)S(1)}, s32[4]{0:T(128)S(1)}, bf16[4096,1024]{1,0:T(8,128)(2,1)}, bf16[2,1152,1024]{2,1,0:T(8,128)(2,1)}...) while((s32[]{:T(128)}, f32[4,3,1024]{2,1,0:T(4,128)S(1)}, ...), condition=%wide.region_19.20_spmd.clone, body=%wide.region_15.19_spmd.clone.sunk | while | flops 2424179712 | bytes 13951155 | solution.py:208
  222.9 5.3 %fusion.207 = (f32[1024]{0:T(1024)S(1)}, f32[1024,1152]{1,0:T(8,128)S(1)}) fusion(bf16[2,1152,1024]{2,1,0:T(8,128)(2,1)} %get-tuple-element.310, bf16[4096,1024]{1,0:T(8,128)(2,1)} %get-tuple-element.309, s32[]{:T(128)S(6)} %select_n.42), kind=kOutput, calls=%fused_computation.226.clone.1 | convolution fusion | flops 2418277376 | bytes 9179140 | tf_op jit(solution)/shard_map/while/body/eval_jaxpr/td,vd->tv/dot_general | solution.py:200
  231.3 5.4 %fusion.207 = (f32[1024]{0:T(1024)S(1)}, f32[1024,1152]{1,0:T(8,128)S(1)}) fusion(bf16[2,1152,1024]{2,1,0:T(8,128)(2,1)} %get-tuple-element.310, bf16[4096,1024]{1,0:T(8,128)(2,1)} %get-tuple-element.309, s32[]{:T(128)S(6)} %select_n.42), kind=kOutput, calls=%fused_computation.226.clone.1 | convolution fusion | flops 2418277376 | bytes 9179140 | tf_op jit(solution)/shard_map/while/body/eval_jaxpr/td,vd->tv/dot_general | solution.py:200
  239.8 5.3 %fusion.207 = (f32[1024]{0:T(1024)S(1)}, f32[1024,1152]{1,0:T(8,128)S(1)}) fusion(bf16[2,1152,1024]{2,1,0:T(8,128)(2,1)} %get-tuple-element.310, bf16[4096,1024]{1,0:T(8,128)(2,1)} %get-tuple-element.309, s32[]{:T(128)S(6)} %select_n.42), kind=kOutput, calls=%fused_computation.226.clone.1 | convolution fusion | flops 2418277376 | bytes 9179140 | tf_op jit(solution)/shard_map/while/body/eval_jaxpr/td,vd->tv/dot_general | solution.py:200
  248.1 5.3 %fusion.207 = (f32[1024]{0:T(1024)S(1)}, f32[1024,1152]{1,0:T(8,128)S(1)}) fusion(bf16[2,1152,1024]{2,1,0:T(8,128)(2,1)} %get-tuple-element.310, bf16[4096,1024]{1,0:T(8,128)(2,1)} %get-tuple-element.309, s32[]{:T(128)S(6)} %select_n.42), kind=kOutput, calls=%fused_computation.226.clone.1 | convolution fusion | flops 2418277376 | bytes 9179140 | tf_op jit(solution)/shard_map/while/body/eval_jaxpr/td,vd->tv/dot_general | solution.py:200
  255.3 21.2 %all-gather.5.cloned.1.call-done = bf16[4096,1024]{1,0:T(8,128)(2,1)} async-done(((bf16[128,1024]{1,0:T(8,128)(2,1)}), bf16[4096,1024]{1,0:T(8,128)(2,1)}) %all-gather.5.cloned.1.call-update) | async-done | bytes 8388624 | tf_op jit(solution)/shard_map/all_gather | solution.py:220
  276.5 33.4 %while.23 = (s32[]{:T(128)}, f32[4,3,1024]{2,1,0:T(4,128)S(1)}, s32[4]{0:T(128)S(1)}, bf16[4096,1024]{1,0:T(8,128)(2,1)}, bf16[2,1152,1024]{2,1,0:T(8,128)(2,1)}...) while((s32[]{:T(128)}, f32[4,3,1024]{2,1,0:T(4,128)S(1)}, ...), condition=%wide.region_26.27_spmd.clone, body=%wide.region_22.26_spmd.clone.sunk | while | flops 2424179712 | bytes 13951155 | solution.py:208
  277.8 5.3 %fusion.209 = (f32[1024]{0:T(1024)S(1)}, f32[1024,1152]{1,0:T(8,128)S(1)}) fusion(bf16[2,1152,1024]{2,1,0:T(8,128)(2,1)} %get-tuple-element.280, bf16[4096,1024]{1,0:T(8,128)(2,1)} %get-tuple-element.279, s32[]{:T(128)S(6)} %select_n.43), kind=kOutput, calls=%fused_computation.227.clone.1 | convolution fusion | flops 2418277376 | bytes 9179140 | tf_op jit(solution)/shard_map/while/body/eval_jaxpr/td,vd->tv/dot_general | solution.py:200
  286.1 5.3 %fusion.209 = (f32[1024]{0:T(1024)S(1)}, f32[1024,1152]{1,0:T(8,128)S(1)}) fusion(bf16[2,1152,1024]{2,1,0:T(8,128)(2,1)} %get-tuple-element.280, bf16[4096,1024]{1,0:T(8,128)(2,1)} %get-tuple-element.279, s32[]{:T(128)S(6)} %select_n.43), kind=kOutput, calls=%fused_computation.227.clone.1 | convolution fusion | flops 2418277376 | bytes 9179140 | tf_op jit(solution)/shard_map/while/body/eval_jaxpr/td,vd->tv/dot_general | solution.py:200
  294.5 5.3 %fusion.209 = (f32[1024]{0:T(1024)S(1)}, f32[1024,1152]{1,0:T(8,128)S(1)}) fusion(bf16[2,1152,1024]{2,1,0:T(8,128)(2,1)} %get-tuple-element.280, bf16[4096,1024]{1,0:T(8,128)(2,1)} %get-tuple-element.279, s32[]{:T(128)S(6)} %select_n.43), kind=kOutput, calls=%fused_computation.227.clone.1 | convolution fusion | flops 2418277376 | bytes 9179140 | tf_op jit(solution)/shard_map/while/body/eval_jaxpr/td,vd->tv/dot_general | solution.py:200
  302.8 5.3 %fusion.209 = (f32[1024]{0:T(1024)S(1)}, f32[1024,1152]{1,0:T(8,128)S(1)}) fusion(bf16[2,1152,1024]{2,1,0:T(8,128)(2,1)} %get-tuple-element.280, bf16[4096,1024]{1,0:T(8,128)(2,1)} %get-tuple-element.279, s32[]{:T(128)S(6)} %select_n.43), kind=kOutput, calls=%fused_computation.227.clone.1 | convolution fusion | flops 2418277376 | bytes 9179140 | tf_op jit(solution)/shard_map/while/body/eval_jaxpr/td,vd->tv/dot_general | solution.py:200
  310.1 12.7 %all_to_all.29 = f32[32,3,2,128]{3,2,1,0:T(2,128)S(1)} all-to-all(f32[32,3,2,128]{3,2,1,0:T(2,128)S(1)} %copy.102), channel_id=1, replica_groups=mesh['req'=4,'exp'=32] {'exp'}, dimensions={0} | all-to-all | bytes 196608 | tf_op jit(solution)/shard_map/all_to_all | solution.py:224
  323.3 15.0 %all_to_all.30 = f32[128,1,4]{2,1,0:T(1,128)S(1)} all-to-all(f32[128,1,4]{2,1,0:T(1,128)S(1)} %bitcast.303), channel_id=1, replica_groups=mesh['req'=4,'exp'=32] {'req','exp'}, dimensions={0} | all-to-all | bytes 4096 | tf_op jit(solution)/shard_map/all_to_all | solution.py:242
  (142 shorter events, 35.8 us)
Async XLA Ops:
  8.4 4.0 %copy-start.10 = (s32[1,4]{1,0:T(1,128)S(1)}, s32[1,4]{1,0:T(1,128)}, u32[]{:S(2)}) copy-start(s32[1,4]{1,0:T(1,128)} %param.17) | copy-start | bytes 52
  13.2 1.1 copy-start.5
  14.0 1.7 copy-start.1
  22.9 9.8 %copy-start.2 = (bf16[2,128,1024]{2,1,0:T(8,128)(2,1)S(1)}, bf16[2,128,1024]{2,1,0:T(8,128)(2,1)}, u32[]{:S(2)}) copy-start(bf16[2,128,1024]{2,1,0:T(8,128)(2,1)} %param.16) | copy-start | bytes 1572868
  22.9 43.6 %all-to-all-start = ((bf16[32,40,1024]{2,1,0:T(8,128)(2,1)}), bf16[32,40,1024]{2,1,0:T(8,128)(2,1)}, u32[]{:S(2)}, u32[]{:S(2)}) async-start(bf16[32,40,1024]{2,1,0:T(8,128)(2,1)} %bitcast.26), calls=%async_computation | async-start | bytes 5242880 | tf_op jit(solution)/shard_map/all_to_all | solution.py:190
  37.8 1.0 copy-start.3
  46.0 25.8 %copy-start.9 = (bf16[2,1,512,1024]{3,2,1,0:T(8,128)(2,1)S(1)}, bf16[2,1,512,1024]{3,2,1,0:T(8,128)(2,1)}, u32[]{:S(2)}) copy-start(bf16[2,1,512,1024]{3,2,1,0:T(8,128)(2,1)} %param.26) | copy-start | bytes 6291460
  71.8 1.7 copy-start
  76.5 7.5 %copy-start.6 = (f32[2,128,8]{1,2,0:T(8,128)S(1)}, f32[2,128,8]{1,2,0:T(8,128)}, u32[]{:S(2)}) copy-start(f32[2,128,8]{1,2,0:T(8,128)} %param.20) | copy-start | bytes 24580
  76.5 69.0 %all-to-all-start.1 = ((bf16[32,80,1024]{2,1,0:T(8,128)(2,1)}), bf16[32,80,1024]{2,1,0:T(8,128)(2,1)}, u32[]{:S(2)}, u32[]{:S(2)}) async-start(bf16[32,80,1024]{2,1,0:T(8,128)(2,1)} %pad_maximum_fusion), calls=%async_computation.1 | async-start | bytes 10485760 | tf_op jit(solution)/shard_map/all_to_all | solution.py:190
  83.5 138.0 %all-gather.3.cloned.1.call-start = ((), (), s32[]{:S(2)}) async-start(), calls=%async_computation.5 | async-start | bytes 8650752 | tf_op jit(solution)/shard_map/all_gather | solution.py:217
  160.4 44.3 %all-to-all-start.2 = ((bf16[32,40,1024]{2,1,0:T(8,128)(2,1)}), bf16[32,40,1024]{2,1,0:T(8,128)(2,1)}, u32[]{:S(2)}, u32[]{:S(2)}) async-start(bf16[32,40,1024]{2,1,0:T(8,128)(2,1)} %convolution_convert_fusion), calls=%async_computation.2 | async-start | bytes 5242880 | tf_op jit(solution)/shard_map/all_to_all | solution.py:190
  169.2 107.3 %all-gather.5.cloned.1.call-start = ((), (), s32[]{:S(2)}) async-start(), calls=%async_computation.6 | async-start | bytes 8650752 | tf_op jit(solution)/shard_map/all_gather | solution.py:220
  204.7 6.1 %copy-start.4 = (s32[4096]{0:T(1024)S(1)}, s32[4096]{0:T(1024)}, u32[]{:S(2)}) copy-start(s32[4096]{0:T(1024)} %param.18) | copy-start | bytes 49156
  276.5 46.5 %copy-start.8 = (s32[4]{0:T(128)S(1)}, s32[4]{0:T(128)}, u32[]{:S(2)}) copy-start(s32[4]{0:T(128)} %param.21) | copy-start | bytes 52
  322.9 16.0 %copy-start.7 = (f32[2,128]{1,0:T(2,128)}, f32[2,128]{1,0:T(2,128)S(1)}, u32[]{:S(2)}) copy-start(f32[2,128]{1,0:T(2,128)S(1)} %add_subtract_fusion) | copy-start | bytes 3076
Sparse Core Ops, SparseCore 0:
  151.9 69.6 all-gather.2
  223.8 52.5 all-gather.4

commit v7 on v6

--- a/solution.py
+++ b/solution.py
@@ -137,7 +137,7 @@
     lowest = shard * vocab_rows
     vocab_ids = jnp.arange(vocab_rows, dtype=jnp.int32)
     wanted_all = targets - lowest
-    block_rows = 1024
+    block_rows = 2048
 
     def model_entry(which):
         residual = attend(

time: 347 us -> 336 us (0.968)
  matrix products: 90.3 us -> 78.7 us
  waiting for transfers between devices: 149 us -> 159 us
  other arithmetic: 22.4 us -> 18.6 us
    dot_general x8 -> x4, matrix products: 42.4 us -> 30.8 us  [one_block(): jnp.einsum('td,vd->tv', row_block, head, preferred_element_type=jnp.float32)]
    all_gather x1, waiting for transfers between devices: 21.2 us -> 31.5 us  [per_device(): gathered_second = lax.all_gather(final_second, 'exp', axis=0, tiled=True)]
    reduce_sum x8 -> x4, other arithmetic: 14 us -> 10.3 us  [one_block(): masses = jnp.sum(jnp.exp(logits - highest[:, None]), axis=1)]
  transfers between devices with their start and end apart: 5 -> 5, of which waited for: 5 -> 5; matrix products, arithmetic and copies ran while one was open for 17% -> 15% of each run, Pallas kernels for 0% -> 0%
where the time goes in v7:
time: 336 us
  waiting for transfers between devices  159 us (47%)
  matrix products  78.7 us (23%)
  blocking collectives  27.7 us (8%)
  starting transfers between devices  26 us (8%)
  other arithmetic  18.6 us (6%)
  between operations  14.6 us (4%)
  local copies, waits for them, and re-layouts  7.95 us (2%)
    all_to_all x3, waiting for transfers between devices, exchange(): lax.all_to_all(blocks, 'exp', split_axis=0, concat_axis=0, tiled=True)  117 us
    all_gather x1, waiting for transfers between devices, per_device(): gathered_second = lax.all_gather(final_second, 'exp', axis=0, tiled=True)  31.5 us
    dot_general x4, matrix products, one_block(): jnp.einsum('td,vd->tv', row_block, head, preferred_element_type=jnp.float32)  30.8 us
    all_to_all x3, starting transfers between devices, exchange(): lax.all_to_all(blocks, 'exp', split_axis=0, concat_axis=0, tiled=True)  25.5 us
    all_to_all x1, blocking collectives, per_device(): lax.all_to_all(dense_totals.reshape(devices, per_device_seqs), ('req', 'e...  15 us
    all_to_all x1, blocking collectives, per_device(): gathered = lax.all_to_all(stacked, 'exp', 0, 0, tiled=True)  12.7 us
    all_gather x1, waiting for transfers between devices, per_device(): gathered_first = lax.all_gather(final_first, 'exp', axis=0, tiled=True)  10.8 us
    dot_general x2, matrix products, model_experts(): jnp.einsum('slcd,ldf->slcf', inputs, expert_in[which], preferred_element_...  10.6 us
  transfers between devices with their start and end apart: 5, of which 5 were waited for; matrix products, arithmetic and copies ran while one was open for 15% of the time, Pallas kernels for 0%

profile of v7, /device:TPU:1, one launch (start us, length us, event | category | flops | bytes accessed | tf_op | source)
XLA Modules:
  0.0 335.7 jit_solution(15891183799665960970)
XLA Ops:
  9.2 3.1 fusion.22
  15.6 2.2 multiply_reduce_fusion.5
  18.0 5.0 %fusion.29 = bf16[1280,1024]{1,0:T(8,128)(2,1)} fusion(s32[1024]{0:T(1024)S(1)} %multiply_add_fusion.3, bf16[128,1024]{1,0:T(8,128)(2,1)S(1)} %multiply_convert_fusion.3), kind=kOutput, calls=%fused_computation.45 | convolution fusion | flops 2686976000 | bytes 2887680 | tf_op jit(solution)/shard_map/ps,pd->sd/dot_general | solution.py:161
  22.9 9.6 %all-to-all-start = ((bf16[32,40,1024]{2,1,0:T(8,128)(2,1)}), bf16[32,40,1024]{2,1,0:T(8,128)(2,1)}, u32[]{:S(2)}, u32[]{:S(2)}) async-start(bf16[32,40,1024]{2,1,0:T(8,128)(2,1)} %bitcast.26), calls=%async_computation | async-start | bytes 5242880 | tf_op jit(solution)/shard_map/all_to_all | solution.py:190
  32.7 3.0 fusion.20
  38.8 2.2 multiply_reduce_fusion.4
  41.2 4.8 %fusion.28 = bf16[1280,1024]{1,0:T(8,128)(2,1)} fusion(s32[1024]{0:T(1024)S(1)} %multiply_add_fusion.2, bf16[128,1024]{1,0:T(8,128)(2,1)S(1)} %multiply_convert_fusion.2), kind=kOutput, calls=%fused_computation.44 | convolution fusion | flops 2686976000 | bytes 2887680 | tf_op jit(solution)/shard_map/ps,pd->sd/dot_general | solution.py:161
  46.0 20.5 %all-to-all-done = bf16[32,40,1024]{2,1,0:T(8,128)(2,1)} async-done(((bf16[32,40,1024]{2,1,0:T(8,128)(2,1)}), bf16[32,40,1024]{2,1,0:T(8,128)(2,1)}, u32[]{:S(2)}, u32[]{:S(2)}) %all-to-all-start) | async-done | bytes 2621472 | tf_op jit(solution)/shard_map/all_to_all | solution.py:190
  66.5 5.3 %convolution_bitcast_fusion = f32[32,1,40,1024]{3,2,0,1:T(8,128)S(1)} fusion(bf16[32,40,1024]{2,1,0:T(8,128)(2,1)} %all-to-all-done, bf16[2,1,1024,1024]{3,2,1,0:T(8,128)(2,1)} %param.25), kind=kOutput, calls=%fused_computation.57 | convolution fusion | flops 2684354560 | bytes 9961472 | tf_op jit(solution)/shard_map/slcd,ldf->slcf/dot_general | solution.py:168
  73.6 2.9 pad_maximum_fusion
  76.5 7.1 %all-to-all-start.1 = ((bf16[32,80,1024]{2,1,0:T(8,128)(2,1)}), bf16[32,80,1024]{2,1,0:T(8,128)(2,1)}, u32[]{:S(2)}, u32[]{:S(2)}) async-start(bf16[32,80,1024]{2,1,0:T(8,128)(2,1)} %pad_maximum_fusion), calls=%async_computation.1 | async-start | bytes 10485760 | tf_op jit(solution)/shard_map/all_to_all | solution.py:190
  84.0 61.5 %all-to-all-done.1 = bf16[32,80,1024]{2,1,0:T(8,128)(2,1)} async-done(((bf16[32,80,1024]{2,1,0:T(8,128)(2,1)}), bf16[32,80,1024]{2,1,0:T(8,128)(2,1)}, u32[]{:S(2)}, u32[]{:S(2)}) %all-to-all-start.1) | async-done | bytes 5242912 | tf_op jit(solution)/shard_map/all_to_all | solution.py:190
  147.5 3.3 multiply_reduce_fusion.1
  151.8 5.3 %fusion.38 = f32[32,1,40,1024]{3,2,0,1:T(8,128)S(1)} fusion(bf16[32,80,1024]{2,1,0:T(8,128)(2,1)} %all-to-all-done.1, bf16[2,1,1024,1024]{3,2,1,0:T(8,128)(2,1)} %param.25), kind=kOutput, calls=%fused_computation.56 | convolution fusion | flops 2684354560 | bytes 9961472 | tf_op jit(solution)/shard_map/slcd,ldf->slcf/dot_general | solution.py:168
  157.1 3.3 convolution_convert_fusion
  160.5 8.8 %all-to-all-start.2 = ((bf16[32,40,1024]{2,1,0:T(8,128)(2,1)}), bf16[32,40,1024]{2,1,0:T(8,128)(2,1)}, u32[]{:S(2)}, u32[]{:S(2)}) async-start(bf16[32,40,1024]{2,1,0:T(8,128)(2,1)} %convolution_convert_fusion), calls=%async_computation.2 | async-start | bytes 5242880 | tf_op jit(solution)/shard_map/all_to_all | solution.py:190
  169.7 35.0 %all-to-all-done.2 = bf16[32,40,1024]{2,1,0:T(8,128)(2,1)} async-done(((bf16[32,40,1024]{2,1,0:T(8,128)(2,1)}), bf16[32,40,1024]{2,1,0:T(8,128)(2,1)}, u32[]{:S(2)}, u32[]{:S(2)}) %all-to-all-start.2) | async-done | bytes 2621472 | tf_op jit(solution)/shard_map/all_to_all | solution.py:190
  204.7 5.1 %multiply_reduce_fusion = f32[128,1024]{1,0:T(8,128)S(1)} fusion(f32[128,8]{0,1:T(8,128)S(1)} %get-tuple-element.157, bf16[1280,1024,1]{1,0,2:T(8,128)(2,1)} %bitcast.75, s32[128,8]{0,1:T(8,128)S(1)} %copy.100), kind=kOutput, calls=%fused_computation.37 | convolution fusion | flops 2687631360 | bytes 3153920 | tf_op jit(solution)/shard_map/tks,sd->tkd/dot_general | solution.py:182
  210.9 10.8 %all-gather.3.cloned.1.call-done = bf16[4096,1024]{1,0:T(8,128)(2,1)} async-done(((bf16[128,1024]{1,0:T(8,128)(2,1)}), bf16[4096,1024]{1,0:T(8,128)(2,1)}) %all-gather.3.cloned.1.call-update) | async-done | bytes 8388624 | tf_op jit(solution)/shard_map/all_gather | solution.py:217
  221.7 23.3 %while.22 = (s32[]{:T(128)}, f32[2,3,2048]{2,1,0:T(4,128)S(1)}, s32[2]{0:T(128)S(1)}, bf16[4096,1024]{1,0:T(8,128)(2,1)}, bf16[2,1152,1024]{2,1,0:T(8,128)(2,1)}...) while((s32[]{:T(128)}, f32[2,3,2048]{2,1,0:T(4,128)S(1)}, ...), condition=%wide.region_19.20_spmd.clone, body=%wide.region_15.19_spmd.clone.sunk | while | flops 4848359424 | bytes 25542836 | solution.py:208
  222.9 7.7 %fusion.207 = (f32[2048]{0:T(1024)S(1)}, f32[2048,1152]{0,1:T(8,128)S(1)}) fusion(bf16[2,1152,1024]{2,1,0:T(8,128)(2,1)} %get-tuple-element.310, bf16[4096,1024]{1,0:T(8,128)(2,1)} %get-tuple-element.309, s32[]{:T(128)S(6)} %select_n.42), kind=kOutput, calls=%fused_computation.226.clone.1 | convolution fusion | flops 4836554752 | bytes 15998980 | tf_op jit(solution)/shard_map/while/body/eval_jaxpr/td,vd->tv/dot_general | solution.py:200
  230.7 2.6 exponential_reduce_fusion.4
  234.6 7.7 %fusion.207 = (f32[2048]{0:T(1024)S(1)}, f32[2048,1152]{0,1:T(8,128)S(1)}) fusion(bf16[2,1152,1024]{2,1,0:T(8,128)(2,1)} %get-tuple-element.310, bf16[4096,1024]{1,0:T(8,128)(2,1)} %get-tuple-element.309, s32[]{:T(128)S(6)} %select_n.42), kind=kOutput, calls=%fused_computation.226.clone.1 | convolution fusion | flops 4836554752 | bytes 15998980 | tf_op jit(solution)/shard_map/while/body/eval_jaxpr/td,vd->tv/dot_general | solution.py:200
  242.3 2.6 exponential_reduce_fusion.4
  245.0 31.5 %all-gather.5.cloned.1.call-done = bf16[4096,1024]{1,0:T(8,128)(2,1)} async-done(((bf16[128,1024]{1,0:T(8,128)(2,1)}), bf16[4096,1024]{1,0:T(8,128)(2,1)}) %all-gather.5.cloned.1.call-update) | async-done | bytes 8388624 | tf_op jit(solution)/shard_map/all_gather | solution.py:220
  276.6 23.2 %while.23 = (s32[]{:T(128)}, f32[2,3,2048]{2,1,0:T(4,128)S(1)}, s32[2]{0:T(128)S(1)}, bf16[4096,1024]{1,0:T(8,128)(2,1)}, bf16[2,1152,1024]{2,1,0:T(8,128)(2,1)}...) while((s32[]{:T(128)}, f32[2,3,2048]{2,1,0:T(4,128)S(1)}, ...), condition=%wide.region_26.27_spmd.clone, body=%wide.region_22.26_spmd.clone.sunk | while | flops 4848359424 | bytes 25542836 | solution.py:208
  277.8 7.7 %fusion.209 = (f32[2048]{0:T(1024)S(1)}, f32[2048,1152]{0,1:T(8,128)S(1)}) fusion(bf16[2,1152,1024]{2,1,0:T(8,128)(2,1)} %get-tuple-element.280, bf16[4096,1024]{1,0:T(8,128)(2,1)} %get-tuple-element.279, s32[]{:T(128)S(6)} %select_n.43), kind=kOutput, calls=%fused_computation.227.clone.1 | convolution fusion | flops 4836554752 | bytes 15998980 | tf_op jit(solution)/shard_map/while/body/eval_jaxpr/td,vd->tv/dot_general | solution.py:200
  285.5 2.6 exponential_reduce_fusion.5
  289.5 7.7 %fusion.209 = (f32[2048]{0:T(1024)S(1)}, f32[2048,1152]{0,1:T(8,128)S(1)}) fusion(bf16[2,1152,1024]{2,1,0:T(8,128)(2,1)} %get-tuple-element.280, bf16[4096,1024]{1,0:T(8,128)(2,1)} %get-tuple-element.279, s32[]{:T(128)S(6)} %select_n.43), kind=kOutput, calls=%fused_computation.227.clone.1 | convolution fusion | flops 4836554752 | bytes 15998980 | tf_op jit(solution)/shard_map/while/body/eval_jaxpr/td,vd->tv/dot_general | solution.py:200
  297.2 2.6 exponential_reduce_fusion.5
  300.0 12.7 %all_to_all.29 = f32[32,3,2,128]{3,2,1,0:T(2,128)S(1)} all-to-all(f32[32,3,2,128]{3,2,1,0:T(2,128)S(1)} %copy.102), channel_id=1, replica_groups=mesh['req'=4,'exp'=32] {'exp'}, dimensions={0} | all-to-all | bytes 196608 | tf_op jit(solution)/shard_map/all_to_all | solution.py:224
  313.2 15.0 %all_to_all.30 = f32[128,1,4]{2,1,0:T(1,128)S(1)} all-to-all(f32[128,1,4]{2,1,0:T(1,128)S(1)} %bitcast.303), channel_id=1, replica_groups=mesh['req'=4,'exp'=32] {'req','exp'}, dimensions={0} | all-to-all | bytes 4096 | tf_op jit(solution)/shard_map/all_to_all | solution.py:242
  (126 shorter events, 19.3 us)
Async XLA Ops:
  8.4 4.0 %copy-start.12 = (s32[1,4]{1,0:T(1,128)S(1)}, s32[1,4]{1,0:T(1,128)}, u32[]{:S(2)}) copy-start(s32[1,4]{1,0:T(1,128)} %param.17) | copy-start | bytes 52
  12.7 1.3 copy-start.7
  13.2 1.1 copy-start.5
  14.0 1.7 copy-start.1
  22.9 9.8 %copy-start.2 = (bf16[2,128,1024]{2,1,0:T(8,128)(2,1)S(1)}, bf16[2,128,1024]{2,1,0:T(8,128)(2,1)}, u32[]{:S(2)}) copy-start(bf16[2,128,1024]{2,1,0:T(8,128)(2,1)} %param.16) | copy-start | bytes 1572868
  22.9 43.6 %all-to-all-start = ((bf16[32,40,1024]{2,1,0:T(8,128)(2,1)}), bf16[32,40,1024]{2,1,0:T(8,128)(2,1)}, u32[]{:S(2)}, u32[]{:S(2)}) async-start(bf16[32,40,1024]{2,1,0:T(8,128)(2,1)} %bitcast.26), calls=%async_computation | async-start | bytes 5242880 | tf_op jit(solution)/shard_map/all_to_all | solution.py:190
  37.8 1.0 copy-start.3
  46.0 25.9 %copy-start.11 = (bf16[2,1,512,1024]{3,2,1,0:T(8,128)(2,1)S(1)}, bf16[2,1,512,1024]{3,2,1,0:T(8,128)(2,1)}, u32[]{:S(2)}) copy-start(bf16[2,1,512,1024]{3,2,1,0:T(8,128)(2,1)} %param.26) | copy-start | bytes 6291460
  71.9 1.7 copy-start
  76.5 7.5 %copy-start.6 = (f32[2,128,8]{1,2,0:T(8,128)S(1)}, f32[2,128,8]{1,2,0:T(8,128)}, u32[]{:S(2)}) copy-start(f32[2,128,8]{1,2,0:T(8,128)} %param.20) | copy-start | bytes 24580
  76.5 69.0 %all-to-all-start.1 = ((bf16[32,80,1024]{2,1,0:T(8,128)(2,1)}), bf16[32,80,1024]{2,1,0:T(8,128)(2,1)}, u32[]{:S(2)}, u32[]{:S(2)}) async-start(bf16[32,80,1024]{2,1,0:T(8,128)(2,1)} %pad_maximum_fusion), calls=%async_computation.1 | async-start | bytes 10485760 | tf_op jit(solution)/shard_map/all_to_all | solution.py:190
  83.6 138.0 %all-gather.3.cloned.1.call-start = ((), (), s32[]{:S(2)}) async-start(), calls=%async_computation.5 | async-start | bytes 8650752 | tf_op jit(solution)/shard_map/all_gather | solution.py:217
  160.5 44.3 %all-to-all-start.2 = ((bf16[32,40,1024]{2,1,0:T(8,128)(2,1)}), bf16[32,40,1024]{2,1,0:T(8,128)(2,1)}, u32[]{:S(2)}, u32[]{:S(2)}) async-start(bf16[32,40,1024]{2,1,0:T(8,128)(2,1)} %convolution_convert_fusion), calls=%async_computation.2 | async-start | bytes 5242880 | tf_op jit(solution)/shard_map/all_to_all | solution.py:190
  169.2 107.3 %all-gather.5.cloned.1.call-start = ((), (), s32[]{:S(2)}) async-start(), calls=%async_computation.6 | async-start | bytes 8650752 | tf_op jit(solution)/shard_map/all_gather | solution.py:220
  204.7 6.1 %copy-start.4 = (s32[4096]{0:T(1024)S(1)}, s32[4096]{0:T(1024)}, u32[]{:S(2)}) copy-start(s32[4096]{0:T(1024)} %param.18) | copy-start | bytes 49156
  276.5 36.3 %copy-start.8 = (s32[128]{0:T(128)S(1)}, s32[128]{0:T(128)}, u32[]{:S(2)}) copy-start(s32[128]{0:T(128)} %copy-done.7) | copy-start | bytes 1540
  276.6 36.4 %copy-start.10 = (s32[4]{0:T(128)S(1)}, s32[4]{0:T(128)}, u32[]{:S(2)}) copy-start(s32[4]{0:T(128)} %param.21) | copy-start | bytes 52
  312.8 16.0 %copy-start.9 = (f32[2,128]{1,0:T(2,128)}, f32[2,128]{1,0:T(2,128)S(1)}, u32[]{:S(2)}) copy-start(f32[2,128]{1,0:T(2,128)S(1)} %add_subtract_fusion) | copy-start | bytes 3076
Sparse Core Ops, SparseCore 0:
  151.9 69.6 all-gather.2
  223.9 52.5 all-gather.4

commit v8 on v6

--- a/solution.py
+++ b/solution.py
@@ -125,18 +125,29 @@
     token_count = states.shape[1]
     width = states.shape[2]
     segment, member, position = segment_table(lengths[0], token_count)
-    groups = lax.axis_size("exp")
+    groups = lax.axis_size("chip") * lax.axis_size("core")
     local_count = expert_in.shape[1]
     pairs = token_count * TOP
     slots = EXPERTS * CAP
     pair_ids = jnp.arange(pairs, dtype=jnp.int32)
     lower = (pair_ids[None, :] <= pair_ids[:, None]).astype(jnp.bfloat16)
     slot_ids = jnp.arange(slots, dtype=jnp.int32)
-    shard = lax.axis_index("exp")
+    chip = lax.axis_index("chip")
+    core = lax.axis_index("core")
+    chips = lax.axis_size("chip")
     vocab_rows = vocab_head.shape[1]
-    lowest = shard * vocab_rows
-    vocab_ids = jnp.arange(vocab_rows, dtype=jnp.int32)
-    wanted_all = targets - lowest
+    own_shard = chip * 2 + core
+    other_shard = chip * 2 + (1 - core)
+    partner_head = lax.ppermute(vocab_head, "core", perm=[(0, 1), (1, 0)])
+    pair_rows = 2 * vocab_rows
+    vocab_ids = jnp.arange(pair_rows, dtype=jnp.int32)
+    mine = jnp.take(targets.reshape(chips, 2, token_count), core, axis=1).reshape(chips * token_count)
+    place_in = mine % vocab_rows
+    wanted_all = jnp.where(
+        mine // vocab_rows == own_shard,
+        place_in,
+        jnp.where(mine // vocab_rows == other_shard, place_in + vocab_rows, -1),
+    )
     block_rows = 1024
 
     def model_entry(which):
@@ -186,14 +197,12 @@
         ).astype(jnp.bfloat16)
         return final
 
-    def exchange(blocks):
-        return lax.all_to_all(blocks, "exp", split_axis=0, concat_axis=0, tiled=True)
-
     def model_stats(which, chunk):
         chunk_rows = chunk.shape[0]
         block_count = chunk_rows // block_rows
+        head = jnp.concatenate([vocab_head[which], partner_head[which]], axis=0)
+
         def one_block(block_number):
-            head = vocab_head[which]
             row_block = lax.dynamic_slice_in_dim(chunk, block_number * block_rows, block_rows, 0)
             wanted = lax.dynamic_slice_in_dim(wanted_all, block_number * block_rows, block_rows, 0)
             logits = (
@@ -206,7 +215,10 @@
             return jnp.stack([highest, masses, chosen])
 
         stats = lax.map(one_block, jnp.arange(block_count, dtype=jnp.int32))
-        return jnp.transpose(stats, (1, 0, 2)).reshape(3, groups, token_count)
+        return jnp.transpose(stats, (1, 0, 2)).reshape(3, chips, token_count)
+
+    def exchange(blocks):
+        return lax.all_to_all(blocks, ("chip", "core"), split_axis=0, concat_axis=0, tiled=True)
 
     row_span = local_count * CAP
     residual_first, slot_first, outgoing_first = model_entry(0)
@@ -214,14 +226,14 @@
     residual_second, slot_second, outgoing_second = model_entry(1)
     crossed = exchange(jnp.concatenate([produced_first, outgoing_second], axis=1))
     final_first = model_exit(0, residual_first, slot_first, crossed[:, :row_span])
-    gathered_first = lax.all_gather(final_first, "exp", axis=0, tiled=True)
+    gathered_first = lax.all_gather(final_first, "chip", axis=0, tiled=True)
     produced_second = model_experts(1, crossed[:, row_span:])
     final_second = model_exit(1, residual_second, slot_second, exchange(produced_second))
-    gathered_second = lax.all_gather(final_second, "exp", axis=0, tiled=True)
+    gathered_second = lax.all_gather(final_second, "chip", axis=0, tiled=True)
     stats_first = model_stats(0, gathered_first)
     stats_second = model_stats(1, gathered_second)
     stacked = jnp.transpose(jnp.stack([stats_first, stats_second]), (2, 1, 0, 3))
-    gathered = lax.all_to_all(stacked, "exp", 0, 0, tiled=True)
+    gathered = lax.all_to_all(stacked, "chip", 0, 0, tiled=True)
     all_max = gathered[:, 0]
     all_mass = gathered[:, 1]
     all_hit = gathered[:, 2]
@@ -231,7 +243,7 @@
     token_logp = final_hit - (final_max + jnp.log(final_mass))
     difference = token_logp[0] - token_logp[1]
     seq_sums = jnp.sum(member.astype(jnp.float32) * difference[:, None], axis=0)
-    devices = lax.axis_size("req") * lax.axis_size("exp")
+    devices = lax.axis_size("req") * groups
     per_device_seqs = seq_sums.shape[0]
     everyone = devices * per_device_seqs
     dense_totals = jnp.sum(
@@ -240,28 +252,35 @@
         axis=0,
     )
     delivered = lax.all_to_all(
-        dense_totals.reshape(devices, per_device_seqs), ("req", "exp"), 0, 0, tiled=True
+        dense_totals.reshape(devices, per_device_seqs), ("req", "chip", "core"), 0, 0, tiled=True
     )
     seq_totals = jnp.sum(delivered, axis=0)
     return (token_logp, seq_totals)
 
 
 def solution(mesh):
+    requests = mesh.shape["req"]
+    spread = mesh.shape["exp"]
+    split_mesh = jax.sharding.Mesh(
+        mesh.devices.reshape(requests, spread // 2, 2), ("req", "chip", "core")
+    )
+    every = ("req", "chip", "core")
+    group = ("chip", "core")
     in_specs = (
-        P(None, ("req", "exp"), None),
-        P(("req", "exp"), None),
+        P(None, every, None),
+        P(every, None),
         P("req"),
-        P(None, ("req", "exp"), None),
-        P(None, ("req", "exp"), None),
-        P(("req", "exp")),
+        P(None, every, None),
+        P(None, every, None),
+        P(every),
         P(),
         P(),
         P(),
-        P(None, "exp", None, None),
-        P(None, "exp", None, None),
-        P(None, "exp", None),
-    )
-    out_specs = (P(None, ("req", "exp")), P(("req", "exp")))
+        P(None, group, None, None),
+        P(None, group, None, None),
+        P(None, group, None),
+    )
+    out_specs = (P(None, every), P(every))
     return jax.shard_map(
-        per_device, mesh=mesh, in_specs=in_specs, out_specs=out_specs, check_vma=False
-    )
+        per_device, mesh=split_mesh, in_specs=in_specs, out_specs=out_specs, check_vma=False
+    )

time: 347 us -> 344 us (level); the launches traced: 346 us -> 338 us
  matrix products: 90.3 us -> 80.5 us
  waiting for transfers between devices: 149 us -> 140 us
  other arithmetic: 22.4 us -> 31.1 us
    dot_general x8 -> x4, matrix products: 42.4 us -> 32.6 us  [one_block(): jnp.einsum('td,vd->tv', row_block, head, preferred_element_type=jnp.float32)]
    all_gather x2, waiting for transfers between devices: 32 us -> 23.4 us  [the longest x1 23.4 us: per_device(): gathered_second = lax.all_gather(final_second, 'chip', axis=0, tiled=True)]
    squeeze x0 -> x2, local copies, waits for them, and re-layouts: none -> 5.95 us  [model_stats(): head = jnp.concatenate([vocab_head[which], partner_head[which]], axis=0)]
    concatenate x0 -> x2, other arithmetic: none -> 5.31 us  [model_stats(): head = jnp.concatenate([vocab_head[which], partner_head[which]], axis=0)]
    reduce_sum x8 -> x4, other arithmetic: 14 us -> 17.3 us  [one_block(): masses = jnp.sum(jnp.exp(logits - highest[:, None]), axis=1)]
  transfers between devices with their start and end apart: 5 -> 6, of which waited for: 5 -> 4; matrix products, arithmetic and copies ran while one was open for 17% -> 19% of each run, Pallas kernels for 0% -> 0%
where the time goes in v8:
time: 344 us; the launch traced here: 338 us
  waiting for transfers between devices  140 us (41%)
  matrix products  80.5 us (23%)
  other arithmetic  31.1 us (9%)
  blocking collectives  28.1 us (8%)
  starting transfers between devices  27.1 us (8%)
  between operations  14.9 us (4%)
  local copies, waits for them, and re-layouts  13.7 us (4%)
    all_to_all x3, waiting for transfers between devices, exchange(): lax.all_to_all(blocks, ('chip', 'core'), split_axis=0, concat_axis=0, til...  116 us
    dot_general x4, matrix products, one_block(): jnp.einsum('td,vd->tv', row_block, head, preferred_element_type=jnp.float32)  32.6 us
    all_to_all x3, starting transfers between devices, exchange(): lax.all_to_all(blocks, ('chip', 'core'), split_axis=0, concat_axis=0, til...  26.1 us
    all_gather x1, waiting for transfers between devices, per_device(): gathered_second = lax.all_gather(final_second, 'chip', axis=0, tiled=True)  23.4 us
    reduce_sum x4, other arithmetic, one_block(): masses = jnp.sum(jnp.exp(logits - highest[:, None]), axis=1)  17.3 us
    all_to_all x1, blocking collectives, per_device(): lax.all_to_all(dense_totals.reshape(devices, per_device_seqs), ('req', 'c...  16.9 us
    all_to_all x1, blocking collectives, per_device(): gathered = lax.all_to_all(stacked, 'chip', 0, 0, tiled=True)  11.2 us
    dot_general x2, matrix products, model_experts(): jnp.einsum('slcd,ldf->slcf', inputs, expert_in[which], preferred_element_...  10.9 us
  transfers between devices with their start and end apart: 6, of which 4 were waited for; matrix products, arithmetic and copies ran while one was open for 19% of the time, Pallas kernels for 0%

profile of v8, /device:TPU:1, one launch (start us, length us, event | category | flops | bytes accessed | tf_op | source)
XLA Modules:
  0.0 338.3 jit_solution(13139421585096266891)
XLA Ops:
  9.2 3.1 fusion.20
  18.0 5.0 %fusion.27 = bf16[1280,1024]{1,0:T(8,128)(2,1)} fusion(s32[1024]{0:T(1024)S(1)} %multiply_add_fusion.3, bf16[128,1024]{1,0:T(8,128)(2,1)S(1)} %multiply_convert_fusion.3), kind=kOutput, calls=%fused_computation.45 | convolution fusion | flops 2686976000 | bytes 2887680 | tf_op jit(solution)/shard_map/ps,pd->sd/dot_general | solution.py:172
  22.9 10.3 %all-to-all-start = ((bf16[32,40,1024]{2,1,0:T(8,128)(2,1)}), bf16[32,40,1024]{2,1,0:T(8,128)(2,1)}, u32[]{:S(2)}, u32[]{:S(2)}) async-start(bf16[32,40,1024]{2,1,0:T(8,128)(2,1)} %bitcast.26), calls=%async_computation | async-start | bytes 5242880 | tf_op jit(solution)/shard_map/all_to_all | solution.py:221
  33.4 3.0 fusion.18
  41.8 4.8 %fusion.26 = bf16[1280,1024]{1,0:T(8,128)(2,1)} fusion(s32[1024]{0:T(1024)S(1)} %multiply_add_fusion.2, bf16[128,1024]{1,0:T(8,128)(2,1)S(1)} %multiply_convert_fusion.2), kind=kOutput, calls=%fused_computation.44 | convolution fusion | flops 2686976000 | bytes 2887680 | tf_op jit(solution)/shard_map/ps,pd->sd/dot_general | solution.py:172
  46.7 20.4 %all-to-all-done = bf16[32,40,1024]{2,1,0:T(8,128)(2,1)} async-done(((bf16[32,40,1024]{2,1,0:T(8,128)(2,1)}), bf16[32,40,1024]{2,1,0:T(8,128)(2,1)}, u32[]{:S(2)}, u32[]{:S(2)}) %all-to-all-start) | async-done | bytes 2621472 | tf_op jit(solution)/shard_map/all_to_all | solution.py:221
  67.1 5.5 %convolution_bitcast_fusion = f32[32,1,40,1024]{3,2,0,1:T(8,128)S(1)} fusion(bf16[32,40,1024]{2,1,0:T(8,128)(2,1)} %all-to-all-done, bf16[2,1,1024,1024]{3,2,1,0:T(8,128)(2,1)} %param.25), kind=kOutput, calls=%fused_computation.57 | convolution fusion | flops 2684354560 | bytes 9961472 | tf_op jit(solution)/shard_map/slcd,ldf->slcf/dot_general | solution.py:179
  74.3 2.9 pad_maximum_fusion
  77.2 7.1 %all-to-all-start.1 = ((bf16[32,80,1024]{2,1,0:T(8,128)(2,1)}), bf16[32,80,1024]{2,1,0:T(8,128)(2,1)}, u32[]{:S(2)}, u32[]{:S(2)}) async-start(bf16[32,80,1024]{2,1,0:T(8,128)(2,1)} %pad_maximum_fusion), calls=%async_computation.1 | async-start | bytes 10485760 | tf_op jit(solution)/shard_map/all_to_all | solution.py:221
  84.7 61.5 %all-to-all-done.1 = bf16[32,80,1024]{2,1,0:T(8,128)(2,1)} async-done(((bf16[32,80,1024]{2,1,0:T(8,128)(2,1)}), bf16[32,80,1024]{2,1,0:T(8,128)(2,1)}, u32[]{:S(2)}, u32[]{:S(2)}) %all-to-all-start.1) | async-done | bytes 5242912 | tf_op jit(solution)/shard_map/all_to_all | solution.py:221
  148.2 3.3 multiply_reduce_fusion.3
  152.6 5.4 %fusion.36 = f32[32,1,40,1024]{3,2,0,1:T(8,128)S(1)} fusion(bf16[32,80,1024]{2,1,0:T(8,128)(2,1)} %all-to-all-done.1, bf16[2,1,1024,1024]{3,2,1,0:T(8,128)(2,1)} %param.25), kind=kOutput, calls=%fused_computation.56 | convolution fusion | flops 2684354560 | bytes 9961472 | tf_op jit(solution)/shard_map/slcd,ldf->slcf/dot_general | solution.py:179
  158.0 3.2 convolution_convert_fusion
  161.2 8.8 %all-to-all-start.2 = ((bf16[32,40,1024]{2,1,0:T(8,128)(2,1)}), bf16[32,40,1024]{2,1,0:T(8,128)(2,1)}, u32[]{:S(2)}, u32[]{:S(2)}) async-start(bf16[32,40,1024]{2,1,0:T(8,128)(2,1)} %convolution_convert_fusion), calls=%async_computation.2 | async-start | bytes 5242880 | tf_op jit(solution)/shard_map/all_to_all | solution.py:221
  170.9 34.6 %all-to-all-done.2 = bf16[32,40,1024]{2,1,0:T(8,128)(2,1)} async-done(((bf16[32,40,1024]{2,1,0:T(8,128)(2,1)}), bf16[32,40,1024]{2,1,0:T(8,128)(2,1)}, u32[]{:S(2)}, u32[]{:S(2)}) %all-to-all-start.2) | async-done | bytes 2621472 | tf_op jit(solution)/shard_map/all_to_all | solution.py:221
  205.5 5.0 %multiply_reduce_fusion.2 = f32[128,1024]{1,0:T(8,128)S(1)} fusion(f32[128,8]{0,1:T(8,128)S(1)} %get-tuple-element.174, bf16[1280,1024,1]{1,0,2:T(8,128)(2,1)} %bitcast.80, s32[128,8]{0,1:T(8,128)S(1)} %copy.117), kind=kOutput, calls=%fused_computation.37 | convolution fusion | flops 2687631360 | bytes 3153920 | tf_op jit(solution)/shard_map/tks,sd->tkd/dot_general | solution.py:193
  211.7 3.0 slice_bitcast_fusion.3
  214.7 3.0 slice_bitcast_fusion.1
  217.7 2.7 pad_maximum_fusion.1
  223.0 27.6 %while.23 = (s32[]{:T(128)}, f32[2,3,1024]{2,1,0:T(4,128)S(1)}, s32[2]{0:T(128)S(1)}, bf16[2048,1024]{1,0:T(8,128)(2,1)}, bf16[2304,1024]{1,0:T(8,128)(2,1)}, /*...) while((s32[]{:T(128)}, f32[2,3,1024]{2,1,0:T(4,128)S(1)}, ...), condition=%wide.region_19.20_spmd.clone, body=%wide.region_15.19_spmd.clone.sunk | while | flops 4850715648 | bytes 25747636 | solution.py:217
  224.3 8.1 %multiply_reduce_fusion.10 = (f32[1024]{0:T(1024)S(1)}, f32[1024,2304]{1,0:T(8,128)S(1)}) fusion(bf16[2304,1024]{1,0:T(8,128)(2,1)} %get-tuple-element.327, bf16[2048,1024]{1,0:T(8,128)(2,1)} %get-tuple-element.326, s32[]{:T(128)S(6)} %select_n.95), kind=kOutput, calls=%fused_computation.5.clone.1 | convolution fusion | flops 4836555776 | bytes 16257028 | tf_op jit(solution)/shard_map/while/body/eval_jaxpr/td,vd->tv/dot_general | solution.py:209
  232.4 4.3 %exponential_reduce_fusion.4 = (f32[1024]{0:T(1024)S(1)}, f32[1024]{0:T(1024)S(1)}) fusion(f32[1024,2304]{1,0:T(8,128)S(1)} %get-tuple-element.259, f32[1024]{0:T(1024)S(1)} %get-tuple-element.260, s32[1024]{0:T(1024)S(1)} %dynamic_slice.41), kind=kLoop, calls=%fused_computation.4.clone.1 | loop fusion | flops 14153728 | bytes 9453568 | tf_op jit(solution)/shard_map/while/body/eval_jaxpr/reduce_sum | solution.py:213
  238.0 8.2 %multiply_reduce_fusion.10 = (f32[1024]{0:T(1024)S(1)}, f32[1024,2304]{1,0:T(8,128)S(1)}) fusion(bf16[2304,1024]{1,0:T(8,128)(2,1)} %get-tuple-element.327, bf16[2048,1024]{1,0:T(8,128)(2,1)} %get-tuple-element.326, s32[]{:T(128)S(6)} %select_n.95), kind=kOutput, calls=%fused_computation.5.clone.1 | convolution fusion | flops 4836555776 | bytes 16257028 | tf_op jit(solution)/shard_map/while/body/eval_jaxpr/td,vd->tv/dot_general | solution.py:209
  246.2 4.3 %exponential_reduce_fusion.4 = (f32[1024]{0:T(1024)S(1)}, f32[1024]{0:T(1024)S(1)}) fusion(f32[1024,2304]{1,0:T(8,128)S(1)} %get-tuple-element.259, f32[1024]{0:T(1024)S(1)} %get-tuple-element.260, s32[1024]{0:T(1024)S(1)} %dynamic_slice.41), kind=kLoop, calls=%fused_computation.4.clone.1 | loop fusion | flops 14153728 | bytes 9453568 | tf_op jit(solution)/shard_map/while/body/eval_jaxpr/reduce_sum | solution.py:213
  250.6 23.4 %all-gather.5.cloned.1.call-done = bf16[2048,1024]{1,0:T(8,128)(2,1)} async-done(((bf16[128,1024]{1,0:T(8,128)(2,1)}), bf16[2048,1024]{1,0:T(8,128)(2,1)}) %all-gather.5.cloned.1.call-update) | async-done | bytes 4194320 | tf_op jit(solution)/shard_map/all_gather | solution.py:232
  274.1 27.8 %while.24 = (s32[]{:T(128)}, f32[2,3,1024]{2,1,0:T(4,128)S(1)}, s32[2]{0:T(128)S(1)}, bf16[2048,1024]{1,0:T(8,128)(2,1)}, bf16[2304,1024]{1,0:T(8,128)(2,1)}, /*...) while((s32[]{:T(128)}, f32[2,3,1024]{2,1,0:T(4,128)S(1)}, ...), condition=%wide.region_26.27_spmd.clone, body=%wide.region_22.26_spmd.clone.sunk | while | flops 4850715648 | bytes 25747636 | solution.py:217
  275.6 8.1 %multiply_reduce_fusion.11 = (f32[1024]{0:T(1024)S(1)}, f32[1024,2304]{1,0:T(8,128)S(1)}) fusion(bf16[2304,1024]{1,0:T(8,128)(2,1)} %get-tuple-element.297, bf16[2048,1024]{1,0:T(8,128)(2,1)} %get-tuple-element.296, s32[]{:T(128)S(6)} %select_n.96), kind=kOutput, calls=%fused_computation.14.clone.1 | convolution fusion | flops 4836555776 | bytes 16257028 | tf_op jit(solution)/shard_map/while/body/eval_jaxpr/td,vd->tv/dot_general | solution.py:209
  283.8 4.3 %exponential_reduce_fusion.5 = (f32[1024]{0:T(1024)S(1)}, f32[1024]{0:T(1024)S(1)}) fusion(f32[1024,2304]{1,0:T(8,128)S(1)} %get-tuple-element.269, f32[1024]{0:T(1024)S(1)} %get-tuple-element.270, s32[1024]{0:T(1024)S(1)} %dynamic_slice.44), kind=kLoop, calls=%fused_computation.13.clone.1 | loop fusion | flops 14153728 | bytes 9453568 | tf_op jit(solution)/shard_map/while/body/eval_jaxpr/reduce_sum | solution.py:213
  289.4 8.1 %multiply_reduce_fusion.11 = (f32[1024]{0:T(1024)S(1)}, f32[1024,2304]{1,0:T(8,128)S(1)}) fusion(bf16[2304,1024]{1,0:T(8,128)(2,1)} %get-tuple-element.297, bf16[2048,1024]{1,0:T(8,128)(2,1)} %get-tuple-element.296, s32[]{:T(128)S(6)} %select_n.96), kind=kOutput, calls=%fused_computation.14.clone.1 | convolution fusion | flops 4836555776 | bytes 16257028 | tf_op jit(solution)/shard_map/while/body/eval_jaxpr/td,vd->tv/dot_general | solution.py:209
  297.5 4.3 %exponential_reduce_fusion.5 = (f32[1024]{0:T(1024)S(1)}, f32[1024]{0:T(1024)S(1)}) fusion(f32[1024,2304]{1,0:T(8,128)S(1)} %get-tuple-element.269, f32[1024]{0:T(1024)S(1)} %get-tuple-element.270, s32[1024]{0:T(1024)S(1)} %dynamic_slice.44), kind=kLoop, calls=%fused_computation.13.clone.1 | loop fusion | flops 14153728 | bytes 9453568 | tf_op jit(solution)/shard_map/while/body/eval_jaxpr/reduce_sum | solution.py:213
  302.0 11.2 %all_to_all.29 = f32[16,3,2,128]{3,2,1,0:T(2,128)S(1)} all-to-all(f32[16,3,2,128]{3,2,1,0:T(2,128)S(1)} %copy.119), channel_id=1, replica_groups=mesh['req'=4,'chip'=16,'core'=2] {'chip'}, dimensions={0} | all-to-all | bytes 98304 | tf_op jit(solution)/shard_map/all_to_all | solution.py:236
  313.7 16.9 %all_to_all.30 = f32[128,1,4]{2,1,0:T(1,128)S(1)} all-to-all(f32[128,1,4]{2,1,0:T(1,128)S(1)} %bitcast.310), channel_id=1, replica_groups=mesh['req'=4,'chip'=16,'core'=2] {'req','chip','core'}, dimensions={0} | all-to-all | bytes 4096 | tf_op jit(solution)/shard_map/all_to_all | solution.py:254
  (136 shorter events, 26.7 us)
Async XLA Ops:
  8.4 4.0 %copy-start.13 = (s32[1,4]{1,0:T(1,128)S(1)}, s32[1,4]{1,0:T(1,128)}, u32[]{:S(2)}) copy-start(s32[1,4]{1,0:T(1,128)} %param.17) | copy-start | bytes 52
  12.7 1.3 copy-start.7
  13.2 1.1 copy-start.5
  14.0 1.7 copy-start.1
  22.9 10.5 %copy-start.2 = (bf16[2,128,1024]{2,1,0:T(8,128)(2,1)S(1)}, bf16[2,128,1024]{2,1,0:T(8,128)(2,1)}, u32[]{:S(2)}) copy-start(bf16[2,128,1024]{2,1,0:T(8,128)(2,1)} %param.16) | copy-start | bytes 1572868
  22.9 44.2 %all-to-all-start = ((bf16[32,40,1024]{2,1,0:T(8,128)(2,1)}), bf16[32,40,1024]{2,1,0:T(8,128)(2,1)}, u32[]{:S(2)}, u32[]{:S(2)}) async-start(bf16[32,40,1024]{2,1,0:T(8,128)(2,1)} %bitcast.26), calls=%async_computation | async-start | bytes 5242880 | tf_op jit(solution)/shard_map/all_to_all | solution.py:221
  38.5 1.0 copy-start.3
  67.1 5.5 %copy-start.11 = (bf16[2,1,512,1024]{3,2,1,0:T(8,128)(2,1)S(1)}, bf16[2,1,512,1024]{3,2,1,0:T(8,128)(2,1)}, u32[]{:S(2)}) copy-start(bf16[2,1,512,1024]{3,2,1,0:T(8,128)(2,1)} %param.26) | copy-start | bytes 6291460
  72.5 1.7 copy-start
  77.2 7.5 %copy-start.6 = (f32[2,128,8]{1,2,0:T(8,128)S(1)}, f32[2,128,8]{1,2,0:T(8,128)}, u32[]{:S(2)}) copy-start(f32[2,128,8]{1,2,0:T(8,128)} %param.20) | copy-start | bytes 24580
  77.2 69.0 %all-to-all-start.1 = ((bf16[32,80,1024]{2,1,0:T(8,128)(2,1)}), bf16[32,80,1024]{2,1,0:T(8,128)(2,1)}, u32[]{:S(2)}, u32[]{:S(2)}) async-start(bf16[32,80,1024]{2,1,0:T(8,128)(2,1)} %pad_maximum_fusion), calls=%async_computation.1 | async-start | bytes 10485760 | tf_op jit(solution)/shard_map/all_to_all | solution.py:221
  84.3 138.7 %all-gather.3.cloned.1.call-start = ((), (), s32[]{:S(2)}) async-start(), calls=%async_computation.5 | async-start | bytes 4456448 | tf_op jit(solution)/shard_map/all_gather | solution.py:229
  152.6 5.5 %copy-start.12 = (bf16[2,1,512,1024]{3,2,1,0:T(8,128)(2,1)S(1)}, bf16[2,1,512,1024]{3,2,1,0:T(8,128)(2,1)}, u32[]{:S(2)}) copy-start(bf16[2,1,512,1024]{3,2,1,0:T(8,128)(2,1)} %param.26) | copy-start | bytes 6291460
  161.2 44.3 %all-to-all-start.2 = ((bf16[32,40,1024]{2,1,0:T(8,128)(2,1)}), bf16[32,40,1024]{2,1,0:T(8,128)(2,1)}, u32[]{:S(2)}, u32[]{:S(2)}) async-start(bf16[32,40,1024]{2,1,0:T(8,128)(2,1)} %convolution_convert_fusion), calls=%async_computation.2 | async-start | bytes 5242880 | tf_op jit(solution)/shard_map/all_to_all | solution.py:221
  170.0 104.0 %all-gather.5.cloned.1.call-start = ((), (), s32[]{:S(2)}) async-start(), calls=%async_computation.6 | async-start | bytes 4456448 | tf_op jit(solution)/shard_map/all_gather | solution.py:232
  170.1 44.6 %collective-permute-start = (bf16[2,1152,1024]{2,1,0:T(8,128)(2,1)}, bf16[2,1152,1024]{2,1,0:T(8,128)(2,1)}, u32[]{:S(2)}, u32[]{:S(2)}) collective-permute-start(bf16[2,1152,1024]{2,1,0:T(8,128)(2,1)} %param.27), channel_id=1, source_target_pairs={{0,1},{1,0},{2,3},{3,2},{4,5},{5,4},{6,7},{7,6},{8,9},{9,8},{10,11... | collective-permute-start | bytes 14155784 | tf_op jit(solution)/shard_map/ppermute | solution.py:141
  205.5 6.1 %copy-start.4 = (s32[4096]{0:T(1024)S(1)}, s32[4096]{0:T(1024)}, u32[]{:S(2)}) copy-start(s32[4096]{0:T(1024)} %param.18) | copy-start | bytes 49156
  274.1 39.3 %copy-start.8 = (s32[128]{0:T(128)S(1)}, s32[128]{0:T(128)}, u32[]{:S(2)}) copy-start(s32[128]{0:T(128)} %copy-done.7) | copy-start | bytes 1540
  274.1 39.4 %copy-start.10 = (s32[4]{0:T(128)S(1)}, s32[4]{0:T(128)}, u32[]{:S(2)}) copy-start(s32[4]{0:T(128)} %param.21) | copy-start | bytes 52
  313.4 17.9 %copy-start.9 = (f32[2,128]{1,0:T(2,128)}, f32[2,128]{1,0:T(2,128)S(1)}, u32[]{:S(2)}) copy-start(f32[2,128]{1,0:T(2,128)S(1)} %add_subtract_fusion) | copy-start | bytes 3076
Sparse Core Ops, SparseCore 0:
  152.7 68.1 all-gather.2
  223.0 51.0 all-gather.4

commit v9 on v8

--- a/solution.py
+++ b/solution.py
@@ -139,8 +139,7 @@
     own_shard = chip * 2 + core
     other_shard = chip * 2 + (1 - core)
     partner_head = lax.ppermute(vocab_head, "core", perm=[(0, 1), (1, 0)])
-    pair_rows = 2 * vocab_rows
-    vocab_ids = jnp.arange(pair_rows, dtype=jnp.int32)
+    vocab_ids = jnp.arange(vocab_rows, dtype=jnp.int32)
     mine = jnp.take(targets.reshape(chips, 2, token_count), core, axis=1).reshape(chips * token_count)
     place_in = mine % vocab_rows
     wanted_all = jnp.where(
@@ -200,18 +199,29 @@
     def model_stats(which, chunk):
         chunk_rows = chunk.shape[0]
         block_count = chunk_rows // block_rows
-        head = jnp.concatenate([vocab_head[which], partner_head[which]], axis=0)
 
         def one_block(block_number):
             row_block = lax.dynamic_slice_in_dim(chunk, block_number * block_rows, block_rows, 0)
             wanted = lax.dynamic_slice_in_dim(wanted_all, block_number * block_rows, block_rows, 0)
-            logits = (
-                jnp.einsum("td,vd->tv", row_block, head, preferred_element_type=jnp.float32)
+            near = (
+                jnp.einsum(
+                    "td,vd->tv", row_block, vocab_head[which], preferred_element_type=jnp.float32
+                )
                 / LOGIT_DIVISOR
             )
-            highest = jnp.max(logits, axis=1)
-            masses = jnp.sum(jnp.exp(logits - highest[:, None]), axis=1)
-            chosen = jnp.sum(jnp.where(wanted[:, None] == vocab_ids[None, :], logits, 0.0), axis=1)
+            far = (
+                jnp.einsum(
+                    "td,vd->tv", row_block, partner_head[which], preferred_element_type=jnp.float32
+                )
+                / LOGIT_DIVISOR
+            )
+            highest = jnp.maximum(jnp.max(near, axis=1), jnp.max(far, axis=1))
+            masses = jnp.sum(jnp.exp(near - highest[:, None]), axis=1) + jnp.sum(
+                jnp.exp(far - highest[:, None]), axis=1
+            )
+            chosen = jnp.sum(
+                jnp.where(wanted[:, None] == vocab_ids[None, :], near, 0.0), axis=1
+            ) + jnp.sum(jnp.where(wanted[:, None] == vocab_ids[None, :] + vocab_rows, far, 0.0), axis=1)
             return jnp.stack([highest, masses, chosen])
 
         stats = lax.map(one_block, jnp.arange(block_count, dtype=jnp.int32))

time: 344 us -> 342 us (level)
  waiting for transfers between devices: 140 us -> 153 us
  other arithmetic: 31.1 us -> 21.3 us
  local copies, waits for them, and re-layouts: 13.7 us -> 7.84 us
    all_gather x1, waiting for transfers between devices: 0.01 us -> 9.21 us  [per_device(): gathered_first = lax.all_gather(final_first, 'chip', axis=0, tiled=True)]
    squeeze x2 -> x0, local copies, waits for them, and re-layouts: 5.95 us -> none  [model_stats(): head = jnp.concatenate([vocab_head[which], partner_head[which]], axis=0)]
    concatenate x2 -> x0, other arithmetic: 5.31 us -> none  [model_stats(): head = jnp.concatenate([vocab_head[which], partner_head[which]], axis=0)]
    reduce_sum x4, other arithmetic: 17.3 us -> 12.9 us  [one_block(): jnp.sum(jnp.exp(near - highest[:, None]), axis=1)]
    all_gather x1, waiting for transfers between devices: 23.4 us -> 27.1 us  [per_device(): gathered_second = lax.all_gather(final_second, 'chip', axis=0, tiled=True)]
    dot_general x4 -> x8, matrix products: 32.6 us -> 33.8 us  [the longest x4 21.8 us: one_block(): jnp.einsum('td,vd->tv', row_block, partner_head[which], preferred_element...]
  transfers between devices with their start and end apart: 6 -> 6, of which waited for: 4 -> 5; matrix products, arithmetic and copies ran while one was open for 19% -> 16% of each run, Pallas kernels for 0% -> 0%
where the time goes in v9:
time: 342 us; the launch traced here: 337 us
  waiting for transfers between devices  153 us (45%)
  matrix products  81.5 us (24%)
  blocking collectives  28.1 us (8%)
  starting transfers between devices  27.1 us (8%)
  other arithmetic  21.3 us (6%)
  between operations  14.9 us (4%)
  local copies, waits for them, and re-layouts  7.84 us (2%)
    all_to_all x3, waiting for transfers between devices, exchange(): lax.all_to_all(blocks, ('chip', 'core'), split_axis=0, concat_axis=0, til...  116 us
    all_gather x1, waiting for transfers between devices, per_device(): gathered_second = lax.all_gather(final_second, 'chip', axis=0, tiled=True)  27.1 us
    all_to_all x3, starting transfers between devices, exchange(): lax.all_to_all(blocks, ('chip', 'core'), split_axis=0, concat_axis=0, til...  26.1 us
    dot_general x4, matrix products, one_block(): jnp.einsum('td,vd->tv', row_block, partner_head[which], preferred_element...  21.8 us
    all_to_all x1, blocking collectives, per_device(): lax.all_to_all(dense_totals.reshape(devices, per_device_seqs), ('req', 'c...  16.9 us
    reduce_sum x4, other arithmetic, one_block(): jnp.sum(jnp.exp(near - highest[:, None]), axis=1)  12.9 us
    dot_general x4, matrix products, one_block(): jnp.einsum('td,vd->tv', row_block, vocab_head[which], preferred_element_t...  12 us
    all_to_all x1, blocking collectives, per_device(): gathered = lax.all_to_all(stacked, 'chip', 0, 0, tiled=True)  11.2 us
  transfers between devices with their start and end apart: 6, of which 5 were waited for; matrix products, arithmetic and copies ran while one was open for 16% of the time, Pallas kernels for 0%

profile of v9, /device:TPU:1, one launch (start us, length us, event | category | flops | bytes accessed | tf_op | source)
XLA Modules:
  0.0 336.7 jit_solution(6892880971077563166)
XLA Ops:
  9.2 3.1 fusion.30
  18.0 5.0 %fusion.37 = bf16[1280,1024]{1,0:T(8,128)(2,1)} fusion(s32[1024]{0:T(1024)S(1)} %multiply_add_fusion.3, bf16[128,1024]{1,0:T(8,128)(2,1)S(1)} %multiply_convert_fusion.3), kind=kOutput, calls=%fused_computation.61 | convolution fusion | flops 2686976000 | bytes 2887680 | tf_op jit(solution)/shard_map/ps,pd->sd/dot_general | solution.py:171
  22.9 10.3 %all-to-all-start = ((bf16[32,40,1024]{2,1,0:T(8,128)(2,1)}), bf16[32,40,1024]{2,1,0:T(8,128)(2,1)}, u32[]{:S(2)}, u32[]{:S(2)}) async-start(bf16[32,40,1024]{2,1,0:T(8,128)(2,1)} %bitcast.26), calls=%async_computation | async-start | bytes 5242880 | tf_op jit(solution)/shard_map/all_to_all | solution.py:231
  41.8 4.8 %fusion.36 = bf16[1280,1024]{1,0:T(8,128)(2,1)} fusion(s32[1024]{0:T(1024)S(1)} %multiply_add_fusion.2, bf16[128,1024]{1,0:T(8,128)(2,1)S(1)} %multiply_convert_fusion.2), kind=kOutput, calls=%fused_computation.60 | convolution fusion | flops 2686976000 | bytes 2887680 | tf_op jit(solution)/shard_map/ps,pd->sd/dot_general | solution.py:171
  46.7 20.4 %all-to-all-done = bf16[32,40,1024]{2,1,0:T(8,128)(2,1)} async-done(((bf16[32,40,1024]{2,1,0:T(8,128)(2,1)}), bf16[32,40,1024]{2,1,0:T(8,128)(2,1)}, u32[]{:S(2)}, u32[]{:S(2)}) %all-to-all-start) | async-done | bytes 2621472 | tf_op jit(solution)/shard_map/all_to_all | solution.py:231
  67.1 5.3 %convolution_bitcast_fusion = f32[32,1,40,1024]{3,2,0,1:T(8,128)S(1)} fusion(bf16[32,40,1024]{2,1,0:T(8,128)(2,1)} %all-to-all-done, bf16[2,1,1024,1024]{3,2,1,0:T(8,128)(2,1)} %param.25), kind=kOutput, calls=%fused_computation.73 | convolution fusion | flops 2684354560 | bytes 9961472 | tf_op jit(solution)/shard_map/slcd,ldf->slcf/dot_general | solution.py:178
  77.1 7.0 %all-to-all-start.1 = ((bf16[32,80,1024]{2,1,0:T(8,128)(2,1)}), bf16[32,80,1024]{2,1,0:T(8,128)(2,1)}, u32[]{:S(2)}, u32[]{:S(2)}) async-start(bf16[32,80,1024]{2,1,0:T(8,128)(2,1)} %pad_maximum_fusion), calls=%async_computation.1 | async-start | bytes 10485760 | tf_op jit(solution)/shard_map/all_to_all | solution.py:231
  84.6 61.5 %all-to-all-done.1 = bf16[32,80,1024]{2,1,0:T(8,128)(2,1)} async-done(((bf16[32,80,1024]{2,1,0:T(8,128)(2,1)}), bf16[32,80,1024]{2,1,0:T(8,128)(2,1)}, u32[]{:S(2)}, u32[]{:S(2)}) %all-to-all-start.1) | async-done | bytes 5242912 | tf_op jit(solution)/shard_map/all_to_all | solution.py:231
  148.1 3.3 multiply_reduce_fusion.1
  152.4 5.3 %fusion.46 = f32[32,1,40,1024]{3,2,0,1:T(8,128)S(1)} fusion(bf16[32,80,1024]{2,1,0:T(8,128)(2,1)} %all-to-all-done.1, bf16[2,1,1024,1024]{3,2,1,0:T(8,128)(2,1)} %param.25), kind=kOutput, calls=%fused_computation.72 | convolution fusion | flops 2684354560 | bytes 9961472 | tf_op jit(solution)/shard_map/slcd,ldf->slcf/dot_general | solution.py:178
  157.7 3.3 convolution_convert_fusion
  161.0 8.8 %all-to-all-start.2 = ((bf16[32,40,1024]{2,1,0:T(8,128)(2,1)}), bf16[32,40,1024]{2,1,0:T(8,128)(2,1)}, u32[]{:S(2)}, u32[]{:S(2)}) async-start(bf16[32,40,1024]{2,1,0:T(8,128)(2,1)} %convolution_convert_fusion), calls=%async_computation.2 | async-start | bytes 5242880 | tf_op jit(solution)/shard_map/all_to_all | solution.py:231
  170.7 34.5 %all-to-all-done.2 = bf16[32,40,1024]{2,1,0:T(8,128)(2,1)} async-done(((bf16[32,40,1024]{2,1,0:T(8,128)(2,1)}), bf16[32,40,1024]{2,1,0:T(8,128)(2,1)}, u32[]{:S(2)}, u32[]{:S(2)}) %all-to-all-start.2) | async-done | bytes 2621472 | tf_op jit(solution)/shard_map/all_to_all | solution.py:231
  205.2 5.0 %multiply_reduce_fusion = f32[128,1024]{1,0:T(8,128)S(1)} fusion(f32[128,8]{0,1:T(8,128)S(1)} %get-tuple-element.246, bf16[1280,1024,1]{1,0,2:T(8,128)(2,1)} %bitcast.78, s32[128,8]{0,1:T(8,128)S(1)} %copy.117), kind=kOutput, calls=%fused_computation.53 | convolution fusion | flops 2687631360 | bytes 3153920 | tf_op jit(solution)/shard_map/tks,sd->tkd/dot_general | solution.py:192
  211.4 9.2 %all-gather.3.cloned.1.call-done = bf16[2048,1024]{1,0:T(8,128)(2,1)} async-done(((bf16[128,1024]{1,0:T(8,128)(2,1)}), bf16[2048,1024]{1,0:T(8,128)(2,1)}) %all-gather.3.cloned.1.call-update) | async-done | bytes 4194320 | tf_op jit(solution)/shard_map/all_gather | solution.py:239
  220.6 26.1 %while.25 = (s32[]{:T(128)}, f32[2,3,1024]{2,1,0:T(4,128)S(1)}, s32[2]{0:T(128)S(1)}, bf16[2048,1024]{1,0:T(8,128)(2,1)}, bf16[2,1152,1024]{2,1,0:T(8,128)(2,1)}...) while((s32[]{:T(128)}, f32[2,3,1024]{2,1,0:T(4,128)S(1)}, ...), condition=%wide.region_22.23_spmd.clone.clone, body=%wide.region_15.22_spmd.clone.clone.sunk | while | flops 4848357376 | bytes 63554804 | solution.py:227
  221.9 5.4 %fusion.220 = (f32[1024]{0:T(1024)S(1)}, f32[1024,1152]{1,0:T(8,128)S(1)}) fusion(bf16[2,1152,1024]{2,1,0:T(8,128)(2,1)} %get-tuple-element.433, bf16[2048,1024]{1,0:T(8,128)(2,1)} %get-tuple-element.431, s32[]{:T(128)S(6)} %select_n.111), kind=kOutput, calls=%fused_computation.250.clone.1 | convolution fusion | flops 2418277376 | bytes 9179140 | tf_op jit(solution)/shard_map/while/body/eval_jaxpr/td,vd->tv/dot_general | solution.py:213
  227.3 3.0 fusion.219
  230.3 3.2 exponential_reduce_fusion.6
  234.9 5.4 %fusion.220 = (f32[1024]{0:T(1024)S(1)}, f32[1024,1152]{1,0:T(8,128)S(1)}) fusion(bf16[2,1152,1024]{2,1,0:T(8,128)(2,1)} %get-tuple-element.433, bf16[2048,1024]{1,0:T(8,128)(2,1)} %get-tuple-element.431, s32[]{:T(128)S(6)} %select_n.111), kind=kOutput, calls=%fused_computation.250.clone.1 | convolution fusion | flops 2418277376 | bytes 9179140 | tf_op jit(solution)/shard_map/while/body/eval_jaxpr/td,vd->tv/dot_general | solution.py:213
  240.4 3.0 fusion.219
  243.4 3.2 exponential_reduce_fusion.6
  246.7 27.1 %all-gather.5.cloned.1.call-done = bf16[2048,1024]{1,0:T(8,128)(2,1)} async-done(((bf16[128,1024]{1,0:T(8,128)(2,1)}), bf16[2048,1024]{1,0:T(8,128)(2,1)}) %all-gather.5.cloned.1.call-update) | async-done | bytes 4194320 | tf_op jit(solution)/shard_map/all_gather | solution.py:242
  273.9 26.4 %while.26 = (s32[]{:T(128)}, f32[2,3,1024]{2,1,0:T(4,128)S(1)}, s32[2]{0:T(128)S(1)}, bf16[2048,1024]{1,0:T(8,128)(2,1)}, bf16[2,1152,1024]{2,1,0:T(8,128)(2,1)}...) while((s32[]{:T(128)}, f32[2,3,1024]{2,1,0:T(4,128)S(1)}, ...), condition=%wide.region_32.33_spmd.clone.clone, body=%wide.region_25.32_spmd.clone.clone.sunk | while | flops 4848357376 | bytes 63554804 | solution.py:227
  275.4 5.4 %fusion.223 = (f32[1024]{0:T(1024)S(1)}, f32[1024,1152]{1,0:T(8,128)S(1)}) fusion(bf16[2,1152,1024]{2,1,0:T(8,128)(2,1)} %get-tuple-element.400, bf16[2048,1024]{1,0:T(8,128)(2,1)} %get-tuple-element.398, s32[]{:T(128)S(6)} %select_n.112), kind=kOutput, calls=%fused_computation.252.clone.1 | convolution fusion | flops 2418277376 | bytes 9179140 | tf_op jit(solution)/shard_map/while/body/eval_jaxpr/td,vd->tv/dot_general | solution.py:213
  280.9 3.0 fusion.222
  283.9 3.2 exponential_reduce_fusion.7
  288.5 5.4 %fusion.223 = (f32[1024]{0:T(1024)S(1)}, f32[1024,1152]{1,0:T(8,128)S(1)}) fusion(bf16[2,1152,1024]{2,1,0:T(8,128)(2,1)} %get-tuple-element.400, bf16[2048,1024]{1,0:T(8,128)(2,1)} %get-tuple-element.398, s32[]{:T(128)S(6)} %select_n.112), kind=kOutput, calls=%fused_computation.252.clone.1 | convolution fusion | flops 2418277376 | bytes 9179140 | tf_op jit(solution)/shard_map/while/body/eval_jaxpr/td,vd->tv/dot_general | solution.py:213
  294.0 3.0 fusion.222
  297.0 3.2 exponential_reduce_fusion.7
  300.4 11.2 %all_to_all.29 = f32[16,3,2,128]{3,2,1,0:T(2,128)S(1)} all-to-all(f32[16,3,2,128]{3,2,1,0:T(2,128)S(1)} %copy.119), channel_id=1, replica_groups=mesh['req'=4,'chip'=16,'core'=2] {'chip'}, dimensions={0} | all-to-all | bytes 98304 | tf_op jit(solution)/shard_map/all_to_all | solution.py:246
  312.1 16.9 %all_to_all.30 = f32[128,1,4]{2,1,0:T(1,128)S(1)} all-to-all(f32[128,1,4]{2,1,0:T(1,128)S(1)} %bitcast.324), channel_id=1, replica_groups=mesh['req'=4,'chip'=16,'core'=2] {'req','chip','core'}, dimensions={0} | all-to-all | bytes 4096 | tf_op jit(solution)/shard_map/all_to_all | solution.py:264
  (166 shorter events, 30.0 us)
Async XLA Ops:
  8.4 4.0 %copy-start.16 = (s32[1,4]{1,0:T(1,128)S(1)}, s32[1,4]{1,0:T(1,128)}, u32[]{:S(2)}) copy-start(s32[1,4]{1,0:T(1,128)} %param.17) | copy-start | bytes 52
  12.7 1.3 copy-start.7
  13.2 1.1 copy-start.5
  14.0 1.7 copy-start.1
  22.9 10.5 %copy-start.2 = (bf16[2,128,1024]{2,1,0:T(8,128)(2,1)S(1)}, bf16[2,128,1024]{2,1,0:T(8,128)(2,1)}, u32[]{:S(2)}) copy-start(bf16[2,128,1024]{2,1,0:T(8,128)(2,1)} %param.16) | copy-start | bytes 1572868
  22.9 44.2 %all-to-all-start = ((bf16[32,40,1024]{2,1,0:T(8,128)(2,1)}), bf16[32,40,1024]{2,1,0:T(8,128)(2,1)}, u32[]{:S(2)}, u32[]{:S(2)}) async-start(bf16[32,40,1024]{2,1,0:T(8,128)(2,1)} %bitcast.26), calls=%async_computation | async-start | bytes 5242880 | tf_op jit(solution)/shard_map/all_to_all | solution.py:231
  38.5 1.0 copy-start.3
  46.7 25.7 %copy-start.15 = (bf16[2,1,512,1024]{3,2,1,0:T(8,128)(2,1)S(1)}, bf16[2,1,512,1024]{3,2,1,0:T(8,128)(2,1)}, u32[]{:S(2)}) copy-start(bf16[2,1,512,1024]{3,2,1,0:T(8,128)(2,1)} %param.26) | copy-start | bytes 6291460
  72.4 1.8 copy-start
  77.1 7.4 %copy-start.6 = (f32[2,128,8]{1,2,0:T(8,128)S(1)}, f32[2,128,8]{1,2,0:T(8,128)}, u32[]{:S(2)}) copy-start(f32[2,128,8]{1,2,0:T(8,128)} %param.20) | copy-start | bytes 24580
  77.1 69.0 %all-to-all-start.1 = ((bf16[32,80,1024]{2,1,0:T(8,128)(2,1)}), bf16[32,80,1024]{2,1,0:T(8,128)(2,1)}, u32[]{:S(2)}, u32[]{:S(2)}) async-start(bf16[32,80,1024]{2,1,0:T(8,128)(2,1)} %pad_maximum_fusion), calls=%async_computation.1 | async-start | bytes 10485760 | tf_op jit(solution)/shard_map/all_to_all | solution.py:231
  84.2 136.4 %all-gather.3.cloned.1.call-start = ((), (), s32[]{:S(2)}) async-start(), calls=%async_computation.5 | async-start | bytes 4456448 | tf_op jit(solution)/shard_map/all_gather | solution.py:239
  161.0 44.2 %all-to-all-start.2 = ((bf16[32,40,1024]{2,1,0:T(8,128)(2,1)}), bf16[32,40,1024]{2,1,0:T(8,128)(2,1)}, u32[]{:S(2)}, u32[]{:S(2)}) async-start(bf16[32,40,1024]{2,1,0:T(8,128)(2,1)} %convolution_convert_fusion), calls=%async_computation.2 | async-start | bytes 5242880 | tf_op jit(solution)/shard_map/all_to_all | solution.py:231
  169.8 104.1 %all-gather.5.cloned.1.call-start = ((), (), s32[]{:S(2)}) async-start(), calls=%async_computation.6 | async-start | bytes 4456448 | tf_op jit(solution)/shard_map/all_gather | solution.py:242
  169.8 41.5 %collective-permute-start = (bf16[2,1152,1024]{2,1,0:T(8,128)(2,1)}, bf16[2,1152,1024]{2,1,0:T(8,128)(2,1)}, u32[]{:S(2)}, u32[]{:S(2)}) collective-permute-start(bf16[2,1152,1024]{2,1,0:T(8,128)(2,1)} %param.27), channel_id=1, source_target_pairs={{0,1},{1,0},{2,3},{3,2},{4,5},{5,4},{6,7},{7,6},{8,9},{9,8},{10,11... | collective-permute-start | bytes 14155784 | tf_op jit(solution)/shard_map/ppermute | solution.py:141
  205.2 6.0 %copy-start.4 = (s32[4096]{0:T(1024)S(1)}, s32[4096]{0:T(1024)}, u32[]{:S(2)}) copy-start(s32[4096]{0:T(1024)} %param.18) | copy-start | bytes 49156
  221.8 5.5 %copy-start.11 = (bf16[2,1152,1024]{2,1,0:T(8,128)(2,1)S(1)}, bf16[2,1152,1024]{2,1,0:T(8,128)(2,1)}, u32[]{:S(2)}) copy-start(bf16[2,1152,1024]{2,1,0:T(8,128)(2,1)} %get-tuple-element.432) | copy-start | bytes 14155780 | tf_op jit(solution)/shard_map/while
  221.8 5.5 %copy-start.14 = (bf16[2048,1024]{1,0:T(8,128)(2,1)S(1)}, bf16[2048,1024]{1,0:T(8,128)(2,1)}, u32[]{:S(2)}) copy-start(bf16[2048,1024]{1,0:T(8,128)(2,1)} %get-tuple-element.431) | copy-start | bytes 12582916 | tf_op jit(solution)/shard_map/while
  234.9 5.5 %copy-start.11 = (bf16[2,1152,1024]{2,1,0:T(8,128)(2,1)S(1)}, bf16[2,1152,1024]{2,1,0:T(8,128)(2,1)}, u32[]{:S(2)}) copy-start(bf16[2,1152,1024]{2,1,0:T(8,128)(2,1)} %get-tuple-element.432) | copy-start | bytes 14155780 | tf_op jit(solution)/shard_map/while
  234.9 5.5 %copy-start.14 = (bf16[2048,1024]{1,0:T(8,128)(2,1)S(1)}, bf16[2048,1024]{1,0:T(8,128)(2,1)}, u32[]{:S(2)}) copy-start(bf16[2048,1024]{1,0:T(8,128)(2,1)} %get-tuple-element.431) | copy-start | bytes 12582916 | tf_op jit(solution)/shard_map/while
  273.9 37.9 %copy-start.8 = (s32[128]{0:T(128)S(1)}, s32[128]{0:T(128)}, u32[]{:S(2)}) copy-start(s32[128]{0:T(128)} %copy-done.7) | copy-start | bytes 1540
  273.9 38.0 %copy-start.10 = (s32[4]{0:T(128)S(1)}, s32[4]{0:T(128)}, u32[]{:S(2)}) copy-start(s32[4]{0:T(128)} %param.21) | copy-start | bytes 52
  275.4 5.5 %copy-start.12 = (bf16[2,1152,1024]{2,1,0:T(8,128)(2,1)S(1)}, bf16[2,1152,1024]{2,1,0:T(8,128)(2,1)}, u32[]{:S(2)}) copy-start(bf16[2,1152,1024]{2,1,0:T(8,128)(2,1)} %get-tuple-element.399) | copy-start | bytes 14155780 | tf_op jit(solution)/shard_map/while
  275.4 5.5 %copy-start.13 = (bf16[2048,1024]{1,0:T(8,128)(2,1)S(1)}, bf16[2048,1024]{1,0:T(8,128)(2,1)}, u32[]{:S(2)}) copy-start(bf16[2048,1024]{1,0:T(8,128)(2,1)} %get-tuple-element.398) | copy-start | bytes 12582916 | tf_op jit(solution)/shard_map/while
  288.5 5.5 %copy-start.12 = (bf16[2,1152,1024]{2,1,0:T(8,128)(2,1)S(1)}, bf16[2,1152,1024]{2,1,0:T(8,128)(2,1)}, u32[]{:S(2)}) copy-start(bf16[2,1152,1024]{2,1,0:T(8,128)(2,1)} %get-tuple-element.399) | copy-start | bytes 14155780 | tf_op jit(solution)/shard_map/while
  288.5 5.5 %copy-start.13 = (bf16[2048,1024]{1,0:T(8,128)(2,1)S(1)}, bf16[2048,1024]{1,0:T(8,128)(2,1)}, u32[]{:S(2)}) copy-start(bf16[2048,1024]{1,0:T(8,128)(2,1)} %get-tuple-element.398) | copy-start | bytes 12582916 | tf_op jit(solution)/shard_map/while
  311.7 17.9 %copy-start.9 = (f32[2,128]{1,0:T(2,128)}, f32[2,128]{1,0:T(2,128)S(1)}, u32[]{:S(2)}) copy-start(f32[2,128]{1,0:T(2,128)S(1)} %add_subtract_fusion) | copy-start | bytes 3076
Sparse Core Ops, SparseCore 0:
  152.5 68.0 all-gather.2
  222.7 51.0 all-gather.4

commit v10 on v7

--- a/solution.py
+++ b/solution.py
@@ -178,9 +178,17 @@
 
     def model_exit(which, residual, local_slot, returned):
         returned = returned.reshape(slots, width)
-        picker = (local_slot[..., None] == slot_ids[None, None, :]).astype(jnp.bfloat16)
-        picked = jnp.einsum("tks,sd->tkd", picker, returned, preferred_element_type=jnp.float32)
-        mixture = jnp.sum(gate_probs[which][..., None] * picked, axis=1)
+        blend = jnp.sum(
+            jnp.where(
+                local_slot[..., None] == slot_ids[None, None, :], gate_probs[which][..., None], 0.0
+            ),
+            axis=1,
+        )
+        blend_high = blend.astype(jnp.bfloat16)
+        blend_low = (blend - blend_high.astype(jnp.float32)).astype(jnp.bfloat16)
+        mixture = jnp.dot(blend_high, returned, preferred_element_type=jnp.float32) + jnp.dot(
+            blend_low, returned, preferred_element_type=jnp.float32
+        )
         final = root_norm(
             residual.astype(jnp.float32) + RESIDUAL_SCALE * mixture, norm_gains[which, 2]
         ).astype(jnp.bfloat16)

time: 336 us -> 334 us (level)
  matrix products: 78.7 us -> 72.7 us
    dot_general x2 -> x4, matrix products: 8.36 us -> 3.49 us  [the longest x2 2.45 us: model_exit(): jnp.dot(blend_low, returned, preferred_element_type=jnp.float32)]
where the time goes in v10:
time: 334 us
  waiting for transfers between devices  159 us (48%)
  matrix products  72.7 us (22%)
  blocking collectives  27.7 us (8%)
  starting transfers between devices  25.4 us (8%)
  other arithmetic  21.6 us (6%)
  between operations  14.8 us (4%)
  local copies, waits for them, and re-layouts  10.2 us (3%)
    all_to_all x3, waiting for transfers between devices, exchange(): lax.all_to_all(blocks, 'exp', split_axis=0, concat_axis=0, tiled=True)  114 us
    all_gather x1, waiting for transfers between devices, per_device(): gathered_second = lax.all_gather(final_second, 'exp', axis=0, tiled=True)  31.1 us
    dot_general x4, matrix products, one_block(): jnp.einsum('td,vd->tv', row_block, head, preferred_element_type=jnp.float32)  30.7 us
    all_to_all x3, starting transfers between devices, exchange(): lax.all_to_all(blocks, 'exp', split_axis=0, concat_axis=0, tiled=True)  24.9 us
    all_to_all x1, blocking collectives, per_device(): lax.all_to_all(dense_totals.reshape(devices, per_device_seqs), ('req', 'e...  15 us
    all_gather x1, waiting for transfers between devices, per_device(): gathered_first = lax.all_gather(final_first, 'exp', axis=0, tiled=True)  13.6 us
    all_to_all x1, blocking collectives, per_device(): gathered = lax.all_to_all(stacked, 'exp', 0, 0, tiled=True)  12.7 us
    dot_general x2, matrix products, model_experts(): jnp.einsum('slcd,ldf->slcf', inputs, expert_in[which], preferred_element_...  10.9 us
  transfers between devices with their start and end apart: 5, of which 5 were waited for; matrix products, arithmetic and copies ran while one was open for 15% of the time, Pallas kernels for 0%

profile of v10, /device:TPU:1, one launch (start us, length us, event | category | flops | bytes accessed | tf_op | source)
XLA Modules:
  0.0 333.6 jit_solution(2011690977276274307)
XLA Ops:
  9.8 3.1 fusion.20
  16.4 2.2 multiply_reduce_fusion.3
  18.7 4.9 %fusion.27 = bf16[1280,1024]{1,0:T(8,128)(2,1)} fusion(s32[1024]{0:T(1024)S(1)} %multiply_add_fusion.1, bf16[128,1024]{1,0:T(8,128)(2,1)S(1)} %multiply_convert_fusion.3), kind=kOutput, calls=%fused_computation.43 | convolution fusion | flops 2686976000 | bytes 2887680 | tf_op jit(solution)/shard_map/ps,pd->sd/dot_general | solution.py:161
  23.6 9.6 %all-to-all-start = ((bf16[32,40,1024]{2,1,0:T(8,128)(2,1)}), bf16[32,40,1024]{2,1,0:T(8,128)(2,1)}, u32[]{:S(2)}, u32[]{:S(2)}) async-start(bf16[32,40,1024]{2,1,0:T(8,128)(2,1)} %bitcast.26), calls=%async_computation | async-start | bytes 5242880 | tf_op jit(solution)/shard_map/all_to_all | solution.py:198
  33.4 3.0 fusion.18
  40.1 2.2 multiply_reduce_fusion.2
  43.2 3.7 %fusion.26 = bf16[1280,1024]{1,0:T(8,128)(2,1)S(1)} fusion(s32[1024]{0:T(1024)S(1)} %multiply_add_fusion, bf16[128,1024]{1,0:T(8,128)(2,1)S(1)} %multiply_convert_fusion.2), kind=kOutput, calls=%fused_computation.42 | convolution fusion | flops 2686976000 | bytes 2887680 | tf_op jit(solution)/shard_map/ps,pd->sd/dot_general | solution.py:161
  46.9 20.3 %all-to-all-done = bf16[32,40,1024]{2,1,0:T(8,128)(2,1)} async-done(((bf16[32,40,1024]{2,1,0:T(8,128)(2,1)}), bf16[32,40,1024]{2,1,0:T(8,128)(2,1)}, u32[]{:S(2)}, u32[]{:S(2)}) %all-to-all-start) | async-done | bytes 2621472 | tf_op jit(solution)/shard_map/all_to_all | solution.py:198
  67.2 5.5 %convolution_bitcast_fusion = f32[32,1,40,1024]{3,2,0,1:T(8,128)S(1)} fusion(bf16[32,40,1024]{2,1,0:T(8,128)(2,1)} %all-to-all-done, bf16[2,1,1024,1024]{3,2,1,0:T(8,128)(2,1)} %param.25), kind=kOutput, calls=%fused_computation.53 | convolution fusion | flops 2684354560 | bytes 9961472 | tf_op jit(solution)/shard_map/slcd,ldf->slcf/dot_general | solution.py:168
  74.4 3.0 pad_maximum_fusion
  77.5 7.0 %all-to-all-start.1 = ((bf16[32,80,1024]{2,1,0:T(8,128)(2,1)}), bf16[32,80,1024]{2,1,0:T(8,128)(2,1)}, u32[]{:S(2)}, u32[]{:S(2)}) async-start(bf16[32,80,1024]{2,1,0:T(8,128)(2,1)} %pad_maximum_fusion), calls=%async_computation.1 | async-start | bytes 10485760 | tf_op jit(solution)/shard_map/all_to_all | solution.py:198
  86.7 59.8 %all-to-all-done.1 = bf16[32,80,1024]{2,1,0:T(8,128)(2,1)} async-done(((bf16[32,80,1024]{2,1,0:T(8,128)(2,1)}), bf16[32,80,1024]{2,1,0:T(8,128)(2,1)}, u32[]{:S(2)}, u32[]{:S(2)}) %all-to-all-start.1) | async-done | bytes 5242912 | tf_op jit(solution)/shard_map/all_to_all | solution.py:198
  146.4 2.0 slice.206
  150.5 5.4 %fusion.34 = f32[32,1,40,1024]{3,2,0,1:T(8,128)S(1)} fusion(bf16[32,80,1024]{2,1,0:T(8,128)(2,1)} %all-to-all-done.1, bf16[2,1,1024,1024]{3,2,1,0:T(8,128)(2,1)} %param.25), kind=kOutput, calls=%fused_computation.52 | convolution fusion | flops 2684354560 | bytes 9961472 | tf_op jit(solution)/shard_map/slcd,ldf->slcf/dot_general | solution.py:168
  156.0 3.3 convolution_convert_fusion
  159.3 8.2 %all-to-all-start.2 = ((bf16[32,40,1024]{2,1,0:T(8,128)(2,1)}), bf16[32,40,1024]{2,1,0:T(8,128)(2,1)S(1)}, u32[]{:S(2)}, u32[]{:S(2)}) async-start(bf16[32,40,1024]{2,1,0:T(8,128)(2,1)} %convolution_convert_fusion), calls=%async_computation.2 | async-start | bytes 5242880 | tf_op jit(solution)/shard_map/all_to_all | solution.py:198
  169.7 33.7 %all-to-all-done.2 = bf16[32,40,1024]{2,1,0:T(8,128)(2,1)S(1)} async-done(((bf16[32,40,1024]{2,1,0:T(8,128)(2,1)}), bf16[32,40,1024]{2,1,0:T(8,128)(2,1)S(1)}, u32[]{:S(2)}, u32[]{:S(2)}) %all-to-all-start.2) | async-done | bytes 2621472 | tf_op jit(solution)/shard_map/all_to_all | solution.py:198
  203.9 1.8 multiply_reduce_fusion
  206.6 13.6 %all-gather.3.cloned.1.call-done = bf16[4096,1024]{1,0:T(8,128)(2,1)} async-done(((bf16[128,1024]{1,0:T(8,128)(2,1)}), bf16[4096,1024]{1,0:T(8,128)(2,1)}) %all-gather.3.cloned.1.call-update) | async-done | bytes 8388624 | tf_op jit(solution)/shard_map/all_gather | solution.py:225
  220.2 23.2 %while.22 = (s32[]{:T(128)}, f32[2,3,2048]{2,1,0:T(4,128)S(1)}, s32[2]{0:T(128)S(1)}, bf16[4096,1024]{1,0:T(8,128)(2,1)}, bf16[2,1152,1024]{2,1,0:T(8,128)(2,1)}...) while((s32[]{:T(128)}, f32[2,3,2048]{2,1,0:T(4,128)S(1)}, ...), condition=%wide.region_19.20_spmd.clone, body=%wide.region_15.19_spmd.clone.sunk | while | flops 4848359424 | bytes 25542836 | solution.py:216
  221.5 7.7 %fusion.215 = (f32[2048]{0:T(1024)S(1)}, f32[2048,1152]{0,1:T(8,128)S(1)}) fusion(bf16[2,1152,1024]{2,1,0:T(8,128)(2,1)} %get-tuple-element.314, bf16[4096,1024]{1,0:T(8,128)(2,1)} %get-tuple-element.313, s32[]{:T(128)S(6)} %select_n.53), kind=kOutput, calls=%fused_computation.234.clone.1 | convolution fusion | flops 4836554752 | bytes 15998980 | tf_op jit(solution)/shard_map/while/body/eval_jaxpr/td,vd->tv/dot_general | solution.py:208
  229.2 2.6 exponential_reduce_fusion.4
  233.1 7.7 %fusion.215 = (f32[2048]{0:T(1024)S(1)}, f32[2048,1152]{0,1:T(8,128)S(1)}) fusion(bf16[2,1152,1024]{2,1,0:T(8,128)(2,1)} %get-tuple-element.314, bf16[4096,1024]{1,0:T(8,128)(2,1)} %get-tuple-element.313, s32[]{:T(128)S(6)} %select_n.53), kind=kOutput, calls=%fused_computation.234.clone.1 | convolution fusion | flops 4836554752 | bytes 15998980 | tf_op jit(solution)/shard_map/while/body/eval_jaxpr/td,vd->tv/dot_general | solution.py:208
  240.8 2.6 exponential_reduce_fusion.4
  243.5 31.1 %all-gather.5.cloned.1.call-done = bf16[4096,1024]{1,0:T(8,128)(2,1)} async-done(((bf16[128,1024]{1,0:T(8,128)(2,1)}), bf16[4096,1024]{1,0:T(8,128)(2,1)}) %all-gather.5.cloned.1.call-update) | async-done | bytes 8388624 | tf_op jit(solution)/shard_map/all_gather | solution.py:228
  274.6 23.1 %while.23 = (s32[]{:T(128)}, f32[2,3,2048]{2,1,0:T(4,128)S(1)}, s32[2]{0:T(128)S(1)}, bf16[4096,1024]{1,0:T(8,128)(2,1)}, bf16[2,1152,1024]{2,1,0:T(8,128)(2,1)}...) while((s32[]{:T(128)}, f32[2,3,2048]{2,1,0:T(4,128)S(1)}, ...), condition=%wide.region_26.27_spmd.clone, body=%wide.region_22.26_spmd.clone.sunk | while | flops 4848359424 | bytes 25542836 | solution.py:216
  275.9 7.7 %fusion.217 = (f32[2048]{0:T(1024)S(1)}, f32[2048,1152]{0,1:T(8,128)S(1)}) fusion(bf16[2,1152,1024]{2,1,0:T(8,128)(2,1)} %get-tuple-element.284, bf16[4096,1024]{1,0:T(8,128)(2,1)} %get-tuple-element.283, s32[]{:T(128)S(6)} %select_n.54), kind=kOutput, calls=%fused_computation.235.clone.1 | convolution fusion | flops 4836554752 | bytes 15998980 | tf_op jit(solution)/shard_map/while/body/eval_jaxpr/td,vd->tv/dot_general | solution.py:208
  283.5 2.6 exponential_reduce_fusion.5
  287.4 7.7 %fusion.217 = (f32[2048]{0:T(1024)S(1)}, f32[2048,1152]{0,1:T(8,128)S(1)}) fusion(bf16[2,1152,1024]{2,1,0:T(8,128)(2,1)} %get-tuple-element.284, bf16[4096,1024]{1,0:T(8,128)(2,1)} %get-tuple-element.283, s32[]{:T(128)S(6)} %select_n.54), kind=kOutput, calls=%fused_computation.235.clone.1 | convolution fusion | flops 4836554752 | bytes 15998980 | tf_op jit(solution)/shard_map/while/body/eval_jaxpr/td,vd->tv/dot_general | solution.py:208
  295.1 2.6 exponential_reduce_fusion.5
  297.9 12.7 %all_to_all.29 = f32[32,3,2,128]{3,2,1,0:T(2,128)S(1)} all-to-all(f32[32,3,2,128]{3,2,1,0:T(2,128)S(1)} %copy.106), channel_id=1, replica_groups=mesh['req'=4,'exp'=32] {'exp'}, dimensions={0} | all-to-all | bytes 196608 | tf_op jit(solution)/shard_map/all_to_all | solution.py:232
  311.1 15.0 %all_to_all.30 = f32[128,1,4]{2,1,0:T(1,128)S(1)} all-to-all(f32[128,1,4]{2,1,0:T(1,128)S(1)} %bitcast.304), channel_id=1, replica_groups=mesh['req'=4,'exp'=32] {'req','exp'}, dimensions={0} | all-to-all | bytes 4096 | tf_op jit(solution)/shard_map/all_to_all | solution.py:250
  (146 shorter events, 24.2 us)
Async XLA Ops:
  8.4 4.6 %copy-start.21 = (s32[1,4]{1,0:T(1,128)S(1)}, s32[1,4]{1,0:T(1,128)}, u32[]{:S(2)}) copy-start(s32[1,4]{1,0:T(1,128)} %param.17) | copy-start | bytes 52
  13.3 0.5 copy-start.15
  14.0 1.1 copy-start.13
  14.7 1.7 copy-start.1
  15.8 2.9 copy-start.10
  23.6 9.8 %copy-start.2 = (bf16[2,128,1024]{2,1,0:T(8,128)(2,1)S(1)}, bf16[2,128,1024]{2,1,0:T(8,128)(2,1)}, u32[]{:S(2)}) copy-start(bf16[2,128,1024]{2,1,0:T(8,128)(2,1)} %param.16) | copy-start | bytes 1572868
  23.6 43.6 %all-to-all-start = ((bf16[32,40,1024]{2,1,0:T(8,128)(2,1)}), bf16[32,40,1024]{2,1,0:T(8,128)(2,1)}, u32[]{:S(2)}, u32[]{:S(2)}) async-start(bf16[32,40,1024]{2,1,0:T(8,128)(2,1)} %bitcast.26), calls=%async_computation | async-start | bytes 5242880 | tf_op jit(solution)/shard_map/all_to_all | solution.py:198
  37.1 5.2 %copy-start.8 = (f32[1024]{0:T(1024)}, f32[1024]{0:T(1024)S(1)}, u32[]{:S(2)}) copy-start(f32[1024]{0:T(1024)S(1)} %fusion.99) | copy-start | bytes 12292
  37.9 1.2 copy-start.4
  39.1 1.0 copy-start.3
  39.1 4.0 %copy-start.7 = (f32[1,1,1024]{2,0,1:T(1,128)S(1)}, f32[1,1,1024]{2,0,1:T(1,128)}, u32[]{:S(2)}) copy-start(f32[1,1,1024]{2,0,1:T(1,128)} %get-tuple-element.149) | copy-start | bytes 12292
  42.3 0.8 copy-start
  67.2 5.5 %copy-start.19 = (bf16[2,1,512,1024]{3,2,1,0:T(8,128)(2,1)S(1)}, bf16[2,1,512,1024]{3,2,1,0:T(8,128)(2,1)}, u32[]{:S(2)}) copy-start(bf16[2,1,512,1024]{3,2,1,0:T(8,128)(2,1)} %param.26) | copy-start | bytes 6291460
  77.5 7.3 %copy-start.11 = (f32[1024]{0:T(1024)S(1)}, f32[1024]{0:T(1024)}, u32[]{:S(2)}) copy-start(f32[1024]{0:T(1024)} %copy-done.10) | copy-start | bytes 12292
  77.5 7.4 %copy-start.14 = (f32[2,128,8]{1,2,0:T(8,128)S(1)}, f32[2,128,8]{1,2,0:T(8,128)}, u32[]{:S(2)}) copy-start(f32[2,128,8]{1,2,0:T(8,128)} %param.20) | copy-start | bytes 24580
  77.5 69.0 %all-to-all-start.1 = ((bf16[32,80,1024]{2,1,0:T(8,128)(2,1)}), bf16[32,80,1024]{2,1,0:T(8,128)(2,1)}, u32[]{:S(2)}, u32[]{:S(2)}) async-start(bf16[32,80,1024]{2,1,0:T(8,128)(2,1)} %pad_maximum_fusion), calls=%async_computation.1 | async-start | bytes 10485760 | tf_op jit(solution)/shard_map/all_to_all | solution.py:198
  84.5 135.7 %all-gather.3.cloned.1.call-start = ((), (), s32[]{:S(2)}) async-start(), calls=%async_computation.5 | async-start | bytes 8650752 | tf_op jit(solution)/shard_map/all_gather | solution.py:225
  148.4 1.3 copy-start.6
  150.5 5.5 %copy-start.20 = (bf16[2,1,512,1024]{3,2,1,0:T(8,128)(2,1)S(1)}, bf16[2,1,512,1024]{3,2,1,0:T(8,128)(2,1)}, u32[]{:S(2)}) copy-start(bf16[2,1,512,1024]{3,2,1,0:T(8,128)(2,1)} %param.26) | copy-start | bytes 6291460
  159.3 8.5 %copy-start.9 = (f32[1024]{0:T(1024)S(1)}, f32[1024]{0:T(1024)}, u32[]{:S(2)}) copy-start(f32[1024]{0:T(1024)} %copy-done.8) | copy-start | bytes 12292
  159.3 44.1 %all-to-all-start.2 = ((bf16[32,40,1024]{2,1,0:T(8,128)(2,1)}), bf16[32,40,1024]{2,1,0:T(8,128)(2,1)S(1)}, u32[]{:S(2)}, u32[]{:S(2)}) async-start(bf16[32,40,1024]{2,1,0:T(8,128)(2,1)} %convolution_convert_fusion), calls=%async_computation.2 | async-start | bytes 5242880 | tf_op jit(solution)/shard_map/all_to_all | solution.py:198
  167.5 107.0 %all-gather.5.cloned.1.call-start = ((), (), s32[]{:S(2)}) async-start(), calls=%async_computation.6 | async-start | bytes 8650752 | tf_op jit(solution)/shard_map/all_gather | solution.py:228
  203.4 2.3 copy-start.5
  203.4 3.1 copy-start.12
  274.6 36.2 %copy-start.16 = (s32[128]{0:T(128)S(1)}, s32[128]{0:T(128)}, u32[]{:S(2)}) copy-start(s32[128]{0:T(128)} %copy-done.15) | copy-start | bytes 1540
  274.6 36.3 %copy-start.18 = (s32[4]{0:T(128)S(1)}, s32[4]{0:T(128)}, u32[]{:S(2)}) copy-start(s32[4]{0:T(128)} %param.21) | copy-start | bytes 52
  310.8 16.0 %copy-start.17 = (f32[2,128]{1,0:T(2,128)}, f32[2,128]{1,0:T(2,128)S(1)}, u32[]{:S(2)}) copy-start(f32[2,128]{1,0:T(2,128)S(1)} %add_subtract_fusion) | copy-start | bytes 3076
Sparse Core Ops, SparseCore 0:
  150.7 69.5 all-gather.2
  222.5 52.0 all-gather.4

commit v11 on v10

--- a/solution.py
+++ b/solution.py
@@ -157,10 +157,15 @@
         rank_slot = jnp.sum((running - 1.0) * onehot.astype(jnp.float32), axis=1).astype(jnp.int32)
         local_slot = (flat_routes * CAP + rank_slot).reshape(token_count, TOP)
         chooser = (local_slot.reshape(pairs)[:, None] == slot_ids[None, :]).astype(jnp.bfloat16)
-        repeated = jnp.repeat(moe_in, TOP, axis=0)
-        outgoing = jnp.einsum(
-            "ps,pd->sd", chooser, repeated, preferred_element_type=jnp.float32
+        owner = (pair_ids[:, None] // TOP == jnp.arange(token_count, dtype=jnp.int32)[None, :]).astype(
+            jnp.bfloat16
+        )
+        slot_token = jnp.einsum(
+            "ps,pt->st", chooser, owner, preferred_element_type=jnp.float32
         ).astype(jnp.bfloat16)
+        outgoing = jnp.dot(slot_token, moe_in, preferred_element_type=jnp.float32).astype(
+            jnp.bfloat16
+        )
         return residual, local_slot, outgoing.reshape(groups, local_count * CAP, width)
 
     def model_experts(which, arrived):

time: 334 us -> 340 us (1.018); the launches traced: 334 us -> 334 us
  no operation moved by 1% of the time
where the time goes in v11:
time: 340 us; the launch traced here: 334 us
  waiting for transfers between devices  160 us (47%)
  matrix products  73.6 us (22%)
  blocking collectives  27.7 us (8%)
  starting transfers between devices  25.5 us (8%)
  other arithmetic  21.4 us (6%)
  between operations  15.1 us (4%)
  local copies, waits for them, and re-layouts  8.05 us (2%)
    all_to_all x3, waiting for transfers between devices, exchange(): lax.all_to_all(blocks, 'exp', split_axis=0, concat_axis=0, tiled=True)  115 us
    all_gather x1, waiting for transfers between devices, per_device(): gathered_second = lax.all_gather(final_second, 'exp', axis=0, tiled=True)  31 us
    dot_general x4, matrix products, one_block(): jnp.einsum('td,vd->tv', row_block, head, preferred_element_type=jnp.float32)  30.8 us
    all_to_all x3, starting transfers between devices, exchange(): lax.all_to_all(blocks, 'exp', split_axis=0, concat_axis=0, tiled=True)  25 us
    all_to_all x1, blocking collectives, per_device(): lax.all_to_all(dense_totals.reshape(devices, per_device_seqs), ('req', 'e...  15 us
    all_gather x1, waiting for transfers between devices, per_device(): gathered_first = lax.all_gather(final_first, 'exp', axis=0, tiled=True)  13.9 us
    all_to_all x1, blocking collectives, per_device(): gathered = lax.all_to_all(stacked, 'exp', 0, 0, tiled=True)  12.7 us
    dot_general x2, matrix products, model_experts(): jnp.einsum('slcd,ldf->slcf', inputs, expert_in[which], preferred_element_...  10.9 us
  transfers between devices with their start and end apart: 5, of which 5 were waited for; matrix products, arithmetic and copies ran while one was open for 15% of the time, Pallas kernels for 0%

profile of v11, /device:TPU:1, one launch (start us, length us, event | category | flops | bytes accessed | tf_op | source)
XLA Modules:
  0.0 333.7 jit_solution(4243663570507734706)
XLA Ops:
  9.2 3.1 fusion.20
  16.4 2.2 multiply_reduce_fusion.3
  18.6 4.5 %convolution_convert_fusion.1 = bf16[1280,1024]{1,0:T(8,128)(2,1)} fusion(s32[1024]{0:T(1024)S(1)} %multiply_add_fusion.1, f32[128,1024]{1,0:T(8,128)S(1)} %get-tuple-element.163, f32[1024]{0:T(1024)S(1)} %bitcast.305, f32[128]{0:T(128)S(1)} %add_rsqrt_fusion.4, s32[1024]{0:T(1024)S(1)} %get-tuple-element.170), kind=kOutput, calls=%fused_computation.43 | convolution fusion | flops 674398208 | bytes 3158528 | tf_op jit(solution)/shard_map/dot_general | solution.py:166
  23.1 9.8 %all-to-all-start = ((bf16[32,40,1024]{2,1,0:T(8,128)(2,1)}), bf16[32,40,1024]{2,1,0:T(8,128)(2,1)}, u32[]{:S(2)}, u32[]{:S(2)}) async-start(bf16[32,40,1024]{2,1,0:T(8,128)(2,1)} %bitcast.25), calls=%async_computation | async-start | bytes 5242880 | tf_op jit(solution)/shard_map/all_to_all | solution.py:203
  33.0 3.0 fusion.18
  38.5 2.9 multiply_reduce_fusion.2
  41.4 4.0 %convolution_convert_fusion = bf16[1280,1024]{1,0:T(8,128)(2,1)S(1)} fusion(s32[1024]{0:T(1024)S(1)} %get-tuple-element.171, f32[128,1024]{1,0:T(8,128)} %get-tuple-element.161, f32[1024]{0:T(1024)S(1)} %bitcast.303, f32[128]{0:T(128)S(1)} %add_rsqrt_fusion.2, s32[1024]{0:T(1024)S(1)} %get-tuple-element.170), kind=kOutput, calls=%fused_computation.42 | convolution fusion | flops 674398208 | bytes 3158528 | tf_op jit(solution)/shard_map/dot_general | solution.py:166
  45.4 21.4 %all-to-all-done = bf16[32,40,1024]{2,1,0:T(8,128)(2,1)} async-done(((bf16[32,40,1024]{2,1,0:T(8,128)(2,1)}), bf16[32,40,1024]{2,1,0:T(8,128)(2,1)}, u32[]{:S(2)}, u32[]{:S(2)}) %all-to-all-start) | async-done | bytes 2621472 | tf_op jit(solution)/shard_map/all_to_all | solution.py:203
  66.8 5.5 %convolution_bitcast_fusion = f32[32,1,40,1024]{3,2,0,1:T(8,128)S(1)} fusion(bf16[32,40,1024]{2,1,0:T(8,128)(2,1)} %all-to-all-done, bf16[2,1,1024,1024]{3,2,1,0:T(8,128)(2,1)} %param.25), kind=kOutput, calls=%fused_computation.53 | convolution fusion | flops 2684354560 | bytes 9961472 | tf_op jit(solution)/shard_map/slcd,ldf->slcf/dot_general | solution.py:173
  74.0 2.9 pad_maximum_fusion
  77.0 7.1 %all-to-all-start.1 = ((bf16[32,80,1024]{2,1,0:T(8,128)(2,1)}), bf16[32,80,1024]{2,1,0:T(8,128)(2,1)}, u32[]{:S(2)}, u32[]{:S(2)}) async-start(bf16[32,80,1024]{2,1,0:T(8,128)(2,1)} %pad_maximum_fusion), calls=%async_computation.1 | async-start | bytes 10485760 | tf_op jit(solution)/shard_map/all_to_all | solution.py:203
  86.2 59.8 %all-to-all-done.1 = bf16[32,80,1024]{2,1,0:T(8,128)(2,1)} async-done(((bf16[32,80,1024]{2,1,0:T(8,128)(2,1)}), bf16[32,80,1024]{2,1,0:T(8,128)(2,1)}, u32[]{:S(2)}, u32[]{:S(2)}) %all-to-all-start.1) | async-done | bytes 5242912 | tf_op jit(solution)/shard_map/all_to_all | solution.py:203
  146.0 2.0 slice.206
  150.1 5.5 %fusion.32 = f32[32,1,40,1024]{3,2,0,1:T(8,128)S(1)} fusion(bf16[32,80,1024]{2,1,0:T(8,128)(2,1)} %all-to-all-done.1, bf16[2,1,1024,1024]{3,2,1,0:T(8,128)(2,1)} %param.25), kind=kOutput, calls=%fused_computation.52 | convolution fusion | flops 2684354560 | bytes 9961472 | tf_op jit(solution)/shard_map/slcd,ldf->slcf/dot_general | solution.py:173
  155.5 3.3 convolution_convert_fusion.2
  158.9 8.1 %all-to-all-start.2 = ((bf16[32,40,1024]{2,1,0:T(8,128)(2,1)}), bf16[32,40,1024]{2,1,0:T(8,128)(2,1)S(1)}, u32[]{:S(2)}, u32[]{:S(2)}) async-start(bf16[32,40,1024]{2,1,0:T(8,128)(2,1)} %convolution_convert_fusion.2), calls=%async_computation.2 | async-start | bytes 5242880 | tf_op jit(solution)/shard_map/all_to_all | solution.py:203
  169.1 33.5 %all-to-all-done.2 = bf16[32,40,1024]{2,1,0:T(8,128)(2,1)S(1)} async-done(((bf16[32,40,1024]{2,1,0:T(8,128)(2,1)}), bf16[32,40,1024]{2,1,0:T(8,128)(2,1)S(1)}, u32[]{:S(2)}, u32[]{:S(2)}) %all-to-all-start.2) | async-done | bytes 2621472 | tf_op jit(solution)/shard_map/all_to_all | solution.py:203
  203.2 1.8 multiply_reduce_fusion
  205.8 13.9 %all-gather.3.cloned.1.call-done = bf16[4096,1024]{1,0:T(8,128)(2,1)} async-done(((bf16[128,1024]{1,0:T(8,128)(2,1)}), bf16[4096,1024]{1,0:T(8,128)(2,1)}) %all-gather.3.cloned.1.call-update) | async-done | bytes 8388624 | tf_op jit(solution)/shard_map/all_gather | solution.py:230
  219.7 23.2 %while.22 = (s32[]{:T(128)}, f32[2,3,2048]{2,1,0:T(4,128)S(1)}, s32[2]{0:T(128)S(1)}, bf16[4096,1024]{1,0:T(8,128)(2,1)}, bf16[2,1152,1024]{2,1,0:T(8,128)(2,1)}...) while((s32[]{:T(128)}, f32[2,3,2048]{2,1,0:T(4,128)S(1)}, ...), condition=%wide.region_19.20_spmd.clone, body=%wide.region_15.19_spmd.clone.sunk | while | flops 4848359424 | bytes 25542836 | solution.py:221
  221.0 7.7 %fusion.222 = (f32[2048]{0:T(1024)S(1)}, f32[2048,1152]{0,1:T(8,128)S(1)}) fusion(bf16[2,1152,1024]{2,1,0:T(8,128)(2,1)} %get-tuple-element.316, bf16[4096,1024]{1,0:T(8,128)(2,1)} %get-tuple-element.315, s32[]{:T(128)S(6)} %select_n.68), kind=kOutput, calls=%fused_computation.246.clone.1 | convolution fusion | flops 4836554752 | bytes 15998980 | tf_op jit(solution)/shard_map/while/body/eval_jaxpr/td,vd->tv/dot_general | solution.py:213
  228.7 2.6 exponential_reduce_fusion.4
  232.6 7.7 %fusion.222 = (f32[2048]{0:T(1024)S(1)}, f32[2048,1152]{0,1:T(8,128)S(1)}) fusion(bf16[2,1152,1024]{2,1,0:T(8,128)(2,1)} %get-tuple-element.316, bf16[4096,1024]{1,0:T(8,128)(2,1)} %get-tuple-element.315, s32[]{:T(128)S(6)} %select_n.68), kind=kOutput, calls=%fused_computation.246.clone.1 | convolution fusion | flops 4836554752 | bytes 15998980 | tf_op jit(solution)/shard_map/while/body/eval_jaxpr/td,vd->tv/dot_general | solution.py:213
  240.3 2.6 exponential_reduce_fusion.4
  243.1 31.0 %all-gather.5.cloned.1.call-done = bf16[4096,1024]{1,0:T(8,128)(2,1)} async-done(((bf16[128,1024]{1,0:T(8,128)(2,1)}), bf16[4096,1024]{1,0:T(8,128)(2,1)}) %all-gather.5.cloned.1.call-update) | async-done | bytes 8388624 | tf_op jit(solution)/shard_map/all_gather | solution.py:233
  274.2 23.2 %while.23 = (s32[]{:T(128)}, f32[2,3,2048]{2,1,0:T(4,128)S(1)}, s32[2]{0:T(128)S(1)}, bf16[4096,1024]{1,0:T(8,128)(2,1)}, bf16[2,1152,1024]{2,1,0:T(8,128)(2,1)}...) while((s32[]{:T(128)}, f32[2,3,2048]{2,1,0:T(4,128)S(1)}, ...), condition=%wide.region_26.27_spmd.clone, body=%wide.region_22.26_spmd.clone.sunk | while | flops 4848359424 | bytes 25542836 | solution.py:221
  275.4 7.7 %fusion.224 = (f32[2048]{0:T(1024)S(1)}, f32[2048,1152]{0,1:T(8,128)S(1)}) fusion(bf16[2,1152,1024]{2,1,0:T(8,128)(2,1)} %get-tuple-element.286, bf16[4096,1024]{1,0:T(8,128)(2,1)} %get-tuple-element.285, s32[]{:T(128)S(6)} %select_n.69), kind=kOutput, calls=%fused_computation.247.clone.1 | convolution fusion | flops 4836554752 | bytes 15998980 | tf_op jit(solution)/shard_map/while/body/eval_jaxpr/td,vd->tv/dot_general | solution.py:213
  283.1 2.6 exponential_reduce_fusion.5
  287.0 7.7 %fusion.224 = (f32[2048]{0:T(1024)S(1)}, f32[2048,1152]{0,1:T(8,128)S(1)}) fusion(bf16[2,1152,1024]{2,1,0:T(8,128)(2,1)} %get-tuple-element.286, bf16[4096,1024]{1,0:T(8,128)(2,1)} %get-tuple-element.285, s32[]{:T(128)S(6)} %select_n.69), kind=kOutput, calls=%fused_computation.247.clone.1 | convolution fusion | flops 4836554752 | bytes 15998980 | tf_op jit(solution)/shard_map/while/body/eval_jaxpr/td,vd->tv/dot_general | solution.py:213
  294.7 2.6 exponential_reduce_fusion.5
  297.6 12.7 %all_to_all.29 = f32[32,3,2,128]{3,2,1,0:T(2,128)S(1)} all-to-all(f32[32,3,2,128]{3,2,1,0:T(2,128)S(1)} %copy.106), channel_id=1, replica_groups=mesh['req'=4,'exp'=32] {'exp'}, dimensions={0} | all-to-all | bytes 196608 | tf_op jit(solution)/shard_map/all_to_all | solution.py:237
  310.8 15.0 %all_to_all.30 = f32[128,1,4]{2,1,0:T(1,128)S(1)} all-to-all(f32[128,1,4]{2,1,0:T(1,128)S(1)} %bitcast.298), channel_id=1, replica_groups=mesh['req'=4,'exp'=32] {'req','exp'}, dimensions={0} | all-to-all | bytes 4096 | tf_op jit(solution)/shard_map/all_to_all | solution.py:255
  (124 shorter events, 21.9 us)
Async XLA Ops:
  8.4 4.0 %copy-start.11 = (s32[1,4]{1,0:T(1,128)S(1)}, s32[1,4]{1,0:T(1,128)}, u32[]{:S(2)}) copy-start(s32[1,4]{1,0:T(1,128)} %param.17) | copy-start | bytes 52
  12.7 1.7 copy-start.5
  13.2 1.1 copy-start.3
  14.4 2.1 copy-start
  23.1 43.7 %all-to-all-start = ((bf16[32,40,1024]{2,1,0:T(8,128)(2,1)}), bf16[32,40,1024]{2,1,0:T(8,128)(2,1)}, u32[]{:S(2)}, u32[]{:S(2)}) async-start(bf16[32,40,1024]{2,1,0:T(8,128)(2,1)} %bitcast.25), calls=%async_computation | async-start | bytes 5242880 | tf_op jit(solution)/shard_map/all_to_all | solution.py:203
  37.5 1.0 copy-start.1
  66.8 5.5 %copy-start.9 = (bf16[2,1,512,1024]{3,2,1,0:T(8,128)(2,1)S(1)}, bf16[2,1,512,1024]{3,2,1,0:T(8,128)(2,1)}, u32[]{:S(2)}) copy-start(bf16[2,1,512,1024]{3,2,1,0:T(8,128)(2,1)} %param.26) | copy-start | bytes 6291460
  77.0 7.5 %copy-start.4 = (f32[2,128,8]{1,2,0:T(8,128)S(1)}, f32[2,128,8]{1,2,0:T(8,128)}, u32[]{:S(2)}) copy-start(f32[2,128,8]{1,2,0:T(8,128)} %param.20) | copy-start | bytes 24580
  77.0 69.0 %all-to-all-start.1 = ((bf16[32,80,1024]{2,1,0:T(8,128)(2,1)}), bf16[32,80,1024]{2,1,0:T(8,128)(2,1)}, u32[]{:S(2)}, u32[]{:S(2)}) async-start(bf16[32,80,1024]{2,1,0:T(8,128)(2,1)} %pad_maximum_fusion), calls=%async_computation.1 | async-start | bytes 10485760 | tf_op jit(solution)/shard_map/all_to_all | solution.py:203
  84.0 135.7 %all-gather.3.cloned.1.call-start = ((), (), s32[]{:S(2)}) async-start(), calls=%async_computation.5 | async-start | bytes 8650752 | tf_op jit(solution)/shard_map/all_gather | solution.py:230
  150.0 5.5 %copy-start.10 = (bf16[2,1,512,1024]{3,2,1,0:T(8,128)(2,1)S(1)}, bf16[2,1,512,1024]{3,2,1,0:T(8,128)(2,1)}, u32[]{:S(2)}) copy-start(bf16[2,1,512,1024]{3,2,1,0:T(8,128)(2,1)} %param.26) | copy-start | bytes 6291460
  158.9 43.8 %all-to-all-start.2 = ((bf16[32,40,1024]{2,1,0:T(8,128)(2,1)}), bf16[32,40,1024]{2,1,0:T(8,128)(2,1)S(1)}, u32[]{:S(2)}, u32[]{:S(2)}) async-start(bf16[32,40,1024]{2,1,0:T(8,128)(2,1)} %convolution_convert_fusion.2), calls=%async_computation.2 | async-start | bytes 5242880 | tf_op jit(solution)/shard_map/all_to_all | solution.py:203
  167.0 107.2 %all-gather.5.cloned.1.call-start = ((), (), s32[]{:S(2)}) async-start(), calls=%async_computation.6 | async-start | bytes 8650752 | tf_op jit(solution)/shard_map/all_gather | solution.py:233
  202.7 3.1 copy-start.2
  274.1 36.3 %copy-start.6 = (s32[128]{0:T(128)S(1)}, s32[128]{0:T(128)}, u32[]{:S(2)}) copy-start(s32[128]{0:T(128)} %copy-done.5) | copy-start | bytes 1540
  274.1 36.4 %copy-start.8 = (s32[4]{0:T(128)S(1)}, s32[4]{0:T(128)}, u32[]{:S(2)}) copy-start(s32[4]{0:T(128)} %param.21) | copy-start | bytes 52
  310.4 16.0 %copy-start.7 = (f32[2,128]{1,0:T(2,128)}, f32[2,128]{1,0:T(2,128)S(1)}, u32[]{:S(2)}) copy-start(f32[2,128]{1,0:T(2,128)S(1)} %add_subtract_fusion) | copy-start | bytes 3076
Sparse Core Ops, SparseCore 0:
  150.2 69.5 all-gather.2
  222.0 52.0 all-gather.4

commit v12 on v10

--- a/solution.py
+++ b/solution.py
@@ -176,11 +176,13 @@
         ).astype(jnp.bfloat16)
         return produced.reshape(groups, local_count * CAP, width)
 
-    def model_exit(which, residual, local_slot, returned):
-        returned = returned.reshape(slots, width)
+    def model_exit(which, residual, local_slot, returned, stride=CAP):
+        returned = returned.reshape(-1, width)
+        row_of_slot = (local_slot // CAP) * stride + local_slot % CAP
+        row_ids = jnp.arange(returned.shape[0], dtype=jnp.int32)
         blend = jnp.sum(
             jnp.where(
-                local_slot[..., None] == slot_ids[None, None, :], gate_probs[which][..., None], 0.0
+                row_of_slot[..., None] == row_ids[None, None, :], gate_probs[which][..., None], 0.0
             ),
             axis=1,
         )
@@ -221,7 +223,7 @@
     produced_first = model_experts(0, exchange(outgoing_first))
     residual_second, slot_second, outgoing_second = model_entry(1)
     crossed = exchange(jnp.concatenate([produced_first, outgoing_second], axis=1))
-    final_first = model_exit(0, residual_first, slot_first, crossed[:, :row_span])
+    final_first = model_exit(0, residual_first, slot_first, crossed, stride=2 * row_span)
     gathered_first = lax.all_gather(final_first, "exp", axis=0, tiled=True)
     produced_second = model_experts(1, crossed[:, row_span:])
     final_second = model_exit(1, residual_second, slot_second, exchange(produced_second))

time: 334 us -> 346 us (1.036); the launches traced: 334 us -> 341 us
  matrix products: 72.7 us -> 80.3 us
  waiting for transfers between devices: 159 us -> 155 us
  other arithmetic: 21.6 us -> 25.2 us
where the time goes in v12:
time: 346 us; the launch traced here: 341 us
  waiting for transfers between devices  155 us (45%)
  matrix products  80.3 us (23%)
  blocking collectives  27.7 us (8%)
  starting transfers between devices  25.6 us (7%)
  other arithmetic  25.2 us (7%)
  between operations  15.2 us (4%)
  local copies, waits for them, and re-layouts  8.51 us (2%)
    all_to_all x3, waiting for transfers between devices, exchange(): lax.all_to_all(blocks, 'exp', split_axis=0, concat_axis=0, tiled=True)  111 us
    all_gather x1, waiting for transfers between devices, per_device(): gathered_second = lax.all_gather(final_second, 'exp', axis=0, tiled=True)  31 us
    dot_general x4, matrix products, one_block(): jnp.einsum('td,vd->tv', row_block, head, preferred_element_type=jnp.float32)  30.8 us
    all_to_all x3, starting transfers between devices, exchange(): lax.all_to_all(blocks, 'exp', split_axis=0, concat_axis=0, tiled=True)  25.1 us
    all_to_all x1, blocking collectives, per_device(): lax.all_to_all(dense_totals.reshape(devices, per_device_seqs), ('req', 'e...  15 us
    all_gather x1, waiting for transfers between devices, per_device(): gathered_first = lax.all_gather(final_first, 'exp', axis=0, tiled=True)  13.7 us
    all_to_all x1, blocking collectives, per_device(): gathered = lax.all_to_all(stacked, 'exp', 0, 0, tiled=True)  12.7 us
    dot_general x2, matrix products, model_experts(): jnp.einsum('slcd,ldf->slcf', inputs, expert_in[which], preferred_element_...  10.9 us
  transfers between devices with their start and end apart: 5, of which 5 were waited for; matrix products, arithmetic and copies ran while one was open for 15% of the time, Pallas kernels for 0%

profile of v12, /device:TPU:1, one launch (start us, length us, event | category | flops | bytes accessed | tf_op | source)
XLA Modules:
  0.0 340.8 jit_solution(6390050460015687412)
XLA Ops:
  9.8 3.1 fusion.20
  21.6 4.8 %fusion.27 = bf16[1280,1024]{1,0:T(8,128)(2,1)} fusion(s32[1024]{0:T(1024)S(1)} %multiply_add_fusion.1, bf16[128,1024]{1,0:T(8,128)(2,1)S(1)} %multiply_convert_fusion.3), kind=kOutput, calls=%fused_computation.43 | convolution fusion | flops 2686976000 | bytes 2887680 | tf_op jit(solution)/shard_map/ps,pd->sd/dot_general | solution.py:161
  26.5 9.8 %all-to-all-start = ((bf16[32,40,1024]{2,1,0:T(8,128)(2,1)}), bf16[32,40,1024]{2,1,0:T(8,128)(2,1)}, u32[]{:S(2)}, u32[]{:S(2)}) async-start(bf16[32,40,1024]{2,1,0:T(8,128)(2,1)} %bitcast.26), calls=%async_computation | async-start | bytes 5242880 | tf_op jit(solution)/shard_map/all_to_all | solution.py:200
  36.3 3.0 fusion.18
  43.2 2.2 multiply_reduce_fusion.2
  46.3 3.7 %fusion.26 = bf16[1280,1024]{1,0:T(8,128)(2,1)S(1)} fusion(s32[1024]{0:T(1024)S(1)} %multiply_add_fusion, bf16[128,1024]{1,0:T(8,128)(2,1)S(1)} %multiply_convert_fusion.2), kind=kOutput, calls=%fused_computation.42 | convolution fusion | flops 2686976000 | bytes 2887680 | tf_op jit(solution)/shard_map/ps,pd->sd/dot_general | solution.py:161
  50.0 20.1 %all-to-all-done = bf16[32,40,1024]{2,1,0:T(8,128)(2,1)} async-done(((bf16[32,40,1024]{2,1,0:T(8,128)(2,1)}), bf16[32,40,1024]{2,1,0:T(8,128)(2,1)}, u32[]{:S(2)}, u32[]{:S(2)}) %all-to-all-start) | async-done | bytes 2621472 | tf_op jit(solution)/shard_map/all_to_all | solution.py:200
  70.2 5.5 %convolution_bitcast_fusion = f32[32,1,40,1024]{3,2,0,1:T(8,128)S(1)} fusion(bf16[32,40,1024]{2,1,0:T(8,128)(2,1)} %all-to-all-done, bf16[2,1,1024,1024]{3,2,1,0:T(8,128)(2,1)} %param.25), kind=kOutput, calls=%fused_computation.53 | convolution fusion | flops 2684354560 | bytes 9961472 | tf_op jit(solution)/shard_map/slcd,ldf->slcf/dot_general | solution.py:168
  77.4 3.0 pad_maximum_fusion
  80.4 7.1 %all-to-all-start.1 = ((bf16[32,80,1024]{2,1,0:T(8,128)(2,1)}), bf16[32,80,1024]{2,1,0:T(8,128)(2,1)}, u32[]{:S(2)}, u32[]{:S(2)}) async-start(bf16[32,80,1024]{2,1,0:T(8,128)(2,1)} %pad_maximum_fusion), calls=%async_computation.1 | async-start | bytes 10485760 | tf_op jit(solution)/shard_map/all_to_all | solution.py:200
  88.1 4.3 %select_reduce_fusion.2 = f32[128,2560]{1,0:T(8,128)S(1)} fusion(f32[128,8]{1,0:T(8,128)S(1)} %copy.96, s32[128,8]{1,0:T(8,128)S(1)} %fusion.156), kind=kLoop, calls=%fused_computation.24 | loop fusion | flops 7536640 | bytes 1318912 | tf_op jit(solution)/shard_map/reduce_sum | solution.py:183
  92.4 57.0 %all-to-all-done.1 = bf16[32,80,1024]{2,1,0:T(8,128)(2,1)} async-done(((bf16[32,80,1024]{2,1,0:T(8,128)(2,1)}), bf16[32,80,1024]{2,1,0:T(8,128)(2,1)}, u32[]{:S(2)}, u32[]{:S(2)}) %all-to-all-start.1) | async-done | bytes 5242912 | tf_op jit(solution)/shard_map/all_to_all | solution.py:200
  149.4 3.3 fusion.120
  152.8 3.5 %multiply_reduce_fusion.1 = (f32[128]{0:T(128)S(1)}, f32[128,1024]{1,0:T(8,128)S(1)}) fusion(f32[128,1024]{1,0:T(8,128)S(1)} %get-tuple-element.163, f32[128,1024]{1,0:T(8,128)S(1)} %fusion.120, bf16[2560,1024]{1,0:T(8,128)(2,1)} %bitcast.58, f32[128,2560]{1,0:T(8,128)S(1)} %select_reduce_fusion.2), kind=kOutput, calls=%fused_computation.135 | convolution fusion | flops 673054592 | bytes 8126976 | tf_op jit(solution)/shard_map/dot_general | solution.py:191
  157.1 5.4 %fusion.34 = f32[32,1,40,1024]{3,2,0,1:T(8,128)S(1)} fusion(bf16[32,80,1024]{2,1,0:T(8,128)(2,1)} %all-to-all-done.1, bf16[2,1,1024,1024]{3,2,1,0:T(8,128)(2,1)} %param.25), kind=kOutput, calls=%fused_computation.52 | convolution fusion | flops 2684354560 | bytes 9961472 | tf_op jit(solution)/shard_map/slcd,ldf->slcf/dot_general | solution.py:168
  162.6 3.3 convolution_convert_fusion
  165.9 8.2 %all-to-all-start.2 = ((bf16[32,40,1024]{2,1,0:T(8,128)(2,1)}), bf16[32,40,1024]{2,1,0:T(8,128)(2,1)S(1)}, u32[]{:S(2)}, u32[]{:S(2)}) async-start(bf16[32,40,1024]{2,1,0:T(8,128)(2,1)} %convolution_convert_fusion), calls=%async_computation.2 | async-start | bytes 5242880 | tf_op jit(solution)/shard_map/all_to_all | solution.py:200
  176.3 33.6 %all-to-all-done.2 = bf16[32,40,1024]{2,1,0:T(8,128)(2,1)S(1)} async-done(((bf16[32,40,1024]{2,1,0:T(8,128)(2,1)}), bf16[32,40,1024]{2,1,0:T(8,128)(2,1)S(1)}, u32[]{:S(2)}, u32[]{:S(2)}) %all-to-all-start.2) | async-done | bytes 2621472 | tf_op jit(solution)/shard_map/all_to_all | solution.py:200
  213.1 13.7 %all-gather.3.cloned.1.call-done = bf16[4096,1024]{1,0:T(8,128)(2,1)} async-done(((bf16[128,1024]{1,0:T(8,128)(2,1)}), bf16[4096,1024]{1,0:T(8,128)(2,1)}) %all-gather.3.cloned.1.call-update) | async-done | bytes 8388624 | tf_op jit(solution)/shard_map/all_gather | solution.py:227
  226.8 23.2 %while.22 = (s32[]{:T(128)}, f32[2,3,2048]{2,1,0:T(4,128)S(1)}, s32[2]{0:T(128)S(1)}, bf16[4096,1024]{1,0:T(8,128)(2,1)}, bf16[2,1152,1024]{2,1,0:T(8,128)(2,1)}...) while((s32[]{:T(128)}, f32[2,3,2048]{2,1,0:T(4,128)S(1)}, ...), condition=%wide.region_19.20_spmd.clone, body=%wide.region_15.19_spmd.clone.sunk | while | flops 4848359424 | bytes 25542828 | solution.py:218
  228.1 7.7 %fusion.221 = (f32[2048]{0:T(1024)S(1)}, f32[2048,1152]{0,1:T(8,128)S(1)}) fusion(bf16[2,1152,1024]{2,1,0:T(8,128)(2,1)} %get-tuple-element.314, bf16[4096,1024]{1,0:T(8,128)(2,1)} %get-tuple-element.313, s32[]{:T(128)S(6)} %select_n.109), kind=kOutput, calls=%fused_computation.248.clone.1 | convolution fusion | flops 4836554752 | bytes 15998980 | tf_op jit(solution)/shard_map/while/body/eval_jaxpr/td,vd->tv/dot_general | solution.py:210
  235.8 2.6 exponential_reduce_fusion.4
  239.7 7.7 %fusion.221 = (f32[2048]{0:T(1024)S(1)}, f32[2048,1152]{0,1:T(8,128)S(1)}) fusion(bf16[2,1152,1024]{2,1,0:T(8,128)(2,1)} %get-tuple-element.314, bf16[4096,1024]{1,0:T(8,128)(2,1)} %get-tuple-element.313, s32[]{:T(128)S(6)} %select_n.109), kind=kOutput, calls=%fused_computation.248.clone.1 | convolution fusion | flops 4836554752 | bytes 15998980 | tf_op jit(solution)/shard_map/while/body/eval_jaxpr/td,vd->tv/dot_general | solution.py:210
  247.4 2.6 exponential_reduce_fusion.4
  250.2 31.0 %all-gather.5.cloned.1.call-done = bf16[4096,1024]{1,0:T(8,128)(2,1)} async-done(((bf16[128,1024]{1,0:T(8,128)(2,1)}), bf16[4096,1024]{1,0:T(8,128)(2,1)}) %all-gather.5.cloned.1.call-update) | async-done | bytes 8388624 | tf_op jit(solution)/shard_map/all_gather | solution.py:230
  281.2 23.2 %while.23 = (s32[]{:T(128)}, f32[2,3,2048]{2,1,0:T(4,128)S(1)}, s32[2]{0:T(128)S(1)}, bf16[4096,1024]{1,0:T(8,128)(2,1)}, bf16[2,1152,1024]{2,1,0:T(8,128)(2,1)}...) while((s32[]{:T(128)}, f32[2,3,2048]{2,1,0:T(4,128)S(1)}, ...), condition=%wide.region_26.27_spmd.clone, body=%wide.region_22.26_spmd.clone.sunk | while | flops 4848359424 | bytes 25542828 | solution.py:218
  282.4 7.7 %fusion.223 = (f32[2048]{0:T(1024)S(1)}, f32[2048,1152]{0,1:T(8,128)S(1)}) fusion(bf16[2,1152,1024]{2,1,0:T(8,128)(2,1)} %get-tuple-element.284, bf16[4096,1024]{1,0:T(8,128)(2,1)} %get-tuple-element.283, s32[]{:T(128)S(6)} %select_n.110), kind=kOutput, calls=%fused_computation.249.clone.1 | convolution fusion | flops 4836554752 | bytes 15998980 | tf_op jit(solution)/shard_map/while/body/eval_jaxpr/td,vd->tv/dot_general | solution.py:210
  290.2 2.6 exponential_reduce_fusion.5
  294.1 7.7 %fusion.223 = (f32[2048]{0:T(1024)S(1)}, f32[2048,1152]{0,1:T(8,128)S(1)}) fusion(bf16[2,1152,1024]{2,1,0:T(8,128)(2,1)} %get-tuple-element.284, bf16[4096,1024]{1,0:T(8,128)(2,1)} %get-tuple-element.283, s32[]{:T(128)S(6)} %select_n.110), kind=kOutput, calls=%fused_computation.249.clone.1 | convolution fusion | flops 4836554752 | bytes 15998980 | tf_op jit(solution)/shard_map/while/body/eval_jaxpr/td,vd->tv/dot_general | solution.py:210
  301.8 2.6 exponential_reduce_fusion.5
  304.6 12.7 %all_to_all.29 = f32[32,3,2,128]{3,2,1,0:T(2,128)S(1)} all-to-all(f32[32,3,2,128]{3,2,1,0:T(2,128)S(1)} %copy.106), channel_id=1, replica_groups=mesh['req'=4,'exp'=32] {'exp'}, dimensions={0} | all-to-all | bytes 196608 | tf_op jit(solution)/shard_map/all_to_all | solution.py:234
  317.8 15.0 %all_to_all.30 = f32[128,1,4]{2,1,0:T(1,128)S(1)} all-to-all(f32[128,1,4]{2,1,0:T(1,128)S(1)} %bitcast.306), channel_id=1, replica_groups=mesh['req'=4,'exp'=32] {'req','exp'}, dimensions={0} | all-to-all | bytes 4096 | tf_op jit(solution)/shard_map/all_to_all | solution.py:252
  (143 shorter events, 28.4 us)
Async XLA Ops:
  9.8 4.3 %copy-start.20 = (s32[1,4]{1,0:T(1,128)S(1)}, s32[1,4]{1,0:T(1,128)}, u32[]{:S(2)}) copy-start(s32[1,4]{1,0:T(1,128)} %param.17) | copy-start | bytes 52
  14.3 3.8 %copy-start.14 = (s32[128]{0:T(128)}, s32[128]{0:T(128)S(1)}, u32[]{:S(2)}) copy-start(s32[128]{0:T(128)S(1)} %convert_reduce_fusion) | copy-start | bytes 1540
  17.5 1.0 copy-start.1
  17.5 3.2 copy-start.12
  21.5 5.0 %copy-start.9 = (f32[1024]{0:T(1024)}, f32[1024]{0:T(1024)S(1)}, u32[]{:S(2)}) copy-start(f32[1024]{0:T(1024)S(1)} %fusion.100) | copy-start | bytes 12292
  26.5 43.7 %all-to-all-start = ((bf16[32,40,1024]{2,1,0:T(8,128)(2,1)}), bf16[32,40,1024]{2,1,0:T(8,128)(2,1)}, u32[]{:S(2)}, u32[]{:S(2)}) async-start(bf16[32,40,1024]{2,1,0:T(8,128)(2,1)} %bitcast.26), calls=%async_computation | async-start | bytes 5242880 | tf_op jit(solution)/shard_map/all_to_all | solution.py:200
  40.2 5.2 %copy-start.7 = (f32[1024]{0:T(1024)}, f32[1024]{0:T(1024)S(1)}, u32[]{:S(2)}) copy-start(f32[1024]{0:T(1024)S(1)} %fusion.99) | copy-start | bytes 12292
  41.2 1.0 copy-start.3
  42.2 1.0 copy-start.2
  42.2 4.0 %copy-start.6 = (f32[1,1,1024]{2,0,1:T(1,128)S(1)}, f32[1,1,1024]{2,0,1:T(1,128)}, u32[]{:S(2)}) copy-start(f32[1,1,1024]{2,0,1:T(1,128)} %get-tuple-element.149) | copy-start | bytes 12292
  45.4 0.8 copy-start
  70.2 5.5 %copy-start.18 = (bf16[2,1,512,1024]{3,2,1,0:T(8,128)(2,1)S(1)}, bf16[2,1,512,1024]{3,2,1,0:T(8,128)(2,1)}, u32[]{:S(2)}) copy-start(bf16[2,1,512,1024]{3,2,1,0:T(8,128)(2,1)} %param.26) | copy-start | bytes 6291460
  80.4 7.3 %copy-start.10 = (f32[1024]{0:T(1024)S(1)}, f32[1024]{0:T(1024)}, u32[]{:S(2)}) copy-start(f32[1024]{0:T(1024)} %copy-done.9) | copy-start | bytes 12292
  80.4 7.4 %copy-start.13 = (f32[2,128,8]{1,2,0:T(8,128)S(1)}, f32[2,128,8]{1,2,0:T(8,128)}, u32[]{:S(2)}) copy-start(f32[2,128,8]{1,2,0:T(8,128)} %param.20) | copy-start | bytes 24580
  80.4 69.0 %all-to-all-start.1 = ((bf16[32,80,1024]{2,1,0:T(8,128)(2,1)}), bf16[32,80,1024]{2,1,0:T(8,128)(2,1)}, u32[]{:S(2)}, u32[]{:S(2)}) async-start(bf16[32,80,1024]{2,1,0:T(8,128)(2,1)} %pad_maximum_fusion), calls=%async_computation.1 | async-start | bytes 10485760 | tf_op jit(solution)/shard_map/all_to_all | solution.py:200
  87.5 139.3 %all-gather.3.cloned.1.call-start = ((), (), s32[]{:S(2)}) async-start(), calls=%async_computation.5 | async-start | bytes 8650752 | tf_op jit(solution)/shard_map/all_gather | solution.py:227
  152.7 3.5 %copy-start.5 = (f32[1,1,1024]{2,0,1:T(1,128)S(1)}, f32[1,1,1024]{2,0,1:T(1,128)}, u32[]{:S(2)}) copy-start(f32[1,1,1024]{2,0,1:T(1,128)} %get-tuple-element.148) | copy-start | bytes 12292
  157.1 5.5 %copy-start.19 = (bf16[2,1,512,1024]{3,2,1,0:T(8,128)(2,1)S(1)}, bf16[2,1,512,1024]{3,2,1,0:T(8,128)(2,1)}, u32[]{:S(2)}) copy-start(bf16[2,1,512,1024]{3,2,1,0:T(8,128)(2,1)} %param.26) | copy-start | bytes 6291460
  165.9 8.5 %copy-start.8 = (f32[1024]{0:T(1024)S(1)}, f32[1024]{0:T(1024)}, u32[]{:S(2)}) copy-start(f32[1024]{0:T(1024)} %copy-done.7) | copy-start | bytes 12292
  165.9 44.1 %all-to-all-start.2 = ((bf16[32,40,1024]{2,1,0:T(8,128)(2,1)}), bf16[32,40,1024]{2,1,0:T(8,128)(2,1)S(1)}, u32[]{:S(2)}, u32[]{:S(2)}) async-start(bf16[32,40,1024]{2,1,0:T(8,128)(2,1)} %convolution_convert_fusion), calls=%async_computation.2 | async-start | bytes 5242880 | tf_op jit(solution)/shard_map/all_to_all | solution.py:200
  174.1 107.0 %all-gather.5.cloned.1.call-start = ((), (), s32[]{:S(2)}) async-start(), calls=%async_computation.6 | async-start | bytes 8650752 | tf_op jit(solution)/shard_map/all_gather | solution.py:230
  210.0 2.3 copy-start.4
  210.0 3.1 copy-start.11
  281.2 36.3 %copy-start.15 = (s32[128]{0:T(128)S(1)}, s32[128]{0:T(128)}, u32[]{:S(2)}) copy-start(s32[128]{0:T(128)} %copy-done.14) | copy-start | bytes 1540
  281.2 36.4 %copy-start.17 = (s32[4]{0:T(128)S(1)}, s32[4]{0:T(128)}, u32[]{:S(2)}) copy-start(s32[4]{0:T(128)} %param.21) | copy-start | bytes 52
  317.4 16.0 %copy-start.16 = (f32[2,128]{1,0:T(2,128)}, f32[2,128]{1,0:T(2,128)S(1)}, u32[]{:S(2)}) copy-start(f32[2,128]{1,0:T(2,128)S(1)} %add_subtract_fusion) | copy-start | bytes 3076
Sparse Core Ops, SparseCore 0:
  157.2 69.5 all-gather.2
  229.1 52.0 all-gather.4
